TPU v7x, 256 devices: a whole 4x4x8 slice. The times are simulated.
256 devices in a mesh: seq: 16 (over x, y), exp: 16 (over z, core).
Axes of the slice: x: 4, y: 4, z: 8, core: 2. Of those that a mesh axis runs over, the one named last changes fastest.
Arguments:
- tokens: bfloat16 [16384, 2048], P('seq', 'exp'), may hold values from -51 to 51
- in_gain: float32 [2048], replicated, may hold values from 0.1 to 1.9
- w_query: bfloat16 [2048, 2048], P(None, 'exp'), may hold values from -0.125 to 0.125
- w_key: bfloat16 [2048, 2048], P(None, 'exp'), may hold values from -0.125 to 0.125
- w_value: bfloat16 [2048, 4096], P(None, 'exp'), may hold values from -0.125 to 0.125
- w_zgate: bfloat16 [2048, 4096], P(None, 'exp'), may hold values from -0.125 to 0.125
- conv_query: float32 [4, 2048], P(None, 'exp'), may hold values from -3 to 3
- conv_key: float32 [4, 2048], P(None, 'exp'), may hold values from -3 to 3
- conv_value: float32 [4, 4096], P(None, 'exp'), may hold values from -3 to 3
- log_decay: float32 [16384, 32], P('seq', 'exp'), may hold values from -1.7 to 0
- write_rate: float32 [16384, 32], P('seq', 'exp'), may hold values from 0 to 1
- norm_gain: float32 [128], replicated, may hold values from 0.1 to 1.9
- w_out: bfloat16 [4096, 2048], P('exp'), may hold values from -0.09375 to 0.09375
- post_gain: float32 [2048], replicated, may hold values from 0.1 to 1.9
- expert_ids: int32 [16384, 2], P(('seq', 'exp')), may hold values from 0 to 15, as said below
- route_weight: float32 [16384, 2], P(('seq', 'exp')), may hold values from 0.1 to 1
- w_gate: bfloat16 [16, 2048, 512], P('exp'), may hold values from -0.125 to 0.125
- w_up: bfloat16 [16, 2048, 512], P('exp'), may hold values from -0.125 to 0.125
- w_down: bfloat16 [16, 512, 2048], P('exp'), may hold values from -0.25 to 0.25
Outputs:
- block_out: bfloat16 [16384, 2048], P(('seq', 'exp'))
Inputs may be any that keep to these rules, and one draw needn't show every extreme that they name: `expert_ids`: each row names 2 different experts. In each aligned block of 64 rows (the rows of one device) no expert is named more than 16 times, and in every aligned block of 1024 rows some expert is named exactly 16 times in each of its blocks of 64 rows.
All inputs are finite; a program needn't handle non-finite values.
Results may differ from a plain program's by a relative error of at most 0.015.
Values may be sent and summed in bfloat16 or wider, within the bound.
No kernel may reach another device: no remote copies, remote signals or barrier semaphores. Data moves between devices by JAX's collectives and lax.ppermute only.
A program may use at most 128 MiB of HBM per device.

v0:
```python
import jax
import jax.numpy as jnp
from jax import lax
from jax.sharding import PartitionSpec as P

DK = 128
DV = 128
STRETCH = 64


EPS = 1e-06
HIGH = lax.Precision.HIGHEST


def passed_along(block, axis, distance):
    devices = range(lax.axis_size(axis))
    route = [(i - distance, i) for i in devices if i - distance in devices]
    return lax.ppermute(block, axis, route)


def rms_scale(values, gain):
    return values * lax.rsqrt(jnp.mean(values * values, -1, keepdims=True) + EPS) * gain


def mix(form, left_arr, right_arr):
    return jnp.einsum(form, left_arr, right_arr, precision=HIGH)


def unit_heads(values, heads):
    shaped = values.reshape(values.shape[0], heads, -1)
    return shaped * lax.rsqrt(jnp.sum(shaped * shaped, -1, keepdims=True) + EPS)


def per_device(
    tokens,
    in_gain,
    w_query,
    w_key,
    w_value,
    w_zgate,
    conv_query,
    conv_key,
    conv_value,
    log_decay,
    write_rate,
    norm_gain,
    w_out,
    post_gain,
    expert_ids,
    route_weight,
    w_gate,
    w_up,
    w_down,
):
    whole = lax.all_gather(tokens, "exp", axis=1, tiled=True)
    x_float = whole.astype(jnp.float32)
    normed = rms_scale(x_float, in_gain).astype(jnp.bfloat16)

    def project(weight):
        return jnp.dot(normed, weight, preferred_element_type=jnp.float32).astype(jnp.bfloat16)

    projected = jnp.concatenate([project(w_query), project(w_key), project(w_value)], 1)
    z_gate = project(w_zgate)
    conv_all = jnp.concatenate([conv_query, conv_key, conv_value], 1)
    taps = conv_all.shape[0]
    length = projected.shape[0]
    tail = projected[length - (taps - 1) :]
    before = passed_along(tail, "seq", 1)
    extended = jnp.concatenate([before, projected], 0).astype(jnp.float32)
    conv_out = conv_all[0] * extended[0:length]
    for index in range(1, taps):
        conv_out = conv_out + conv_all[index] * extended[index : index + length]
    conv_out = jax.nn.silu(conv_out)
    width_q = w_query.shape[1]
    width_k = w_key.shape[1]
    key_heads = width_q // DK
    value_heads = w_value.shape[1] // DV
    group = value_heads // key_heads
    query = unit_heads(conv_out[:, :width_q], key_heads) * DK ** (-0.5)
    keyvec = unit_heads(conv_out[:, width_q : width_q + width_k], key_heads)
    values = conv_out[:, width_q + width_k :].reshape(length, value_heads, DV)
    query = jnp.repeat(query, group, axis=1)
    keyvec = jnp.repeat(keyvec, group, axis=1)
    blocks = length // STRETCH

    def by_block(array):
        return array.reshape(blocks, STRETCH, value_heads, -1).transpose(2, 0, 1, 3)

    q_blk = by_block(query)
    k_blk = by_block(keyvec)
    v_blk = by_block(values)
    g_blk = log_decay.reshape(blocks, STRETCH, value_heads).transpose(2, 0, 1)
    b_blk = write_rate.reshape(blocks, STRETCH, value_heads).transpose(2, 0, 1)
    cumul = jnp.cumsum(g_blk, -1)
    last_cum = cumul[..., -1:]
    places = jnp.arange(STRETCH)
    lower_incl = places[:, None] >= places[None, :]
    lower_strict = places[:, None] > places[None, :]
    spread_log = cumul[..., :, None] - cumul[..., None, :]
    ratio_incl = jnp.where(lower_incl, jnp.exp(jnp.where(lower_incl, spread_log, 0.0)), 0.0)
    key_gram = mix("hnid,hnjd->hnij", k_blk, k_blk)
    system = jnp.eye(STRETCH, dtype=jnp.float32) + jnp.where(
        lower_strict, b_blk[..., None] * key_gram * ratio_incl, 0.0
    )
    decay_in = jnp.exp(cumul)[..., None]
    right_side = jnp.concatenate(
        [b_blk[..., None] * decay_in * k_blk, b_blk[..., None] * v_blk], -1
    )
    solved = jax.scipy.linalg.solve_triangular(system, right_side, lower=True, unit_diagonal=True)
    w_mat = solved[..., :DK]
    u_mat = solved[..., DK:]
    key_tail = k_blk * jnp.exp(last_cum - cumul)[..., None]
    eye_key = jnp.eye(DK, dtype=jnp.float32)
    transit = jnp.exp(last_cum)[..., None] * eye_key - mix("hnik,hnil->hnkl", w_mat, key_tail)
    inject = mix("hniv,hnik->hnvk", u_mat, key_tail)

    def local_step(carry, pair):
        map_pre, add_pre = carry
        map_now, add_now = pair
        new_carry = (
            mix("hkl,hlm->hkm", map_pre, map_now),
            mix("hvl,hlm->hvm", add_pre, map_now) + add_now,
        )
        return (new_carry, carry)

    ident_maps = jnp.broadcast_to(eye_key, (value_heads, DK, DK))
    zero_add = jnp.zeros((value_heads, DV, DK), jnp.float32)
    (map_total, add_total), (map_prefix, add_prefix) = lax.scan(
        local_step,
        (ident_maps, zero_add),
        (transit.transpose(1, 0, 2, 3), inject.transpose(1, 0, 2, 3)),
    )

    def relay(step_index, state):
        passed = mix("hvk,hkl->hvl", state, map_total) + add_total
        return passed_along(passed.astype(jnp.bfloat16), "seq", 1).astype(passed.dtype)

    incoming = lax.fori_loop(0, lax.axis_size("seq") - 1, relay, zero_add)
    starts = (mix("hvk,nhkl->nhvl", incoming, map_prefix) + add_prefix).transpose(1, 0, 2, 3)
    new_values = u_mat - mix("hnik,hnvk->hniv", w_mat, starts)
    scores = mix("hnid,hnjd->hnij", q_blk, k_blk) * ratio_incl
    out_blk = decay_in * mix("hnik,hnvk->hniv", q_blk, starts) + mix(
        "hnij,hnjv->hniv", scores, new_values
    )
    delta_out = out_blk.transpose(1, 2, 0, 3).reshape(length, value_heads, DV)
    gate_z = z_gate.astype(jnp.float32).reshape(length, value_heads, DV)
    gated = (
        (rms_scale(delta_out, norm_gain) * jax.nn.silu(gate_z))
        .astype(jnp.bfloat16)
        .reshape(length, value_heads * DV)
    )
    n_exp = lax.axis_size("exp")
    row_share = length // n_exp
    attn_rows = lax.psum_scatter(
        jnp.dot(gated, w_out, preferred_element_type=jnp.float32).astype(jnp.bfloat16),
        "exp",
        scatter_dimension=0,
        tiled=True,
    ).astype(jnp.float32)
    own_rows = lax.dynamic_slice_in_dim(
        whole, lax.axis_index("exp") * row_share, row_share, 0
    ).astype(jnp.float32)
    resid = own_rows + attn_rows
    post = rms_scale(resid, post_gain).astype(jnp.bfloat16)
    topk = expert_ids.shape[1]
    experts = w_gate.shape[0] * n_exp
    capacity = 2 * row_share * topk // experts
    flat_ids = expert_ids.reshape(-1)
    hits = (flat_ids[:, None] == jnp.arange(experts)[None, :]).astype(jnp.int32)
    earlier_hits = jnp.cumsum(hits, 0) - hits
    slot_of = jnp.sum(earlier_hits * hits, 1)
    target = flat_ids * capacity + slot_of
    route_map = (target[:, None] == jnp.arange(experts * capacity)[None, :]).astype(jnp.bfloat16)
    spread_rows = jnp.repeat(post, topk, axis=0)
    outgoing = jnp.einsum(
        "rp,rd->pd", route_map, spread_rows, preferred_element_type=jnp.float32
    ).astype(jnp.bfloat16)
    outgoing = outgoing.reshape(experts, 1, capacity, post.shape[1])
    batch = lax.all_to_all(outgoing, "exp", split_axis=0, concat_axis=1, tiled=True)
    gate_v = jnp.einsum("esnd,edf->esnf", batch, w_gate, preferred_element_type=jnp.float32)
    up_v = jnp.einsum("esnd,edf->esnf", batch, w_up, preferred_element_type=jnp.float32)
    act = (jax.nn.silu(gate_v) * up_v).astype(jnp.bfloat16)
    processed = jnp.einsum(
        "esnf,efd->esnd", act, w_down, preferred_element_type=jnp.float32
    ).astype(jnp.bfloat16)
    returned = lax.all_to_all(processed, "exp", split_axis=1, concat_axis=0, tiled=True)
    flat_back = returned.reshape(experts * capacity, post.shape[1])
    fetched = jnp.dot(route_map, flat_back, preferred_element_type=jnp.float32).reshape(
        row_share, topk, post.shape[1]
    )
    moe_sum = jnp.sum(route_weight[..., None] * fetched, 1)
    return (resid + moe_sum).astype(jnp.bfloat16)


def solution(mesh):
    return jax.shard_map(
        per_device,
        mesh=mesh,
        in_specs=(
            P("seq", "exp"),
            P(),
            P(None, "exp"),
            P(None, "exp"),
            P(None, "exp"),
            P(None, "exp"),
            P(None, "exp"),
            P(None, "exp"),
            P(None, "exp"),
            P("seq", "exp"),
            P("seq", "exp"),
            P(),
            P("exp", None),
            P(),
            P(("seq", "exp"), None),
            P(("seq", "exp"), None),
            P("exp", None, None),
            P("exp", None, None),
            P("exp", None, None),
        ),
        out_specs=P(("seq", "exp"), None),
        check_vma=False,
    )
```

profile of v0, /device:TPU:1, one launch (start us, length us, event | category | flops | bytes accessed | tf_op | source)
XLA Modules:
  0.0 643.8 jit_solution(5141278856322808113)
XLA Ops:
  15.9 46.7 %all-gather.2.cloned.1.call-done = bf16[1024,2048]{1,0:T(8,128)(2,1)} async-done(((bf16[1024,128]{1,0:T(8,128)(2,1)}), bf16[1024,2048]{1,0:T(8,128)(2,1)}) %all-gather.2.cloned.1.call-update) | async-done | bytes 4194320 | tf_op jit(solution)/shard_map/all_gather | solution.py:55
  72.5 3.4 collective-permute-start.1
  84.2 3.7 fusion.53
  88.0 158.7 %custom-call.4 = f32[2,16,1,64,64]{3,4,2,1,0:T(8,128)} custom-call(f32[2,16,1,64,64]{4,3,2,1,0:T(8,128)} %fusion.53), custom_call_target="InvertDiagBlocksLowerTriangular" | custom-call | tf_op jit(solution)/shard_map/jit(_solve_triangular)/vmap(vmap())/triangular_solve | solution.py:109
  248.0 3.3 reshape.217
  251.3 3.3 copy.88
  258.5 5.1 convolution_bitcast_fusion.2
  263.7 5.4 bitcast_subtract_fusion
  269.1 70.9 %while.28 = (s32[]{:T(128)}, f32[2,128,128]{1,2,0:T(8,128)S(1)}, f32[2,128,128]{1,2,0:T(8,128)S(1)}, f32[16,2,128,128]{2,3,0,1:T(8,128)}, f32[16,2,128,128]{2,3,...) while((s32[]{:T(128)}, f32[2,128,128]{1,2,0:T(8,128)S(1)}, ...), condition=%wide.region_5.6_spmd.clone, body=%wide.region_4.5_spmd.clone.sunk | while | flops 100761600 | bytes 2492012 | solution.py:128
  340.2 104.4 %while.29 = (s32[]{:T(128)}, f32[2,128,128]{2,1,0:T(8,128)S(1)}, f32[2,128,128]{2,1,0:T(8,128)S(1)}, f32[2,128,128]{2,1,0:T(8,128)S(1)}, s32[]{:T(128)}, /*index=5*/s32[]{:T(128)}) while((s32[]{:T(128)}, f32[2,128,128]{2,1,0:T(8,128)S(1)}, f32[2,128,128]{2,1,0:T(8,128)S(1)}, f32[2,128,128]{2,1,0:T(8,128)S(1)}, s32[]{:T(128)}, ...), condition=%wide.region_7.8_spmd.clone, body=%wide.region_6.7_spmd.clone.sunk | while | flops 50462720 | bytes 917623 | solution.py:138
  340.6 4.1 collective-permute-start
  346.4 3.7 collective-permute-start
  351.7 3.7 collective-permute-start
  357.0 3.7 collective-permute-start
  362.3 5.8 collective-permute-start
  369.8 5.8 collective-permute-start
  377.2 5.8 collective-permute-start
  384.6 5.8 collective-permute-start
  392.5 5.7 collective-permute-start
  399.8 6.1 collective-permute-start
  407.5 6.0 collective-permute-start
  415.2 5.8 collective-permute-start
  422.6 5.8 collective-permute-start
  430.0 5.8 collective-permute-start
  437.5 5.8 collective-permute-start
  444.6 4.3 bitcast_add_fusion
  463.2 9.4 %convolution_convert_fusion = bf16[1024,2048]{1,0:T(8,128)(2,1)} fusion(bf16[256,2048]{1,0:T(8,128)(2,1)} %param.35, bf16[1024,2048]{1,0:T(8,128)(2,1)} %copy-done.1, bf16[2048,256]{1,0:T(8,128)(2,1)} %param.28, f32[128,8,2,128]{3,2,1,0:T(2,128)S(1)} %bitcast.176, f32[128,8,2,128]{3,2,1,0:T(2,128)} %bitcast.177, f32[256]{0:T(256)S(1)} %copy-done.31), kind=kOutput, calls=%fused_computation.27 | convolution fusion | flops 2152202240 | bytes 12583936 | tf_op jit(solution)/shard_map/dot_general | solution.py:155
  474.1 84.1 %reduce-scatter.2.cloned.1.call-done = bf16[64,2048]{1,0:T(8,128)(2,1)} async-done(((bf16[1024,2048]{1,0:T(8,128)(2,1)}), bf16[64,2048]{1,0:T(8,128)(2,1)}) %reduce-scatter.2.cloned.1.call-update) | async-done | bytes 262160 | tf_op jit(solution)/shard_map/reduce_scatter | solution.py:154
  561.7 36.3 %all_to_all.8 = bf16[16,1,16,2048]{3,2,1,0:T(8,128)(2,1)S(1)} all-to-all(bf16[16,1,16,2048]{3,2,1,0:T(8,128)(2,1)S(1)} %bitcast.174), channel_id=1, replica_groups=mesh['seq'=16,'exp'=16] {'exp'}, dimensions={0} | all-to-all | bytes 2097152 | tf_op jit(solution)/shard_map/all_to_all | solution.py:179
  599.5 4.0 fusion.19
  603.5 3.7 all-to-all-start.1
  607.4 27.1 %all-to-all-done.1 = bf16[1,16,16,2048]{3,2,0,1:T(8,128)(2,1)S(1)} async-done(((bf16[1,16,16,2048]{3,2,0,1:T(8,128)(2,1)}), bf16[1,16,16,2048]{3,2,0,1:T(8,128)(2,1)S(1)}, u32[]{:S(2)}, u32[]{:S(2)}) %all-to-all-start.1) | async-done | bytes 1048608 | tf_op jit(solution)/shard_map/all_to_all | solution.py:186
  (293 shorter events, 149.8 us)
Async XLA Ops:
  6.5 593.0 %copy-start = (bf16[1,512,2048]{2,1,0:T(8,128)(2,1)S(1)}, bf16[1,512,2048]{2,1,0:T(8,128)(2,1)}, u32[]{:S(2)}) copy-start(bf16[1,512,2048]{2,1,0:T(8,128)(2,1)} %param.41) | copy-start | bytes 6291460
  6.5 56.1 %all-gather.2.cloned.1.call-start = ((), (), s32[]{:S(2)}) async-start(), calls=%async_computation.3 | async-start | bytes 4456448 | tf_op jit(solution)/shard_map/all_gather | solution.py:55
  7.3 550.9 %reduce-scatter.2.cloned.1.call-start = ((), (), s32[]{:S(2)}) async-start(), calls=%async_computation.4 | async-start | bytes 4456448 | tf_op jit(solution)/shard_map/reduce_scatter | solution.py:154
  8.9 57.0 %copy-start.15 = (f32[16,64,2]{1,0,2:T(8,128)}, f32[16,64,2]{1,0,2:T(8,128)S(1)}, u32[]{:S(2)}) copy-start(f32[16,64,2]{1,0,2:T(8,128)S(1)} %reshape.203) | copy-start | bytes 24580
  15.9 49.9 %copy-start.20 = (f32[2048]{0:T(1024)S(1)}, f32[2048]{0:T(1024)}, u32[]{:S(2)}) copy-start(f32[2048]{0:T(1024)} %param.24) | copy-start | bytes 24580
  72.5 5.7 collective-permute-start.1
  84.2 162.4 %copy-start.18 = (f32[2,16,64]{2,1,0:T(8,128)S(1)}, f32[2,16,64]{2,1,0:T(8,128)}, u32[]{:S(2)}) copy-start(f32[2,16,64]{2,1,0:T(8,128)} %get-tuple-element.187) | copy-start | bytes 24580
  258.5 10.6 %copy-start.5 = (f32[2,16,64,256]{3,2,1,0:T(8,128)}, f32[2,16,64,256]{3,2,1,0:T(8,128)S(1)}, u32[]{:S(2)}) copy-start(f32[2,16,64,256]{3,2,1,0:T(8,128)S(1)} %fusion.23) | copy-start | bytes 6291460
  258.5 5.2 copy-start.27
  340.6 5.4 collective-permute-start
  346.4 5.0 collective-permute-start
  351.7 5.0 collective-permute-start
  357.0 5.0 collective-permute-start
  362.3 7.1 %collective-permute-start = (bf16[2,128,128]{2,1,0:T(8,128)(2,1)S(1)}, bf16[2,128,128]{2,1,0:T(8,128)(2,1)S(1)}, u32[]{:S(2)}, u32[]{:S(2)}) collective-permute-start(bf16[2,128,128]{2,1,0:T(8,128)(2,1)S(1)} %fusion.141), channel_id=1, source_target_pairs={{0,16},{16,32},{32,48},{48,64},{64,80},{80,96},{96,112},{112,128},... | collective-permute-start | bytes 196616 | tf_op jit(solution)/shard_map/while/body/eval_jaxpr/ppermute | solution.py:18
  369.8 7.1 %collective-permute-start = (bf16[2,128,128]{2,1,0:T(8,128)(2,1)S(1)}, bf16[2,128,128]{2,1,0:T(8,128)(2,1)S(1)}, u32[]{:S(2)}, u32[]{:S(2)}) collective-permute-start(bf16[2,128,128]{2,1,0:T(8,128)(2,1)S(1)} %fusion.141), channel_id=1, source_target_pairs={{0,16},{16,32},{32,48},{48,64},{64,80},{80,96},{96,112},{112,128},... | collective-permute-start | bytes 196616 | tf_op jit(solution)/shard_map/while/body/eval_jaxpr/ppermute | solution.py:18
  377.2 7.1 %collective-permute-start = (bf16[2,128,128]{2,1,0:T(8,128)(2,1)S(1)}, bf16[2,128,128]{2,1,0:T(8,128)(2,1)S(1)}, u32[]{:S(2)}, u32[]{:S(2)}) collective-permute-start(bf16[2,128,128]{2,1,0:T(8,128)(2,1)S(1)} %fusion.141), channel_id=1, source_target_pairs={{0,16},{16,32},{32,48},{48,64},{64,80},{80,96},{96,112},{112,128},... | collective-permute-start | bytes 196616 | tf_op jit(solution)/shard_map/while/body/eval_jaxpr/ppermute | solution.py:18
  384.6 7.5 %collective-permute-start = (bf16[2,128,128]{2,1,0:T(8,128)(2,1)S(1)}, bf16[2,128,128]{2,1,0:T(8,128)(2,1)S(1)}, u32[]{:S(2)}, u32[]{:S(2)}) collective-permute-start(bf16[2,128,128]{2,1,0:T(8,128)(2,1)S(1)} %fusion.141), channel_id=1, source_target_pairs={{0,16},{16,32},{32,48},{48,64},{64,80},{80,96},{96,112},{112,128},... | collective-permute-start | bytes 196616 | tf_op jit(solution)/shard_map/while/body/eval_jaxpr/ppermute | solution.py:18
  392.5 7.0 %collective-permute-start = (bf16[2,128,128]{2,1,0:T(8,128)(2,1)S(1)}, bf16[2,128,128]{2,1,0:T(8,128)(2,1)S(1)}, u32[]{:S(2)}, u32[]{:S(2)}) collective-permute-start(bf16[2,128,128]{2,1,0:T(8,128)(2,1)S(1)} %fusion.141), channel_id=1, source_target_pairs={{0,16},{16,32},{32,48},{48,64},{64,80},{80,96},{96,112},{112,128},... | collective-permute-start | bytes 196616 | tf_op jit(solution)/shard_map/while/body/eval_jaxpr/ppermute | solution.py:18
  399.8 7.4 %collective-permute-start = (bf16[2,128,128]{2,1,0:T(8,128)(2,1)S(1)}, bf16[2,128,128]{2,1,0:T(8,128)(2,1)S(1)}, u32[]{:S(2)}, u32[]{:S(2)}) collective-permute-start(bf16[2,128,128]{2,1,0:T(8,128)(2,1)S(1)} %fusion.141), channel_id=1, source_target_pairs={{0,16},{16,32},{32,48},{48,64},{64,80},{80,96},{96,112},{112,128},... | collective-permute-start | bytes 196616 | tf_op jit(solution)/shard_map/while/body/eval_jaxpr/ppermute | solution.py:18
  407.5 7.4 %collective-permute-start = (bf16[2,128,128]{2,1,0:T(8,128)(2,1)S(1)}, bf16[2,128,128]{2,1,0:T(8,128)(2,1)S(1)}, u32[]{:S(2)}, u32[]{:S(2)}) collective-permute-start(bf16[2,128,128]{2,1,0:T(8,128)(2,1)S(1)} %fusion.141), channel_id=1, source_target_pairs={{0,16},{16,32},{32,48},{48,64},{64,80},{80,96},{96,112},{112,128},... | collective-permute-start | bytes 196616 | tf_op jit(solution)/shard_map/while/body/eval_jaxpr/ppermute | solution.py:18
  415.2 7.1 %collective-permute-start = (bf16[2,128,128]{2,1,0:T(8,128)(2,1)S(1)}, bf16[2,128,128]{2,1,0:T(8,128)(2,1)S(1)}, u32[]{:S(2)}, u32[]{:S(2)}) collective-permute-start(bf16[2,128,128]{2,1,0:T(8,128)(2,1)S(1)} %fusion.141), channel_id=1, source_target_pairs={{0,16},{16,32},{32,48},{48,64},{64,80},{80,96},{96,112},{112,128},... | collective-permute-start | bytes 196616 | tf_op jit(solution)/shard_map/while/body/eval_jaxpr/ppermute | solution.py:18
  422.6 7.1 %collective-permute-start = (bf16[2,128,128]{2,1,0:T(8,128)(2,1)S(1)}, bf16[2,128,128]{2,1,0:T(8,128)(2,1)S(1)}, u32[]{:S(2)}, u32[]{:S(2)}) collective-permute-start(bf16[2,128,128]{2,1,0:T(8,128)(2,1)S(1)} %fusion.141), channel_id=1, source_target_pairs={{0,16},{16,32},{32,48},{48,64},{64,80},{80,96},{96,112},{112,128},... | collective-permute-start | bytes 196616 | tf_op jit(solution)/shard_map/while/body/eval_jaxpr/ppermute | solution.py:18
  430.0 7.1 %collective-permute-start = (bf16[2,128,128]{2,1,0:T(8,128)(2,1)S(1)}, bf16[2,128,128]{2,1,0:T(8,128)(2,1)S(1)}, u32[]{:S(2)}, u32[]{:S(2)}) collective-permute-start(bf16[2,128,128]{2,1,0:T(8,128)(2,1)S(1)} %fusion.141), channel_id=1, source_target_pairs={{0,16},{16,32},{32,48},{48,64},{64,80},{80,96},{96,112},{112,128},... | collective-permute-start | bytes 196616 | tf_op jit(solution)/shard_map/while/body/eval_jaxpr/ppermute | solution.py:18
  437.5 7.1 %collective-permute-start = (bf16[2,128,128]{2,1,0:T(8,128)(2,1)S(1)}, bf16[2,128,128]{2,1,0:T(8,128)(2,1)S(1)}, u32[]{:S(2)}, u32[]{:S(2)}) collective-permute-start(bf16[2,128,128]{2,1,0:T(8,128)(2,1)S(1)} %fusion.141), channel_id=1, source_target_pairs={{0,16},{16,32},{32,48},{48,64},{64,80},{80,96},{96,112},{112,128},... | collective-permute-start | bytes 196616 | tf_op jit(solution)/shard_map/while/body/eval_jaxpr/ppermute | solution.py:18
  444.6 4.4 copy-start.6
  449.0 4.4 copy-start.19
  458.8 4.4 copy-start.31
  472.7 86.7 %copy-start.21 = (f32[2048]{0:T(1024)S(1)}, f32[2048]{0:T(1024)}, u32[]{:S(2)}) copy-start(f32[2048]{0:T(1024)} %param.36) | copy-start | bytes 24580
  561.1 36.9 %copy-start.29 = (bf16[1,2048,512]{2,1,0:T(8,128)(2,1)S(1)}, bf16[1,2048,512]{2,1,0:T(8,128)(2,1)}, u32[]{:S(2)}) copy-start(bf16[1,2048,512]{2,1,0:T(8,128)(2,1)} %param.39) | copy-start | bytes 6291460
  603.5 31.1 %copy-start.28 = (f32[64,2]{0,1:T(2,128)S(1)}, f32[64,2]{0,1:T(2,128)}, u32[]{:S(2)}) copy-start(f32[64,2]{0,1:T(2,128)} %param.38) | copy-start | bytes 1540
  603.5 31.4 %copy-start.9 = (bf16[64,2048]{1,0:T(8,128)(2,1)S(1)}, bf16[64,2048]{1,0:T(8,128)(2,1)}, u32[]{:S(2)}) copy-start(bf16[64,2048]{1,0:T(8,128)(2,1)} %reduce-scatter.2.cloned.1.call-done) | copy-start | bytes 786436
  603.5 31.0 %all-to-all-start.1 = ((bf16[1,16,16,2048]{3,2,0,1:T(8,128)(2,1)}), bf16[1,16,16,2048]{3,2,0,1:T(8,128)(2,1)S(1)}, u32[]{:S(2)}, u32[]{:S(2)}) async-start(bf16[1,16,16,2048]{3,2,0,1:T(8,128)(2,1)} %fusion.19), calls=%async_computation.2 | async-start | bytes 2097152 | tf_op jit(solution)/shard_map/all_to_all | solution.py:186
  (19 other events, 44.2 us)
Sparse Core Ops, SparseCore 0:
  9.1 53.4 all-gather.1
  472.8 85.3 reduce-scatter.1
where the time goes:
time: 653 us; the launch traced here: 644 us
  other arithmetic  191 us (29%)
  waiting for transfers between devices  180 us (28%)
  matrix products  95 us (15%)
  starting transfers between devices  86.6 us (13%)
  local copies, waits for them, and re-layouts  38.7 us (6%)
  blocking collectives  36.3 us (6%)
  between operations  14.2 us (2%)
    another operation x4, other arithmetic, per_device(): jax.scipy.linalg.solve_triangular(system, right_side, lower=True, unit_di...  160 us
    reduce_scatter x1, waiting for transfers between devices, per_device(): lax.psum_scatter(jnp.dot(gated, w_out, preferred_element_type=jnp.float32...  84.1 us
    ppermute x16, starting transfers between devices, passed_along(): return lax.ppermute(block, axis, route)  82.8 us
    dot_general x55, matrix products, mix(): return jnp.einsum(form, left_arr, right_arr, precision=HIGH)  72.8 us
    all_gather x1, waiting for transfers between devices, per_device(): whole = lax.all_gather(tokens, 'exp', axis=1, tiled=True)  46.7 us
    all_to_all x1, blocking collectives, per_device(): lax.all_to_all(outgoing, 'exp', split_axis=0, concat_axis=1, tiled=True)  36.3 us
    all_to_all x1, waiting for transfers between devices, per_device(): lax.all_to_all(processed, 'exp', split_axis=1, concat_axis=0, tiled=True)  27.1 us
    ppermute x16, waiting for transfers between devices, passed_along(): return lax.ppermute(block, axis, route)  21.6 us
  transfers between devices with their start and end apart: 19, of which 19 were waited for; matrix products, arithmetic and copies ran while one was open for 2% of the time, Pallas kernels for 0%

commit v1 on v0

--- a/solution.py
+++ b/solution.py
@@ -1,11 +1,12 @@
 import jax
 import jax.numpy as jnp
 from jax import lax
-from jax.sharding import PartitionSpec as P
+from jax.sharding import Mesh, PartitionSpec as P
 
 DK = 128
 DV = 128
 STRETCH = 64
+EXP = ("z", "core")
 
 
 EPS = 1e-06
@@ -18,6 +19,10 @@
     return lax.ppermute(block, axis, route)
 
 
+def exp_index():
+    return lax.axis_index("z") * lax.axis_size("core") + lax.axis_index("core")
+
+
 def rms_scale(values, gain):
     return values * lax.rsqrt(jnp.mean(values * values, -1, keepdims=True) + EPS) * gain
 
@@ -29,6 +34,61 @@
 def unit_heads(values, heads):
     shaped = values.reshape(values.shape[0], heads, -1)
     return shaped * lax.rsqrt(jnp.sum(shaped * shaped, -1, keepdims=True) + EPS)
+
+
+def unit_lower_inverse(strict):
+    size = strict.shape[-1]
+    rows = lax.broadcasted_iota(jnp.int32, (size, size), 0)
+    cols = lax.broadcasted_iota(jnp.int32, (size, size), 1)
+    inverse = jnp.broadcast_to(jnp.eye(size, dtype=strict.dtype), strict.shape)
+    span = 1
+    while span < size:
+        pick = (
+            (rows // (2 * span) == cols // (2 * span))
+            & ((rows // span) % 2 == 1)
+            & ((cols // span) % 2 == 0)
+        )
+        coupling = jnp.where(pick, strict, 0.0)
+        spread = lax.optimization_barrier(mix("...ij,...jk->...ik", coupling, inverse))
+        inverse = inverse - lax.optimization_barrier(mix("...ij,...jk->...ik", inverse, spread))
+        span *= 2
+    return inverse
+
+
+def compose(first_map, first_add, then_map, then_add):
+    stacked = jnp.concatenate([first_map, first_add], -2)
+    moved = mix("...kl,...lm->...km", stacked, then_map)
+    rows = first_map.shape[-2]
+    return moved[..., :rows, :], moved[..., rows:, :] + then_add
+
+
+def block_prefix(maps, adds):
+    count = maps.shape[1]
+    eye = jnp.eye(maps.shape[-1], dtype=maps.dtype)
+    shift = 1
+    while shift < count:
+        pad_map = jnp.broadcast_to(eye, maps[:, :shift].shape)
+        pad_add = jnp.zeros_like(adds[:, :shift])
+        prev_map = jnp.concatenate([pad_map, maps[:, :-shift]], 1)
+        prev_add = jnp.concatenate([pad_add, adds[:, :-shift]], 1)
+        maps, adds = compose(prev_map, prev_add, maps, adds)
+        shift *= 2
+    return maps, adds
+
+
+def shard_prefix(total_map, total_add):
+    place = lax.axis_index("seq")
+    count = lax.axis_size("seq")
+    maps, adds = total_map, total_add
+    shift = 1
+    while shift < count:
+        got = passed_along(jnp.stack([maps, adds]), "seq", shift)
+        new_map, new_add = compose(got[0], got[1], maps, adds)
+        later = place >= shift
+        maps = jnp.where(later, new_map, maps)
+        adds = jnp.where(later, new_add, adds)
+        shift *= 2
+    return passed_along(adds, "seq", 1)
 
 
 def per_device(
@@ -52,7 +112,9 @@
     w_up,
     w_down,
 ):
-    whole = lax.all_gather(tokens, "exp", axis=1, tiled=True)
+    near = lax.all_gather(tokens, "z", axis=0)
+    both = lax.all_gather(near, "core", axis=0)
+    whole = both.transpose(2, 1, 0, 3).reshape(tokens.shape[0], -1)
     x_float = whole.astype(jnp.float32)
     normed = rms_scale(x_float, in_gain).astype(jnp.bfloat16)
 
@@ -99,44 +161,26 @@
     spread_log = cumul[..., :, None] - cumul[..., None, :]
     ratio_incl = jnp.where(lower_incl, jnp.exp(jnp.where(lower_incl, spread_log, 0.0)), 0.0)
     key_gram = mix("hnid,hnjd->hnij", k_blk, k_blk)
-    system = jnp.eye(STRETCH, dtype=jnp.float32) + jnp.where(
-        lower_strict, b_blk[..., None] * key_gram * ratio_incl, 0.0
-    )
+    strict = jnp.where(lower_strict, b_blk[..., None] * key_gram * ratio_incl, 0.0)
+    inverse = unit_lower_inverse(strict)
     decay_in = jnp.exp(cumul)[..., None]
     right_side = jnp.concatenate(
         [b_blk[..., None] * decay_in * k_blk, b_blk[..., None] * v_blk], -1
     )
-    solved = jax.scipy.linalg.solve_triangular(system, right_side, lower=True, unit_diagonal=True)
+    solved = mix("hnij,hnjc->hnic", inverse, right_side)
     w_mat = solved[..., :DK]
     u_mat = solved[..., DK:]
     key_tail = k_blk * jnp.exp(last_cum - cumul)[..., None]
     eye_key = jnp.eye(DK, dtype=jnp.float32)
     transit = jnp.exp(last_cum)[..., None] * eye_key - mix("hnik,hnil->hnkl", w_mat, key_tail)
     inject = mix("hniv,hnik->hnvk", u_mat, key_tail)
-
-    def local_step(carry, pair):
-        map_pre, add_pre = carry
-        map_now, add_now = pair
-        new_carry = (
-            mix("hkl,hlm->hkm", map_pre, map_now),
-            mix("hvl,hlm->hvm", add_pre, map_now) + add_now,
-        )
-        return (new_carry, carry)
-
-    ident_maps = jnp.broadcast_to(eye_key, (value_heads, DK, DK))
-    zero_add = jnp.zeros((value_heads, DV, DK), jnp.float32)
-    (map_total, add_total), (map_prefix, add_prefix) = lax.scan(
-        local_step,
-        (ident_maps, zero_add),
-        (transit.transpose(1, 0, 2, 3), inject.transpose(1, 0, 2, 3)),
-    )
-
-    def relay(step_index, state):
-        passed = mix("hvk,hkl->hvl", state, map_total) + add_total
-        return passed_along(passed.astype(jnp.bfloat16), "seq", 1).astype(passed.dtype)
-
-    incoming = lax.fori_loop(0, lax.axis_size("seq") - 1, relay, zero_add)
-    starts = (mix("hvk,nhkl->nhvl", incoming, map_prefix) + add_prefix).transpose(1, 0, 2, 3)
+    map_incl, add_incl = block_prefix(transit, inject)
+    ident_maps = jnp.broadcast_to(eye_key, (value_heads, 1, DK, DK))
+    zero_add = jnp.zeros((value_heads, 1, DV, DK), jnp.float32)
+    map_prefix = jnp.concatenate([ident_maps, map_incl[:, :-1]], 1)
+    add_prefix = jnp.concatenate([zero_add, add_incl[:, :-1]], 1)
+    incoming = shard_prefix(map_incl[:, -1], add_incl[:, -1])
+    starts = mix("hvk,hnkl->hnvl", incoming, map_prefix) + add_prefix
     new_values = u_mat - mix("hnik,hnvk->hniv", w_mat, starts)
     scores = mix("hnid,hnjd->hnij", q_blk, k_blk) * ratio_incl
     out_blk = decay_in * mix("hnik,hnvk->hniv", q_blk, starts) + mix(
@@ -149,16 +193,17 @@
         .astype(jnp.bfloat16)
         .reshape(length, value_heads * DV)
     )
-    n_exp = lax.axis_size("exp")
+    n_exp = lax.axis_size("z") * lax.axis_size("core")
     row_share = length // n_exp
+    projected_out = jnp.dot(gated, w_out, preferred_element_type=jnp.float32).astype(jnp.bfloat16)
+    chips = lax.axis_size("z")
+    by_owner = projected_out.reshape(chips, n_exp // chips, row_share, -1)
+    chip_sum = lax.psum_scatter(by_owner, "core", scatter_dimension=1, tiled=True)
     attn_rows = lax.psum_scatter(
-        jnp.dot(gated, w_out, preferred_element_type=jnp.float32).astype(jnp.bfloat16),
-        "exp",
-        scatter_dimension=0,
-        tiled=True,
-    ).astype(jnp.float32)
+        chip_sum.reshape(chips, row_share, -1), "z", scatter_dimension=0, tiled=True
+    ).reshape(row_share, -1).astype(jnp.float32)
     own_rows = lax.dynamic_slice_in_dim(
-        whole, lax.axis_index("exp") * row_share, row_share, 0
+        whole, exp_index() * row_share, row_share, 0
     ).astype(jnp.float32)
     resid = own_rows + attn_rows
     post = rms_scale(resid, post_gain).astype(jnp.bfloat16)
@@ -176,14 +221,14 @@
         "rp,rd->pd", route_map, spread_rows, preferred_element_type=jnp.float32
     ).astype(jnp.bfloat16)
     outgoing = outgoing.reshape(experts, 1, capacity, post.shape[1])
-    batch = lax.all_to_all(outgoing, "exp", split_axis=0, concat_axis=1, tiled=True)
+    batch = lax.all_to_all(outgoing, EXP, split_axis=0, concat_axis=1, tiled=True)
     gate_v = jnp.einsum("esnd,edf->esnf", batch, w_gate, preferred_element_type=jnp.float32)
     up_v = jnp.einsum("esnd,edf->esnf", batch, w_up, preferred_element_type=jnp.float32)
     act = (jax.nn.silu(gate_v) * up_v).astype(jnp.bfloat16)
     processed = jnp.einsum(
         "esnf,efd->esnd", act, w_down, preferred_element_type=jnp.float32
     ).astype(jnp.bfloat16)
-    returned = lax.all_to_all(processed, "exp", split_axis=1, concat_axis=0, tiled=True)
+    returned = lax.all_to_all(processed, EXP, split_axis=1, concat_axis=0, tiled=True)
     flat_back = returned.reshape(experts * capacity, post.shape[1])
     fetched = jnp.dot(route_map, flat_back, preferred_element_type=jnp.float32).reshape(
         row_share, topk, post.shape[1]
@@ -193,30 +238,32 @@
 
 
 def solution(mesh):
+    grid = mesh.devices.shape
+    fine = Mesh(mesh.devices.reshape(grid[0], grid[1] // 2, 2), ("seq", "z", "core"))
     return jax.shard_map(
         per_device,
-        mesh=mesh,
+        mesh=fine,
         in_specs=(
-            P("seq", "exp"),
+            P("seq", EXP),
             P(),
-            P(None, "exp"),
-            P(None, "exp"),
-            P(None, "exp"),
-            P(None, "exp"),
-            P(None, "exp"),
-            P(None, "exp"),
-            P(None, "exp"),
-            P("seq", "exp"),
-            P("seq", "exp"),
+            P(None, EXP),
+            P(None, EXP),
+            P(None, EXP),
+            P(None, EXP),
+            P(None, EXP),
+            P(None, EXP),
+            P(None, EXP),
+            P("seq", EXP),
+            P("seq", EXP),
             P(),
-            P("exp", None),
+            P(EXP, None),
             P(),
-            P(("seq", "exp"), None),
-            P(("seq", "exp"), None),
-            P("exp", None, None),
-            P("exp", None, None),
-            P("exp", None, None),
+            P(("seq", "z", "core"), None),
+            P(("seq", "z", "core"), None),
+            P(EXP, None, None),
+            P(EXP, None, None),
+            P(EXP, None, None),
         ),
-        out_specs=P(("seq", "exp"), None),
+        out_specs=P(("seq", "z", "core"), None),
         check_vma=False,
     )

time: 653 us -> 406 us (0.62)
  other arithmetic: 191 us -> 23.4 us
  starting transfers between devices: 86.6 us -> 33 us
  matrix products: 95 us -> 81 us
  waiting for transfers between devices: 180 us -> 170 us
    another operation x6, other arithmetic: 160 us -> 1.58 us  [shard_prefix(): got = passed_along(jnp.stack([maps, adds]), 'seq', shift)]
    ppermute x16 -> x6, starting transfers between devices: 82.8 us -> 29.2 us  [passed_along(): return lax.ppermute(block, axis, route)]
    reduce_scatter x1 -> x2, waiting for transfers between devices: 84.1 us -> 64.7 us  [the longest x1 38.6 us: per_device(): lax.psum_scatter(chip_sum.reshape(chips, row_share, -1), 'z', scatter_dim...]
    all_gather x1 -> x2, waiting for transfers between devices: 46.7 us -> 63.5 us  [the longest x1 42.3 us: per_device(): near = lax.all_gather(tokens, 'z', axis=0)]
    dynamic_slice x32 -> x1, local copies, waits for them, and re-layouts: 16.1 us -> 1.26 us  [per_device(): lax.dynamic_slice_in_dim(whole, exp_index() * row_share, row_share, 0)]
    dynamic_update_slice x16 -> x0, other arithmetic: 11.9 us -> none  [per_device(): lax.scan(local_step, (ident_maps, zero_add), (transit.transpose(1, 0, 2,...]
    dot_general x55 -> x29, matrix products: 72.8 us -> 62.2 us  [mix(): return jnp.einsum(form, left_arr, right_arr, precision=HIGH)]
    ppermute x16 -> x6, waiting for transfers between devices: 21.6 us -> 14.2 us  [passed_along(): return lax.ppermute(block, axis, route)]
  transfers between devices with their start and end apart: 19 -> 11, of which waited for: 19 -> 10; matrix products, arithmetic and copies ran while one was open for 2% -> 3% of each run, Pallas kernels for 0% -> 0%
where the time goes in v1:
time: 406 us; the launch traced here: 400 us
  waiting for transfers between devices  170 us (42%)
  matrix products  81 us (20%)
  local copies, waits for them, and re-layouts  39 us (10%)
  blocking collectives  38.3 us (9%)
  starting transfers between devices  33 us (8%)
  other arithmetic  23.4 us (6%)
  between operations  14.5 us (4%)
    dot_general x29, matrix products, mix(): return jnp.einsum(form, left_arr, right_arr, precision=HIGH)  62.2 us
    all_gather x1, waiting for transfers between devices, per_device(): near = lax.all_gather(tokens, 'z', axis=0)  42.3 us
    reduce_scatter x1, waiting for transfers between devices, per_device(): lax.psum_scatter(chip_sum.reshape(chips, row_share, -1), 'z', scatter_dim...  38.6 us
    all_to_all x1, blocking collectives, per_device(): lax.all_to_all(outgoing, EXP, split_axis=0, concat_axis=1, tiled=True)  38.3 us
    ppermute x6, starting transfers between devices, passed_along(): return lax.ppermute(block, axis, route)  29.2 us
    all_to_all x1, waiting for transfers between devices, per_device(): lax.all_to_all(processed, EXP, split_axis=1, concat_axis=0, tiled=True)  27.1 us
    reduce_scatter x1, waiting for transfers between devices, per_device(): lax.psum_scatter(by_owner, 'core', scatter_dimension=1, tiled=True)  26.1 us
    all_gather x1, waiting for transfers between devices, per_device(): both = lax.all_gather(near, 'core', axis=0)  21.2 us
  transfers between devices with their start and end apart: 11, of which 10 were waited for; matrix products, arithmetic and copies ran while one was open for 3% of the time, Pallas kernels for 0%

profile of v1, /device:TPU:1, one launch (start us, length us, event | category | flops | bytes accessed | tf_op | source)
XLA Modules:
  0.0 399.6 jit_solution(5266455715470621347)
XLA Ops:
  7.3 42.3 %all-gather.5.cloned.1.call-done = bf16[8192,128]{1,0:T(8,128)(2,1)} async-done(((bf16[1024,128]{1,0:T(8,128)(2,1)}), bf16[8192,128]{1,0:T(8,128)(2,1)}) %all-gather.5.cloned.1.call-update) | async-done | bytes 2097168 | tf_op jit(solution)/shard_map/all_gather | solution.py:115
  52.7 21.2 %all-gather.7.cloned.1.call-done = bf16[16,1024,128]{2,1,0:T(8,128)(2,1)} async-done(((bf16[8,1024,128]{2,1,0:T(8,128)(2,1)}), bf16[16,1024,128]{2,1,0:T(8,128)(2,1)}) %all-gather.7.cloned.1.call-update) | async-done | bytes 4194320 | tf_op jit(solution)/shard_map/all_gather | solution.py:116
  74.0 6.4 %copy.78 = bf16[1024,8,2,128]{0,3,2,1:T(8,128)(2,1)} copy(bf16[1024,8,2,128]{3,0,1,2:T(8,128)(2,1)} %bitcast.173) | data formatting | bytes 8388608 | tf_op jit(solution)/shard_map/transpose | solution.py:117
  80.4 3.2 multiply_reduce_fusion
  88.8 2.9 collective-permute-start
  94.9 2.4 divide_multiply_fusion
  100.7 3.3 copy.83
  104.0 2.1 multiply_multiply_fusion
  129.7 4.0 %fusion.50 = f32[2,16,128,128]{3,2,1,0:T(8,128)S(1)} fusion(f32[2,16,64,256]{3,2,1,0:T(8,128)S(1)} %fusion.35, f32[2,16,64]{2,1,0:T(8,128)S(1)} %get-tuple-element.27, f32[16,64,128]{2,1,0:T(8,128)S(1)} %bitcast.177), kind=kOutput, calls=%fused_computation.70 | convolution fusion | flops 402915328 | bytes 3686400 | tf_op jit(solution)/shard_map/hniv,hnik->hnvk/dot_general | solution.py:31
  134.4 4.1 %multiply_subtract_fusion = f32[2,16,128,128]{3,2,1,0:T(8,128)S(1)} fusion(f32[128,128]{1,0:T(8,128)S(1)} %fusion.154, f32[2,16]{1,0:T(2,128)S(1)} %copy-done.28, f32[2,16,64,256]{3,2,1,0:T(8,128)S(1)} %fusion.35, f32[2,16,64]{2,1,0:T(8,128)S(1)} %get-tuple-element.27, f32[16,64,128]{2,1,0:T(8,128)S(1)} %bitcast.178), kind=kOutput, calls=%fused_computation.68 | convolution fusion | flops 403963904 | bytes 3752960 | tf_op jit(solution)/shard_map/hnik,hnil->hnkl/dot_general | solution.py:31
  138.7 4.5 %fusion.6 = f32[2,16,256,128]{3,2,1,0:T(8,128)S(1)} fusion(f32[2,16,128,128]{3,2,1,0:T(8,128)S(1)} %multiply_subtract_fusion, f32[2,15,128,128]{3,2,1,0:T(8,128)S(1)} %slice.218, f32[2,15,128,128]{3,2,1,0:T(8,128)S(1)} %slice.216, f32[2,1,128,128]{3,2,1,0:T(8,128)S(1)} %broadcast_in_dim.100), kind=kOutput, calls=%fused_computation.12 | convolution fusion | flops 1614807040 | bytes 10354688 | tf_op jit(solution)/shard_map/...kl,...lm->...km/dot_general | solution.py:31
  144.0 4.9 %fusion.4 = f32[2,16,256,128]{3,2,1,0:T(8,128)S(1)} fusion(f32[2,14,128,128]{3,2,1,0:T(8,128)S(1)} %slice.221, f32[2,14,128,128]{3,2,1,0:T(8,128)S(1)} %slice.219, f32[2,2,128,128]{3,2,1,0:T(8,128)S(1)} %broadcast_in_dim.103, f32[2,16,256,128]{3,2,1,0:T(8,128)S(1)} %fusion.6), kind=kOutput, calls=%fused_computation.9 | convolution fusion | flops 1614807040 | bytes 10223616 | tf_op jit(solution)/shard_map/...kl,...lm->...km/dot_general | solution.py:31
  149.6 4.4 %fusion.2 = f32[2,16,256,128]{3,2,1,0:T(8,128)S(1)} fusion(f32[2,12,128,128]{3,2,1,0:T(8,128)S(1)} %slice.225, f32[2,12,128,128]{3,2,1,0:T(8,128)S(1)} %slice.223, f32[2,4,128,128]{3,2,1,0:T(8,128)S(1)} %broadcast_in_dim.102, f32[2,16,256,128]{3,2,1,0:T(8,128)S(1)} %fusion.4), kind=kOutput, calls=%fused_computation.6 | convolution fusion | flops 1614807040 | bytes 9961472 | tf_op jit(solution)/shard_map/...kl,...lm->...km/dot_general | solution.py:31
  154.5 4.2 %fusion = f32[2,16,256,128]{3,2,1,0:T(8,128)S(1)} fusion(f32[2,8,128,128]{3,2,1,0:T(8,128)S(1)} %slice.229, f32[2,8,128,128]{3,2,1,0:T(8,128)S(1)} %slice.227, f32[2,8,128,128]{3,2,1,0:T(8,128)S(1)} %broadcast_in_dim.101, f32[2,16,256,128]{3,2,1,0:T(8,128)S(1)} %fusion.2), kind=kOutput, calls=%fused_computation.3 | convolution fusion | flops 1614807040 | bytes 9437184 | tf_op jit(solution)/shard_map/...kl,...lm->...km/dot_general | solution.py:31
  162.1 4.1 %collective-permute-start.1 = (f32[2,2,128,128]{3,2,1,0:T(8,128)S(1)}, f32[2,2,128,128]{3,2,1,0:T(8,128)S(1)}, u32[]{:S(2)}, u32[]{:S(2)}) collective-permute-start(f32[2,2,128,128]{3,2,1,0:T(8,128)S(1)} %pad_maximum_fusion), channel_id=1, source_target_pairs={{0,16},{16,32},{32,48},{48,64},{64,80},{80,96},{96,112},{112,128},... | collective-permute-start | bytes 786440 | tf_op jit(solution)/shard_map/ppermute | solution.py:19
  166.2 4.5 %collective-permute-done.1 = f32[2,2,128,128]{3,2,1,0:T(8,128)S(1)} collective-permute-done((f32[2,2,128,128]{3,2,1,0:T(8,128)S(1)}, f32[2,2,128,128]{3,2,1,0:T(8,128)S(1)}, u32[]{:S(2)}, u32[]{:S(2)}) %collective-permute-start.1) | collective-permute-done | bytes 262176 | tf_op jit(solution)/shard_map/ppermute | solution.py:19
  173.1 5.6 %collective-permute-start.2 = (f32[2,2,128,128]{3,2,1,0:T(8,128)S(1)}, f32[2,2,128,128]{3,2,1,0:T(8,128)S(1)}, u32[]{:S(2)}, u32[]{:S(2)}) collective-permute-start(f32[2,2,128,128]{3,2,1,0:T(8,128)S(1)} %pad_maximum_fusion.1), channel_id=1, source_target_pairs={{0,32},{16,48},{32,64},{48,80},{64,96},{80,112},{96,128},{112,144}... | collective-permute-start | bytes 786440 | tf_op jit(solution)/shard_map/ppermute | solution.py:19
  178.8 3.7 collective-permute-done.2
  183.7 9.2 %collective-permute-start.3 = (f32[2,2,128,128]{3,2,1,0:T(8,128)}, f32[2,2,128,128]{3,2,1,0:T(8,128)S(1)}, u32[]{:S(2)}, u32[]{:S(2)}) collective-permute-start(f32[2,2,128,128]{3,2,1,0:T(8,128)} %pad_maximum_fusion.2), channel_id=1, source_target_pairs={{0,64},{16,80},{32,96},{48,112},{64,128},{80,144},{96,160},{112,17... | collective-permute-start | bytes 786440 | tf_op jit(solution)/shard_map/ppermute | solution.py:19
  192.9 3.6 collective-permute-done.3
  197.7 5.9 %collective-permute-start.4 = (f32[2,2,128,128]{3,2,1,0:T(8,128)}, f32[2,2,128,128]{3,2,1,0:T(8,128)}, u32[]{:S(2)}, u32[]{:S(2)}) collective-permute-start(f32[2,2,128,128]{3,2,1,0:T(8,128)} %pad_maximum_fusion.3), channel_id=1, source_target_pairs={{0,128},{16,144},{32,160},{48,176},{64,192},{80,208},{96,224},{112... | collective-permute-start | bytes 786440 | tf_op jit(solution)/shard_map/ppermute | solution.py:19
  210.1 2.5 convolution_multiply_fusion.1
  216.9 4.2 %convolution_subtract_fusion = f32[2,16,64,128]{3,2,1,0:T(8,128)S(1)} fusion(f32[2,16,128,128]{3,2,1,0:T(8,128)S(1)} %bitcast_add_fusion, f32[2,16,64,256]{3,2,1,0:T(8,128)S(1)} %copy-done.4), kind=kOutput, calls=%fused_computation.75 | convolution fusion | flops 402915328 | bytes 5242880 | tf_op jit(solution)/shard_map/hnik,hnvk->hniv/dot_general | solution.py:31
  221.1 4.2 %fusion.54 = f32[16,64,2,128]{3,1,0,2:T(8,128)S(1)} fusion(f32[2,16,128,128]{3,2,1,0:T(8,128)S(1)} %bitcast_add_fusion, f32[16,64,128]{2,1,0:T(8,128)S(1)} %bitcast.181, f32[16,64,2]{1,0,2:T(8,128)S(1)} %copy-done.12), kind=kOutput, calls=%fused_computation.78 | convolution fusion | flops 402915328 | bytes 3678208 | tf_op jit(solution)/shard_map/hnik,hnvk->hniv/dot_general | solution.py:31
  231.1 9.5 %convolution_convert_fusion = bf16[1024,2048]{1,0:T(8,128)(2,1)} fusion(bf16[256,2048]{1,0:T(8,128)(2,1)} %param.31, bf16[1024,2048]{0,1:T(8,128)(2,1)} %copy-done.7, bf16[2048,256]{1,0:T(8,128)(2,1)} %param.24, f32[128,8,2,128]{3,2,1,0:T(2,128)S(1)} %bitcast.192, f32[128,8,2,128]{3,2,1,0:T(2,128)} %bitcast.193, f32[256]{0:T(256)S(1)} %copy-done.36), kind=kOutput, calls=%fused_computation.27 | convolution fusion | flops 2152202240 | bytes 12583936 | tf_op jit(solution)/shard_map/dot_general | solution.py:198
  240.7 4.8 %copy.89 = bf16[8,2,64,2048]{3,2,0,1:T(8,128)(2,1)} copy(bf16[8,2,64,2048]{3,2,1,0:T(8,128)(2,1)} %bitcast.182) | data formatting | bytes 8388608 | tf_op jit(solution)/shard_map/reshape | solution.py:200
  245.6 26.1 %reduce-scatter.3.cloned.1.call-done = bf16[8,1,64,2048]{3,2,0,1:T(8,128)(2,1)} async-done(((bf16[8,2,64,2048]{3,2,0,1:T(8,128)(2,1)}), bf16[8,1,64,2048]{3,2,0,1:T(8,128)(2,1)}) %reduce-scatter.3.cloned.1.call-update) | async-done | bytes 2097168 | tf_op jit(solution)/shard_map/reduce_scatter | solution.py:201
  273.8 38.6 %reduce-scatter.5.cloned.1.call-done = bf16[1,64,2048]{2,1,0:T(8,128)(2,1)} async-done(((bf16[8,64,2048]{2,1,0:T(8,128)(2,1)}), bf16[1,64,2048]{2,1,0:T(8,128)(2,1)}) %reduce-scatter.5.cloned.1.call-update) | async-done | bytes 262160 | tf_op jit(solution)/shard_map/reduce_scatter | solution.py:202
  315.8 38.3 %all_to_all.8 = bf16[16,1,16,2048]{3,2,1,0:T(8,128)(2,1)S(1)} all-to-all(bf16[16,1,16,2048]{3,2,1,0:T(8,128)(2,1)S(1)} %bitcast.184), channel_id=1, replica_groups=mesh['seq'=16,'z'=8,'core'=2] {'z','core'}, dimensions={0} | all-to-all | bytes 2097152 | tf_op jit(solution)/shard_map/all_to_all | solution.py:224
  355.7 4.0 %fusion.20 = bf16[1,16,16,2048]{3,2,0,1:T(8,128)(2,1)} fusion(bf16[1,512,2048]{2,1,0:T(8,128)(2,1)S(1)} %copy-done, bf16[1,2048,512]{2,1,0:T(8,128)(2,1)} %param.36, bf16[16,1,16,2048]{3,2,1,0:T(8,128)(2,1)S(1)} %all_to_all.8, f32[16,16,512]{2,1,0:T(8,128)} %fusion.46), kind=kOutput, calls=%fused_computation.30 | convolution fusion | flops 1075052544 | bytes 6815744 | tf_op jit(solution)/shard_map/esnf,efd->esnd/dot_general | solution.py:228
  359.7 3.7 all-to-all-start.1
  363.6 27.1 %all-to-all-done.1 = bf16[1,16,16,2048]{3,2,0,1:T(8,128)(2,1)S(1)} async-done(((bf16[1,16,16,2048]{3,2,0,1:T(8,128)(2,1)}), bf16[1,16,16,2048]{3,2,0,1:T(8,128)(2,1)S(1)}, u32[]{:S(2)}, u32[]{:S(2)}) %all-to-all-start.1) | async-done | bytes 1048608 | tf_op jit(solution)/shard_map/all_to_all | solution.py:231
  (204 shorter events, 75.3 us)
Async XLA Ops:
  6.5 349.1 %copy-start = (bf16[1,512,2048]{2,1,0:T(8,128)(2,1)S(1)}, bf16[1,512,2048]{2,1,0:T(8,128)(2,1)}, u32[]{:S(2)}) copy-start(bf16[1,512,2048]{2,1,0:T(8,128)(2,1)} %param.37) | copy-start | bytes 6291460
  6.5 43.2 %copy-start.23 = (f32[1024,2]{0,1:T(2,128)S(1)}, f32[1024,2]{0,1:T(2,128)}, u32[]{:S(2)}) copy-start(f32[1024,2]{0,1:T(2,128)} %param.29) | copy-start | bytes 24580
  6.5 43.3 %copy-start.24 = (f32[1024,2]{0,1:T(2,128)S(1)}, f32[1024,2]{0,1:T(2,128)}, u32[]{:S(2)}) copy-start(f32[1024,2]{0,1:T(2,128)} %param.28) | copy-start | bytes 24580
  6.5 43.9 %copy-start.29 = (f32[4,128]{1,0:T(4,128)S(1)}, f32[4,128]{1,0:T(4,128)}, u32[]{:S(2)}) copy-start(f32[4,128]{1,0:T(4,128)} %param.25) | copy-start | bytes 6148
  6.5 43.9 %copy-start.30 = (f32[4,128]{1,0:T(4,128)S(1)}, f32[4,128]{1,0:T(4,128)}, u32[]{:S(2)}) copy-start(f32[4,128]{1,0:T(4,128)} %param.26) | copy-start | bytes 6148
  6.5 43.9 %copy-start.27 = (f32[4,256]{1,0:T(4,128)S(1)}, f32[4,256]{1,0:T(4,128)}, u32[]{:S(2)}) copy-start(f32[4,256]{1,0:T(4,128)} %param.27) | copy-start | bytes 12292
  6.6 43.1 %all-gather.5.cloned.1.call-start = ((), (), s32[]{:S(2)}) async-start(), calls=%async_computation.6 | async-start | bytes 2359296 | tf_op jit(solution)/shard_map/all_gather | solution.py:115
  7.3 66.7 %all-gather.7.cloned.1.call-start = ((), (), s32[]{:S(2)}) async-start(), calls=%async_computation.7 | async-start | bytes 6291456 | tf_op jit(solution)/shard_map/all_gather | solution.py:116
  49.7 222.0 %reduce-scatter.3.cloned.1.call-start = ((), (), s32[]{:S(2)}) async-start(), calls=%async_computation.4 | async-start | bytes 6291456 | tf_op jit(solution)/shard_map/reduce_scatter | solution.py:201
  80.4 3.4 copy-start.1
  80.4 3.4 copy-start.21
  85.2 2.2 copy-start.7
  88.8 5.5 %collective-permute-start = (bf16[3,512]{0,1:T(8,128)(2,1)S(1)}, bf16[3,512]{0,1:T(8,128)(2,1)S(1)}, u32[]{:S(2)}, u32[]{:S(2)}) collective-permute-start(bf16[3,512]{0,1:T(8,128)(2,1)S(1)} %pad_maximum_fusion.6), channel_id=1, source_target_pairs={{0,16},{16,32},{32,48},{48,64},{64,80},{80,96},{96,112},{112,128},... | collective-permute-start | bytes 9224 | tf_op jit(solution)/shard_map/ppermute | solution.py:19
  107.9 2.2 copy-start.19
  129.7 4.3 %copy-start.3 = (f32[2,16,64,256]{3,2,1,0:T(8,128)}, f32[2,16,64,256]{3,2,1,0:T(8,128)S(1)}, u32[]{:S(2)}) copy-start(f32[2,16,64,256]{3,2,1,0:T(8,128)S(1)} %fusion.35) | copy-start | bytes 6291460
  138.7 4.5 %copy-start.9 = (f32[2,1,128,128]{3,2,1,0:T(8,128)}, f32[2,1,128,128]{3,2,1,0:T(8,128)S(1)}, u32[]{:S(2)}) copy-start(f32[2,1,128,128]{3,2,1,0:T(8,128)S(1)} %broadcast_in_dim.100) | copy-start | bytes 393220
  162.1 8.7 %collective-permute-start.1 = (f32[2,2,128,128]{3,2,1,0:T(8,128)S(1)}, f32[2,2,128,128]{3,2,1,0:T(8,128)S(1)}, u32[]{:S(2)}, u32[]{:S(2)}) collective-permute-start(f32[2,2,128,128]{3,2,1,0:T(8,128)S(1)} %pad_maximum_fusion), channel_id=1, source_target_pairs={{0,16},{16,32},{32,48},{48,64},{64,80},{80,96},{96,112},{112,128},... | collective-permute-start | bytes 786440 | tf_op jit(solution)/shard_map/ppermute | solution.py:19
  173.1 9.4 %collective-permute-start.2 = (f32[2,2,128,128]{3,2,1,0:T(8,128)S(1)}, f32[2,2,128,128]{3,2,1,0:T(8,128)S(1)}, u32[]{:S(2)}, u32[]{:S(2)}) collective-permute-start(f32[2,2,128,128]{3,2,1,0:T(8,128)S(1)} %pad_maximum_fusion.1), channel_id=1, source_target_pairs={{0,32},{16,48},{32,64},{48,80},{64,96},{80,112},{96,128},{112,144}... | collective-permute-start | bytes 786440 | tf_op jit(solution)/shard_map/ppermute | solution.py:19
  183.7 12.8 %collective-permute-start.3 = (f32[2,2,128,128]{3,2,1,0:T(8,128)}, f32[2,2,128,128]{3,2,1,0:T(8,128)S(1)}, u32[]{:S(2)}, u32[]{:S(2)}) collective-permute-start(f32[2,2,128,128]{3,2,1,0:T(8,128)} %pad_maximum_fusion.2), channel_id=1, source_target_pairs={{0,64},{16,80},{32,96},{48,112},{64,128},{80,144},{96,160},{112,17... | collective-permute-start | bytes 786440 | tf_op jit(solution)/shard_map/ppermute | solution.py:19
  196.9 7.9 %copy-start.11 = (f32[2,128,128]{2,1,0:T(8,128)}, f32[2,128,128]{2,1,0:T(8,128)S(1)}, u32[]{:S(2)}) copy-start(f32[2,128,128]{2,1,0:T(8,128)S(1)} %get-tuple-element.14) | copy-start | bytes 393220
  197.7 8.8 %collective-permute-start.4 = (f32[2,2,128,128]{3,2,1,0:T(8,128)}, f32[2,2,128,128]{3,2,1,0:T(8,128)}, u32[]{:S(2)}, u32[]{:S(2)}) collective-permute-start(f32[2,2,128,128]{3,2,1,0:T(8,128)} %pad_maximum_fusion.3), channel_id=1, source_target_pairs={{0,128},{16,144},{32,160},{48,176},{64,192},{80,208},{96,224},{112... | collective-permute-start | bytes 786440 | tf_op jit(solution)/shard_map/ppermute | solution.py:19
  208.7 5.9 %collective-permute-start.5 = (f32[2,128,128]{2,1,0:T(8,128)S(1)}, f32[2,128,128]{2,1,0:T(8,128)S(1)}, u32[]{:S(2)}, u32[]{:S(2)}) collective-permute-start(f32[2,128,128]{2,1,0:T(8,128)S(1)} %fusion.64), channel_id=1, source_target_pairs={{0,16},{16,32},{32,48},{48,64},{64,80},{80,96},{96,112},{112,128},... | collective-permute-start | bytes 393224 | tf_op jit(solution)/shard_map/ppermute | solution.py:19
  212.7 2.2 slice-start
  214.5 2.3 copy-start.4
  216.9 4.2 %copy-start.12 = (f32[16,64,2]{1,0,2:T(8,128)S(1)}, f32[16,64,2]{1,0,2:T(8,128)}, u32[]{:S(2)}) copy-start(f32[16,64,2]{1,0,2:T(8,128)} %get-tuple-element.25) | copy-start | bytes 24580
  226.8 4.3 %copy-start.36 = (f32[256]{0:T(256)S(1)}, f32[256]{0:T(256)}, u32[]{:S(2)}) copy-start(f32[256]{0:T(256)} %broadcast_bitcast_fusion) | copy-start | bytes 3076
  245.5 26.2 %copy-start.26 = (s32[64,2]{0,1:T(2,128)S(1)}, s32[64,2]{0,1:T(2,128)}, u32[]{:S(2)}) copy-start(s32[64,2]{0,1:T(2,128)} %param.33) | copy-start | bytes 1540
  245.5 67.0 %reduce-scatter.5.cloned.1.call-start = ((), (), s32[]{:S(2)}) async-start(), calls=%async_computation.5 | async-start | bytes 2359296 | tf_op jit(solution)/shard_map/reduce_scatter | solution.py:202
  271.6 42.0 %copy-start.22 = (f32[2048]{0:T(1024)S(1)}, f32[2048]{0:T(1024)}, u32[]{:S(2)}) copy-start(f32[2048]{0:T(1024)} %param.32) | copy-start | bytes 24580
  315.2 38.9 %copy-start.32 = (bf16[1,2048,512]{2,1,0:T(8,128)(2,1)S(1)}, bf16[1,2048,512]{2,1,0:T(8,128)(2,1)}, u32[]{:S(2)}) copy-start(bf16[1,2048,512]{2,1,0:T(8,128)(2,1)} %param.35) | copy-start | bytes 6291460
  359.7 31.0 %copy-start.31 = (f32[64,2]{0,1:T(2,128)S(1)}, f32[64,2]{0,1:T(2,128)}, u32[]{:S(2)}) copy-start(f32[64,2]{0,1:T(2,128)} %param.34) | copy-start | bytes 1540
  359.7 31.0 %all-to-all-start.1 = ((bf16[1,16,16,2048]{3,2,0,1:T(8,128)(2,1)}), bf16[1,16,16,2048]{3,2,0,1:T(8,128)(2,1)S(1)}, u32[]{:S(2)}, u32[]{:S(2)}) async-start(bf16[1,16,16,2048]{3,2,0,1:T(8,128)(2,1)} %fusion.20), calls=%async_computation.3 | async-start | bytes 2097152 | tf_op jit(solution)/shard_map/all_to_all | solution.py:231
  (17 other events, 24.0 us)
Sparse Core Ops, SparseCore 0:
  9.2 40.4 all-gather.4
  51.4 22.4 all-gather.6
  245.6 25.9 reduce-scatter.2
  274.0 38.3 reduce-scatter.4

commit v2 on v0

--- a/solution.py
+++ b/solution.py
@@ -6,10 +6,11 @@
 DK = 128
 DV = 128
 STRETCH = 64
+RADIX = 4
 
 
 EPS = 1e-06
-HIGH = lax.Precision.HIGHEST
+HIGH = lax.Precision.HIGH
 
 
 def passed_along(block, axis, distance):
@@ -29,6 +30,72 @@
 def unit_heads(values, heads):
     shaped = values.reshape(values.shape[0], heads, -1)
     return shaped * lax.rsqrt(jnp.sum(shaped * shaped, -1, keepdims=True) + EPS)
+
+
+def unit_lower_inverse(strict):
+    size = strict.shape[-1]
+    rows = lax.broadcasted_iota(jnp.int32, (size, size), 0)
+    cols = lax.broadcasted_iota(jnp.int32, (size, size), 1)
+    inverse = jnp.broadcast_to(jnp.eye(size, dtype=strict.dtype), strict.shape)
+    span = 1
+    while span < size:
+        pick = (
+            (rows // (2 * span) == cols // (2 * span))
+            & ((rows // span) % 2 == 1)
+            & ((cols // span) % 2 == 0)
+        )
+        coupling = jnp.where(pick, strict, 0.0)
+        spread = lax.optimization_barrier(mix("...ij,...jk->...ik", coupling, inverse))
+        inverse = inverse - lax.optimization_barrier(mix("...ij,...jk->...ik", inverse, spread))
+        span *= 2
+    return inverse
+
+
+def compose(first_map, first_add, then_map, then_add):
+    stacked = jnp.concatenate([first_map, first_add], -2)
+    moved = mix("...kl,...lm->...km", stacked, then_map)
+    rows = first_map.shape[-2]
+    return moved[..., :rows, :], moved[..., rows:, :] + then_add
+
+
+def block_prefix(maps, adds):
+    count = maps.shape[1]
+    eye = jnp.eye(maps.shape[-1], dtype=maps.dtype)
+    shift = 1
+    while shift < count:
+        pad_map = jnp.broadcast_to(eye, maps[:, :shift].shape)
+        pad_add = jnp.zeros_like(adds[:, :shift])
+        prev_map = jnp.concatenate([pad_map, maps[:, :-shift]], 1)
+        prev_add = jnp.concatenate([pad_add, adds[:, :-shift]], 1)
+        maps, adds = compose(prev_map, prev_add, maps, adds)
+        shift *= 2
+    return maps, adds
+
+
+def shard_prefix(total_map, total_add):
+    place = lax.axis_index("seq")
+    count = lax.axis_size("seq")
+    eye = jnp.broadcast_to(jnp.eye(total_map.shape[-1], dtype=total_map.dtype), total_map.shape)
+
+    def fetch(maps, adds, shift):
+        got = passed_along(jnp.stack([maps, adds]), "seq", shift)
+        valid = place >= shift
+        return jnp.where(valid, got[0], eye), jnp.where(valid, got[1], 0.0)
+
+    maps, adds = total_map, total_add
+    window = 1
+    while window * RADIX < count:
+        parts = [fetch(maps, adds, window * step) for step in range(RADIX - 1, 0, -1)]
+        for prev_map, prev_add in parts[1:] + [(maps, adds)]:
+            parts[0] = compose(parts[0][0], parts[0][1], prev_map, prev_add)
+        maps, adds = parts[0]
+        window *= RADIX
+    shifts = list(range(1, count, window))[::-1]
+    parts = [fetch(maps, adds, shift) for shift in shifts]
+    run_map, run_add = parts[0]
+    for prev_map, prev_add in parts[1:]:
+        run_map, run_add = compose(run_map, run_add, prev_map, prev_add)
+    return run_add
 
 
 def per_device(
@@ -99,44 +166,26 @@
     spread_log = cumul[..., :, None] - cumul[..., None, :]
     ratio_incl = jnp.where(lower_incl, jnp.exp(jnp.where(lower_incl, spread_log, 0.0)), 0.0)
     key_gram = mix("hnid,hnjd->hnij", k_blk, k_blk)
-    system = jnp.eye(STRETCH, dtype=jnp.float32) + jnp.where(
-        lower_strict, b_blk[..., None] * key_gram * ratio_incl, 0.0
-    )
+    strict = jnp.where(lower_strict, b_blk[..., None] * key_gram * ratio_incl, 0.0)
+    inverse = unit_lower_inverse(strict)
     decay_in = jnp.exp(cumul)[..., None]
     right_side = jnp.concatenate(
         [b_blk[..., None] * decay_in * k_blk, b_blk[..., None] * v_blk], -1
     )
-    solved = jax.scipy.linalg.solve_triangular(system, right_side, lower=True, unit_diagonal=True)
+    solved = mix("hnij,hnjc->hnic", inverse, right_side)
     w_mat = solved[..., :DK]
     u_mat = solved[..., DK:]
     key_tail = k_blk * jnp.exp(last_cum - cumul)[..., None]
     eye_key = jnp.eye(DK, dtype=jnp.float32)
     transit = jnp.exp(last_cum)[..., None] * eye_key - mix("hnik,hnil->hnkl", w_mat, key_tail)
     inject = mix("hniv,hnik->hnvk", u_mat, key_tail)
-
-    def local_step(carry, pair):
-        map_pre, add_pre = carry
-        map_now, add_now = pair
-        new_carry = (
-            mix("hkl,hlm->hkm", map_pre, map_now),
-            mix("hvl,hlm->hvm", add_pre, map_now) + add_now,
-        )
-        return (new_carry, carry)
-
-    ident_maps = jnp.broadcast_to(eye_key, (value_heads, DK, DK))
-    zero_add = jnp.zeros((value_heads, DV, DK), jnp.float32)
-    (map_total, add_total), (map_prefix, add_prefix) = lax.scan(
-        local_step,
-        (ident_maps, zero_add),
-        (transit.transpose(1, 0, 2, 3), inject.transpose(1, 0, 2, 3)),
-    )
-
-    def relay(step_index, state):
-        passed = mix("hvk,hkl->hvl", state, map_total) + add_total
-        return passed_along(passed.astype(jnp.bfloat16), "seq", 1).astype(passed.dtype)
-
-    incoming = lax.fori_loop(0, lax.axis_size("seq") - 1, relay, zero_add)
-    starts = (mix("hvk,nhkl->nhvl", incoming, map_prefix) + add_prefix).transpose(1, 0, 2, 3)
+    map_incl, add_incl = block_prefix(transit, inject)
+    ident_maps = jnp.broadcast_to(eye_key, (value_heads, 1, DK, DK))
+    zero_add = jnp.zeros((value_heads, 1, DV, DK), jnp.float32)
+    map_prefix = jnp.concatenate([ident_maps, map_incl[:, :-1]], 1)
+    add_prefix = jnp.concatenate([zero_add, add_incl[:, :-1]], 1)
+    incoming = shard_prefix(map_incl[:, -1], add_incl[:, -1])
+    starts = mix("hvk,hnkl->hnvl", incoming, map_prefix) + add_prefix
     new_values = u_mat - mix("hnik,hnvk->hniv", w_mat, starts)
     scores = mix("hnid,hnjd->hnij", q_blk, k_blk) * ratio_incl
     out_blk = decay_in * mix("hnik,hnvk->hniv", q_blk, starts) + mix(

time: 653 us -> 349 us (0.53)
  other arithmetic: 191 us -> 23.4 us
  starting transfers between devices: 86.6 us -> 34 us
  matrix products: 95 us -> 56.4 us
  waiting for transfers between devices: 180 us -> 152 us
  local copies, waits for them, and re-layouts: 38.7 us -> 26.4 us
    another operation x6 -> x3, other arithmetic: 160 us -> 0.77 us  [fetch(): got = passed_along(jnp.stack([maps, adds]), 'seq', shift)]
    ppermute x16 -> x8, starting transfers between devices: 82.8 us -> 30.3 us  [passed_along(): return lax.ppermute(block, axis, route)]
    dot_general x55 -> x31, matrix products: 72.8 us -> 36.2 us  [mix(): return jnp.einsum(form, left_arr, right_arr, precision=HIGH)]
    reduce_scatter x1, waiting for transfers between devices: 84.1 us -> 67.6 us  [per_device(): lax.psum_scatter(jnp.dot(gated, w_out, preferred_element_type=jnp.float32...]
    dynamic_slice x32 -> x0, local copies, waits for them, and re-layouts: 16.1 us -> none  [per_device(): lax.scan(local_step, (ident_maps, zero_add), (transit.transpose(1, 0, 2,...]
    ppermute x16 -> x8, waiting for transfers between devices: 21.6 us -> 6.35 us  [passed_along(): return lax.ppermute(block, axis, route)]
    dynamic_update_slice x16 -> x0, other arithmetic: 11.9 us -> none  [per_device(): lax.scan(local_step, (ident_maps, zero_add), (transit.transpose(1, 0, 2,...]
  transfers between devices with their start and end apart: 19 -> 11, of which waited for: 19 -> 6; matrix products, arithmetic and copies ran while one was open for 2% -> 4% of each run, Pallas kernels for 0% -> 0%
where the time goes in v2:
time: 349 us; the launch traced here: 343 us
  waiting for transfers between devices  152 us (44%)
  matrix products  56.4 us (16%)
  blocking collectives  36.1 us (10%)
  starting transfers between devices  34 us (10%)
  local copies, waits for them, and re-layouts  26.4 us (8%)
  other arithmetic  23.4 us (7%)
  between operations  14.6 us (4%)
    reduce_scatter x1, waiting for transfers between devices, per_device(): lax.psum_scatter(jnp.dot(gated, w_out, preferred_element_type=jnp.float32...  67.6 us
    all_gather x1, waiting for transfers between devices, per_device(): whole = lax.all_gather(tokens, 'exp', axis=1, tiled=True)  50.6 us
    dot_general x31, matrix products, mix(): return jnp.einsum(form, left_arr, right_arr, precision=HIGH)  36.2 us
    all_to_all x1, blocking collectives, per_device(): lax.all_to_all(outgoing, 'exp', split_axis=0, concat_axis=1, tiled=True)  36.1 us
    ppermute x8, starting transfers between devices, passed_along(): return lax.ppermute(block, axis, route)  30.3 us
    all_to_all x1, waiting for transfers between devices, per_device(): lax.all_to_all(processed, 'exp', split_axis=1, concat_axis=0, tiled=True)  27.1 us
    dot_general x1, matrix products, per_device(): jnp.dot(gated, w_out, preferred_element_type=jnp.float32)  9.49 us
  transfers between devices with their start and end apart: 11, of which 6 were waited for; matrix products, arithmetic and copies ran while one was open for 4% of the time, Pallas kernels for 0%

profile of v2, /device:TPU:1, one launch (start us, length us, event | category | flops | bytes accessed | tf_op | source)
XLA Modules:
  0.0 343.3 jit_solution(697484664038385160)
XLA Ops:
  12.0 50.6 %all-gather.2.cloned.1.call-done = bf16[1024,2048]{1,0:T(8,128)(2,1)} async-done(((bf16[1024,128]{1,0:T(8,128)(2,1)}), bf16[1024,2048]{1,0:T(8,128)(2,1)}) %all-gather.2.cloned.1.call-update) | async-done | bytes 4194320 | tf_op jit(solution)/shard_map/all_gather | solution.py:122
  62.6 3.2 fusion
  71.9 2.8 collective-permute-start
  74.7 2.5 collective-permute-done
  77.9 2.4 divide_multiply_fusion
  94.5 3.2 reshape.224
  97.7 3.3 copy.60
  104.0 2.2 fusion.53
  106.2 2.4 multiply_subtract_fusion
  109.0 2.3 fusion.9
  112.1 2.3 fusion.7
  115.1 2.4 fusion.5
  118.1 2.2 fusion.3
  120.6 1.7 copy-done.3
  124.3 6.1 %collective-permute-start.1 = (f32[2,2,128,128]{3,2,1,0:T(8,128)}, f32[2,2,128,128]{3,2,1,0:T(8,128)}, u32[]{:S(2)}, u32[]{:S(2)}) collective-permute-start(f32[2,2,128,128]{3,2,1,0:T(8,128)} %pad_maximum_fusion), channel_id=1, source_target_pairs={{0,48},{16,64},{32,80},{48,96},{64,112},{80,128},{96,144},{112,160... | collective-permute-start | bytes 786440 | tf_op jit(solution)/shard_map/ppermute | solution.py:19
  130.4 4.0 %collective-permute-start.2 = (f32[2,2,128,128]{3,2,1,0:T(8,128)}, f32[2,2,128,128]{3,2,1,0:T(8,128)}, u32[]{:S(2)}, u32[]{:S(2)}) collective-permute-start(f32[2,2,128,128]{3,2,1,0:T(8,128)} %pad_maximum_fusion), channel_id=1, source_target_pairs={{0,32},{16,48},{32,64},{48,80},{64,96},{80,112},{96,128},{112,144}... | collective-permute-start | bytes 786440 | tf_op jit(solution)/shard_map/ppermute | solution.py:19
  134.4 2.6 collective-permute-start.3
  137.0 3.1 slice.271
  147.9 5.1 %collective-permute-start.4 = (f32[2,2,128,128]{3,2,1,0:T(8,128)S(1)}, f32[2,2,128,128]{3,2,1,0:T(8,128)S(1)}, u32[]{:S(2)}, u32[]{:S(2)}) collective-permute-start(f32[2,2,128,128]{3,2,1,0:T(8,128)S(1)} %pad_maximum_fusion.1), channel_id=1, source_target_pairs={{0,208},{16,224},{32,240},{1,209},{17,225},{33,241},{2,210},{18,22... | collective-permute-start | bytes 786440 | tf_op jit(solution)/shard_map/ppermute | solution.py:19
  155.6 3.6 %collective-permute-start.6 = (f32[2,2,128,128]{3,2,1,0:T(8,128)S(1)}, f32[2,2,128,128]{3,2,1,0:T(8,128)S(1)}, u32[]{:S(2)}, u32[]{:S(2)}) collective-permute-start(f32[2,2,128,128]{3,2,1,0:T(8,128)S(1)} %pad_maximum_fusion.1), channel_id=1, source_target_pairs={{0,80},{16,96},{32,112},{48,128},{64,144},{80,160},{96,176},{112,1... | collective-permute-start | bytes 786440 | tf_op jit(solution)/shard_map/ppermute | solution.py:19
  159.2 4.5 %collective-permute-start.7 = (f32[2,2,128,128]{3,2,1,0:T(8,128)S(1)}, f32[2,2,128,128]{3,2,1,0:T(8,128)S(1)}, u32[]{:S(2)}, u32[]{:S(2)}) collective-permute-start(f32[2,2,128,128]{3,2,1,0:T(8,128)S(1)} %pad_maximum_fusion.1), channel_id=1, source_target_pairs={{0,16},{16,32},{32,48},{48,64},{64,80},{80,96},{96,112},{112,128},... | collective-permute-start | bytes 786440 | tf_op jit(solution)/shard_map/ppermute | solution.py:19
  165.6 2.6 collective-permute-done.7
  170.0 2.2 convolution_subtract_fusion
  172.3 2.2 fusion.57
  176.5 1.8 copy.64
  179.6 9.5 %convolution_convert_fusion = bf16[1024,2048]{1,0:T(8,128)(2,1)} fusion(bf16[256,2048]{1,0:T(8,128)(2,1)} %param.31, bf16[1024,2048]{1,0:T(8,128)(2,1)} %copy-done.1, bf16[2048,256]{1,0:T(8,128)(2,1)} %param.24, f32[128,8,2,128]{3,2,1,0:T(2,128)S(1)} %bitcast.203, f32[128,8,2,128]{3,2,1,0:T(2,128)} %bitcast.204, f32[256]{0:T(256)S(1)} %broadcast_bitcast_fusion), kind=kOutput, calls=%fused_computation.30 | convolution fusion | flops 2152202240 | bytes 12583936 | tf_op jit(solution)/shard_map/dot_general | solution.py:204
  190.4 67.6 %reduce-scatter.2.cloned.1.call-done = bf16[64,2048]{1,0:T(8,128)(2,1)} async-done(((bf16[1024,2048]{1,0:T(8,128)(2,1)}), bf16[64,2048]{1,0:T(8,128)(2,1)}) %reduce-scatter.2.cloned.1.call-update) | async-done | bytes 262160 | tf_op jit(solution)/shard_map/reduce_scatter | solution.py:203
  261.5 36.1 %all_to_all.8 = bf16[16,1,16,2048]{3,2,1,0:T(8,128)(2,1)S(1)} all-to-all(bf16[16,1,16,2048]{3,2,1,0:T(8,128)(2,1)S(1)} %bitcast.201), channel_id=1, replica_groups=mesh['seq'=16,'exp'=16] {'exp'}, dimensions={0} | all-to-all | bytes 2097152 | tf_op jit(solution)/shard_map/all_to_all | solution.py:228
  299.1 4.0 %fusion.23 = bf16[1,16,16,2048]{3,2,0,1:T(8,128)(2,1)} fusion(bf16[1,512,2048]{2,1,0:T(8,128)(2,1)S(1)} %copy-done, bf16[1,2048,512]{2,1,0:T(8,128)(2,1)} %param.36, bf16[16,1,16,2048]{3,2,1,0:T(8,128)(2,1)S(1)} %all_to_all.8, f32[16,16,512]{2,1,0:T(8,128)} %fusion.49), kind=kOutput, calls=%fused_computation.33 | convolution fusion | flops 1075052544 | bytes 6815744 | tf_op jit(solution)/shard_map/esnf,efd->esnd/dot_general | solution.py:232
  303.2 3.7 %all-to-all-start.1 = ((bf16[1,16,16,2048]{3,2,0,1:T(8,128)(2,1)}), bf16[1,16,16,2048]{3,2,0,1:T(8,128)(2,1)S(1)}, u32[]{:S(2)}, u32[]{:S(2)}) async-start(bf16[1,16,16,2048]{3,2,0,1:T(8,128)(2,1)} %fusion.23), calls=%async_computation.2 | async-start | bytes 2097152 | tf_op jit(solution)/shard_map/all_to_all | solution.py:235
  307.1 27.1 %all-to-all-done.1 = bf16[1,16,16,2048]{3,2,0,1:T(8,128)(2,1)S(1)} async-done(((bf16[1,16,16,2048]{3,2,0,1:T(8,128)(2,1)}), bf16[1,16,16,2048]{3,2,0,1:T(8,128)(2,1)S(1)}, u32[]{:S(2)}, u32[]{:S(2)}) %all-to-all-start.1) | async-done | bytes 1048608 | tf_op jit(solution)/shard_map/all_to_all | solution.py:235
  334.6 1.7 add_convert_fusion
  (180 shorter events, 57.5 us)
Async XLA Ops:
  6.5 292.6 %copy-start = (bf16[1,512,2048]{2,1,0:T(8,128)(2,1)S(1)}, bf16[1,512,2048]{2,1,0:T(8,128)(2,1)}, u32[]{:S(2)}) copy-start(bf16[1,512,2048]{2,1,0:T(8,128)(2,1)} %param.37) | copy-start | bytes 6291460
  6.5 56.1 %all-gather.2.cloned.1.call-start = ((), (), s32[]{:S(2)}) async-start(), calls=%async_computation.3 | async-start | bytes 4456448 | tf_op jit(solution)/shard_map/all_gather | solution.py:122
  7.3 250.7 %reduce-scatter.2.cloned.1.call-start = ((), (), s32[]{:S(2)}) async-start(), calls=%async_computation.4 | async-start | bytes 4456448 | tf_op jit(solution)/shard_map/reduce_scatter | solution.py:203
  12.0 53.9 %copy-start.20 = (f32[2048]{0:T(1024)S(1)}, f32[2048]{0:T(1024)}, u32[]{:S(2)}) copy-start(f32[2048]{0:T(1024)} %param.20) | copy-start | bytes 24580
  62.6 3.4 %copy-start.2 = (bf16[1024,2048]{1,0:T(8,128)(2,1)S(1)}, bf16[1024,2048]{1,0:T(8,128)(2,1)}, u32[]{:S(2)}) copy-start(bf16[1024,2048]{1,0:T(8,128)(2,1)} %all-gather.2.cloned.1.call-done) | copy-start | bytes 12582916
  67.3 2.9 copy-start.1
  71.9 5.4 %collective-permute-start = (bf16[3,512]{0,1:T(8,128)(2,1)S(1)}, bf16[3,512]{0,1:T(8,128)(2,1)S(1)}, u32[]{:S(2)}, u32[]{:S(2)}) collective-permute-start(bf16[3,512]{0,1:T(8,128)(2,1)S(1)} %pad_maximum_fusion.4), channel_id=1, source_target_pairs={{0,16},{16,32},{32,48},{48,64},{64,80},{80,96},{96,112},{112,128},... | collective-permute-start | bytes 9224 | tf_op jit(solution)/shard_map/ppermute | solution.py:19
  82.6 1.6 copy-start.6
  91.5 1.6 copy-start.7
  101.0 1.7 copy-start.13
  101.0 1.9 copy-start.14
  104.0 4.6 %copy-start.4 = (f32[2,16,64,256]{3,2,1,0:T(8,128)}, f32[2,16,64,256]{3,2,1,0:T(8,128)S(1)}, u32[]{:S(2)}) copy-start(f32[2,16,64,256]{3,2,1,0:T(8,128)S(1)} %fusion.38) | copy-start | bytes 6291460
  120.3 2.0 copy-start.3
  120.3 10.1 %copy-start.26 = (f32[128]{0:T(128)S(1)}, f32[128]{0:T(128)}, u32[]{:S(2)}) copy-start(f32[128]{0:T(128)} %param.30) | copy-start | bytes 1540
  124.3 16.0 %collective-permute-start.1 = (f32[2,2,128,128]{3,2,1,0:T(8,128)}, f32[2,2,128,128]{3,2,1,0:T(8,128)}, u32[]{:S(2)}, u32[]{:S(2)}) collective-permute-start(f32[2,2,128,128]{3,2,1,0:T(8,128)} %pad_maximum_fusion), channel_id=1, source_target_pairs={{0,48},{16,64},{32,80},{48,96},{64,112},{80,128},{96,144},{112,160... | collective-permute-start | bytes 786440 | tf_op jit(solution)/shard_map/ppermute | solution.py:19
  130.4 11.9 %collective-permute-start.2 = (f32[2,2,128,128]{3,2,1,0:T(8,128)}, f32[2,2,128,128]{3,2,1,0:T(8,128)}, u32[]{:S(2)}, u32[]{:S(2)}) collective-permute-start(f32[2,2,128,128]{3,2,1,0:T(8,128)} %pad_maximum_fusion), channel_id=1, source_target_pairs={{0,32},{16,48},{32,64},{48,80},{64,96},{80,112},{96,128},{112,144}... | collective-permute-start | bytes 786440 | tf_op jit(solution)/shard_map/ppermute | solution.py:19
  134.4 10.1 %collective-permute-start.3 = (f32[2,2,128,128]{3,2,1,0:T(8,128)}, f32[2,2,128,128]{3,2,1,0:T(8,128)}, u32[]{:S(2)}, u32[]{:S(2)}) collective-permute-start(f32[2,2,128,128]{3,2,1,0:T(8,128)} %pad_maximum_fusion), channel_id=1, source_target_pairs={{0,16},{16,32},{32,48},{48,64},{64,80},{80,96},{96,112},{112,128},... | collective-permute-start | bytes 786440 | tf_op jit(solution)/shard_map/ppermute | solution.py:19
  137.0 3.1 copy-start.17
  140.3 7.5 %copy-start.11 = (f32[2,16,128,128]{3,2,1,0:T(8,128)S(1)}, f32[2,16,128,128]{3,2,1,0:T(8,128)}, u32[]{:S(2)}) copy-start(f32[2,16,128,128]{3,2,1,0:T(8,128)} %copy-done.10) | copy-start | bytes 6291460
  143.5 9.5 %copy-start.9 = (f32[1024,128]{1,0:T(8,128)S(1)}, f32[1024,128]{1,0:T(8,128)}, u32[]{:S(2)}) copy-start(f32[1024,128]{1,0:T(8,128)} %copy-done.6) | copy-start | bytes 1572868
  147.9 15.9 %collective-permute-start.4 = (f32[2,2,128,128]{3,2,1,0:T(8,128)S(1)}, f32[2,2,128,128]{3,2,1,0:T(8,128)S(1)}, u32[]{:S(2)}, u32[]{:S(2)}) collective-permute-start(f32[2,2,128,128]{3,2,1,0:T(8,128)S(1)} %pad_maximum_fusion.1), channel_id=1, source_target_pairs={{0,208},{16,224},{32,240},{1,209},{17,225},{33,241},{2,210},{18,22... | collective-permute-start | bytes 786440 | tf_op jit(solution)/shard_map/ppermute | solution.py:19
  154.0 14.4 %slice-start = ((f32[2,16,128,128]{3,2,1,0:T(8,128)}), f32[2,15,128,128]{3,2,1,0:T(8,128)S(1)}, s32[]{:S(2)}) async-start(f32[2,16,128,128]{3,2,1,0:T(8,128)} %copy-done.10), calls=%async_computation.5 | async-start | bytes 3932160 | tf_op jit(solution)/shard_map/slice | solution.py:186
  154.0 14.4 %copy-start.12 = (f32[2,15,128,128]{3,2,1,0:T(8,128)S(1)}, f32[2,15,128,128]{3,2,1,0:T(8,128)}, u32[]{:S(2)}) copy-start(f32[2,15,128,128]{3,2,1,0:T(8,128)} %slice.271) | copy-start | bytes 5898244
  154.0 9.8 %collective-permute-start.5 = (f32[2,2,128,128]{3,2,1,0:T(8,128)S(1)}, f32[2,2,128,128]{3,2,1,0:T(8,128)S(1)}, u32[]{:S(2)}, u32[]{:S(2)}) collective-permute-start(f32[2,2,128,128]{3,2,1,0:T(8,128)S(1)} %pad_maximum_fusion.1), channel_id=1, source_target_pairs={{0,144},{16,160},{32,176},{48,192},{64,208},{80,224},{96,240},{1,1... | collective-permute-start | bytes 786440 | tf_op jit(solution)/shard_map/ppermute | solution.py:19
  155.6 9.7 %collective-permute-start.6 = (f32[2,2,128,128]{3,2,1,0:T(8,128)S(1)}, f32[2,2,128,128]{3,2,1,0:T(8,128)S(1)}, u32[]{:S(2)}, u32[]{:S(2)}) collective-permute-start(f32[2,2,128,128]{3,2,1,0:T(8,128)S(1)} %pad_maximum_fusion.1), channel_id=1, source_target_pairs={{0,80},{16,96},{32,112},{48,128},{64,144},{80,160},{96,176},{112,1... | collective-permute-start | bytes 786440 | tf_op jit(solution)/shard_map/ppermute | solution.py:19
  159.2 9.0 %collective-permute-start.7 = (f32[2,2,128,128]{3,2,1,0:T(8,128)S(1)}, f32[2,2,128,128]{3,2,1,0:T(8,128)S(1)}, u32[]{:S(2)}, u32[]{:S(2)}) collective-permute-start(f32[2,2,128,128]{3,2,1,0:T(8,128)S(1)} %pad_maximum_fusion.1), channel_id=1, source_target_pairs={{0,16},{16,32},{32,48},{48,64},{64,80},{80,96},{96,112},{112,128},... | collective-permute-start | bytes 786440 | tf_op jit(solution)/shard_map/ppermute | solution.py:19
  176.5 1.8 copy-start.16
  189.1 70.2 %copy-start.21 = (f32[2048]{0:T(1024)S(1)}, f32[2048]{0:T(1024)}, u32[]{:S(2)}) copy-start(f32[2048]{0:T(1024)} %param.32) | copy-start | bytes 24580
  260.9 36.7 %copy-start.24 = (bf16[1,2048,512]{2,1,0:T(8,128)(2,1)S(1)}, bf16[1,2048,512]{2,1,0:T(8,128)(2,1)}, u32[]{:S(2)}) copy-start(bf16[1,2048,512]{2,1,0:T(8,128)(2,1)} %param.35) | copy-start | bytes 6291460
  303.2 31.1 %copy-start.23 = (f32[64,2]{0,1:T(2,128)S(1)}, f32[64,2]{0,1:T(2,128)}, u32[]{:S(2)}) copy-start(f32[64,2]{0,1:T(2,128)} %param.34) | copy-start | bytes 1540
  303.2 31.4 %copy-start.15 = (bf16[64,2048]{1,0:T(8,128)(2,1)S(1)}, bf16[64,2048]{1,0:T(8,128)(2,1)}, u32[]{:S(2)}) copy-start(bf16[64,2048]{1,0:T(8,128)(2,1)} %reduce-scatter.2.cloned.1.call-done) | copy-start | bytes 786436
  303.2 31.0 %all-to-all-start.1 = ((bf16[1,16,16,2048]{3,2,0,1:T(8,128)(2,1)}), bf16[1,16,16,2048]{3,2,0,1:T(8,128)(2,1)S(1)}, u32[]{:S(2)}, u32[]{:S(2)}) async-start(bf16[1,16,16,2048]{3,2,0,1:T(8,128)(2,1)} %fusion.23), calls=%async_computation.2 | async-start | bytes 2097152 | tf_op jit(solution)/shard_map/all_to_all | solution.py:235
  (7 other events, 8.9 us)
Sparse Core Ops, SparseCore 0:
  9.1 53.4 all-gather.1
  189.2 68.7 reduce-scatter.1

commit v3 on v2

--- a/solution.py
+++ b/solution.py
@@ -70,6 +70,12 @@
         maps, adds = compose(prev_map, prev_add, maps, adds)
         shift *= 2
     return maps, adds
+
+
+def block_total(maps, adds):
+    while maps.shape[1] > 1:
+        maps, adds = compose(maps[:, 0::2], adds[:, 0::2], maps[:, 1::2], adds[:, 1::2])
+    return maps[:, 0], adds[:, 0]
 
 
 def shard_prefix(total_map, total_add):
@@ -123,16 +129,17 @@
     x_float = whole.astype(jnp.float32)
     normed = rms_scale(x_float, in_gain).astype(jnp.bfloat16)
 
-    def project(weight):
-        return jnp.dot(normed, weight, preferred_element_type=jnp.float32).astype(jnp.bfloat16)
-
-    projected = jnp.concatenate([project(w_query), project(w_key), project(w_value)], 1)
-    z_gate = project(w_zgate)
+    def project(rows, weight):
+        return jnp.dot(rows, weight, preferred_element_type=jnp.float32).astype(jnp.bfloat16)
+
     conv_all = jnp.concatenate([conv_query, conv_key, conv_value], 1)
     taps = conv_all.shape[0]
-    length = projected.shape[0]
-    tail = projected[length - (taps - 1) :]
+    length = normed.shape[0]
+    last_rows = normed[length - (taps - 1) :]
+    tail = jnp.concatenate([project(last_rows, w) for w in (w_query, w_key, w_value)], 1)
     before = passed_along(tail, "seq", 1)
+    projected = jnp.concatenate([project(normed, w) for w in (w_query, w_key, w_value)], 1)
+    z_gate = project(normed, w_zgate)
     extended = jnp.concatenate([before, projected], 0).astype(jnp.float32)
     conv_out = conv_all[0] * extended[0:length]
     for index in range(1, taps):
@@ -179,18 +186,18 @@
     eye_key = jnp.eye(DK, dtype=jnp.float32)
     transit = jnp.exp(last_cum)[..., None] * eye_key - mix("hnik,hnil->hnkl", w_mat, key_tail)
     inject = mix("hniv,hnik->hnvk", u_mat, key_tail)
+    total_map, total_add = block_total(transit, inject)
+    incoming = shard_prefix(total_map, total_add)
     map_incl, add_incl = block_prefix(transit, inject)
     ident_maps = jnp.broadcast_to(eye_key, (value_heads, 1, DK, DK))
     zero_add = jnp.zeros((value_heads, 1, DV, DK), jnp.float32)
     map_prefix = jnp.concatenate([ident_maps, map_incl[:, :-1]], 1)
     add_prefix = jnp.concatenate([zero_add, add_incl[:, :-1]], 1)
-    incoming = shard_prefix(map_incl[:, -1], add_incl[:, -1])
-    starts = mix("hvk,hnkl->hnvl", incoming, map_prefix) + add_prefix
-    new_values = u_mat - mix("hnik,hnvk->hniv", w_mat, starts)
     scores = mix("hnid,hnjd->hnij", q_blk, k_blk) * ratio_incl
-    out_blk = decay_in * mix("hnik,hnvk->hniv", q_blk, starts) + mix(
-        "hnij,hnjv->hniv", scores, new_values
-    )
+    reach = decay_in * q_blk - mix("hnij,hnjk->hnik", scores, w_mat)
+    carried = mix("hnik,hnlk->hnil", reach, map_prefix)
+    local = mix("hnik,hnvk->hniv", reach, add_prefix) + mix("hnij,hnjv->hniv", scores, u_mat)
+    out_blk = mix("hnil,hvl->hniv", carried, incoming) + local
     delta_out = out_blk.transpose(1, 2, 0, 3).reshape(length, value_heads, DV)
     gate_z = z_gate.astype(jnp.float32).reshape(length, value_heads, DV)
     gated = (
@@ -200,6 +207,7 @@
     )
     n_exp = lax.axis_size("exp")
     row_share = length // n_exp
+    gated = lax.optimization_barrier(gated)
     attn_rows = lax.psum_scatter(
         jnp.dot(gated, w_out, preferred_element_type=jnp.float32).astype(jnp.bfloat16),
         "exp",

time: 349 us -> 342 us (0.980)
  starting transfers between devices: 34 us -> 27.2 us
  waiting for transfers between devices: 152 us -> 147 us
    ppermute x8, starting transfers between devices: 30.3 us -> 23.5 us  [passed_along(): return lax.ppermute(block, axis, route)]
    dot_general x1, matrix products: 9.49 us -> 3.29 us  [per_device(): jnp.dot(gated, w_out, preferred_element_type=jnp.float32)]
    reduce_scatter x1, waiting for transfers between devices: 67.6 us -> 61.9 us  [per_device(): lax.psum_scatter(jnp.dot(gated, w_out, preferred_element_type=jnp.float32...]
    dot_general x3 -> x7, matrix products: 4.35 us -> 9.5 us  [project(): jnp.dot(rows, weight, preferred_element_type=jnp.float32)]
    dot_general x31 -> x36, matrix products: 36.2 us -> 37.4 us  [mix(): return jnp.einsum(form, left_arr, right_arr, precision=HIGH)]
  transfers between devices with their start and end apart: 11 -> 11, of which waited for: 6 -> 4; matrix products, arithmetic and copies ran while one was open for 4% -> 10% of each run, Pallas kernels for 0% -> 0%
where the time goes in v3:
time: 342 us; the launch traced here: 336 us
  waiting for transfers between devices  147 us (43%)
  matrix products  56.6 us (17%)
  blocking collectives  36.3 us (11%)
  starting transfers between devices  27.2 us (8%)
  local copies, waits for them, and re-layouts  26.8 us (8%)
  other arithmetic  26.8 us (8%)
  between operations  15.1 us (4%)
    reduce_scatter x1, waiting for transfers between devices, per_device(): lax.psum_scatter(jnp.dot(gated, w_out, preferred_element_type=jnp.float32...  61.9 us
    all_gather x1, waiting for transfers between devices, per_device(): whole = lax.all_gather(tokens, 'exp', axis=1, tiled=True)  49.9 us
    dot_general x36, matrix products, mix(): return jnp.einsum(form, left_arr, right_arr, precision=HIGH)  37.4 us
    all_to_all x1, blocking collectives, per_device(): lax.all_to_all(outgoing, 'exp', split_axis=0, concat_axis=1, tiled=True)  36.3 us
    all_to_all x1, waiting for transfers between devices, per_device(): lax.all_to_all(processed, 'exp', split_axis=1, concat_axis=0, tiled=True)  27.1 us
    ppermute x8, starting transfers between devices, passed_along(): return lax.ppermute(block, axis, route)  23.5 us
    dot_general x7, matrix products, project(): jnp.dot(rows, weight, preferred_element_type=jnp.float32)  9.5 us
    ppermute x8, waiting for transfers between devices, passed_along(): return lax.ppermute(block, axis, route)  7.44 us
  transfers between devices with their start and end apart: 11, of which 4 were waited for; matrix products, arithmetic and copies ran while one was open for 10% of the time, Pallas kernels for 0%

profile of v3, /device:TPU:1, one launch (start us, length us, event | category | flops | bytes accessed | tf_op | source)
XLA Modules:
  0.0 335.8 jit_solution(7417180381141633447)
XLA Ops:
  12.7 49.9 %all-gather.2.cloned.1.call-done = bf16[1024,2048]{1,0:T(8,128)(2,1)} async-done(((bf16[1024,128]{1,0:T(8,128)(2,1)}), bf16[1024,2048]{1,0:T(8,128)(2,1)}) %all-gather.2.cloned.1.call-update) | async-done | bytes 4194320 | tf_op jit(solution)/shard_map/all_gather | solution.py:128
  62.6 3.2 fusion
  69.6 2.2 convolution_convert_fusion.4
  71.9 2.8 collective-permute-start
  78.1 2.7 divide_multiply_fusion
  94.9 3.0 reshape.233
  97.9 3.3 copy.58
  101.3 1.7 bitcast_multiply_fusion.1
  104.3 2.2 fusion.57
  106.6 2.4 multiply_subtract_fusion
  112.7 3.8 %collective-permute-start.3 = (f32[2,2,128,128]{3,2,1,0:T(8,128)}, f32[2,2,128,128]{3,2,1,0:T(8,128)}, u32[]{:S(2)}, u32[]{:S(2)}) collective-permute-start(f32[2,2,128,128]{3,2,1,0:T(8,128)} %pad_maximum_fusion), channel_id=1, source_target_pairs={{0,16},{16,32},{32,48},{48,64},{64,80},{80,96},{96,112},{112,128},... | collective-permute-start | bytes 786440 | tf_op jit(solution)/shard_map/ppermute | solution.py:19
  116.5 4.3 %collective-permute-start.2 = (f32[2,2,128,128]{3,2,1,0:T(8,128)}, f32[2,2,128,128]{3,2,1,0:T(8,128)}, u32[]{:S(2)}, u32[]{:S(2)}) collective-permute-start(f32[2,2,128,128]{3,2,1,0:T(8,128)} %pad_maximum_fusion), channel_id=1, source_target_pairs={{0,32},{16,48},{32,64},{48,80},{64,96},{80,112},{96,128},{112,144}... | collective-permute-start | bytes 786440 | tf_op jit(solution)/shard_map/ppermute | solution.py:19
  120.8 4.0 %collective-permute-start.1 = (f32[2,2,128,128]{3,2,1,0:T(8,128)}, f32[2,2,128,128]{3,2,1,0:T(8,128)}, u32[]{:S(2)}, u32[]{:S(2)}) collective-permute-start(f32[2,2,128,128]{3,2,1,0:T(8,128)} %pad_maximum_fusion), channel_id=1, source_target_pairs={{0,48},{16,64},{32,80},{48,96},{64,112},{80,128},{96,144},{112,160... | collective-permute-start | bytes 786440 | tf_op jit(solution)/shard_map/ppermute | solution.py:19
  126.4 2.3 fusion.9
  129.4 2.3 fusion.7
  132.4 2.2 fusion.5
  136.4 2.2 fusion.3
  138.6 1.7 slice.362
  144.1 2.0 slice_add_fusion.3
  155.9 2.2 fusion.42
  158.1 2.5 collective-permute-start.7
  160.6 3.5 %collective-permute-start.6 = (f32[2,2,128,128]{3,2,1,0:T(8,128)S(1)}, f32[2,2,128,128]{3,2,1,0:T(8,128)S(1)}, u32[]{:S(2)}, u32[]{:S(2)}) collective-permute-start(f32[2,2,128,128]{3,2,1,0:T(8,128)S(1)} %pad_maximum_fusion.1), channel_id=1, source_target_pairs={{0,80},{16,96},{32,112},{48,128},{64,144},{80,160},{96,176},{112,1... | collective-permute-start | bytes 786440 | tf_op jit(solution)/shard_map/ppermute | solution.py:19
  165.5 7.4 %collective-permute-done.5 = f32[2,2,128,128]{3,2,1,0:T(8,128)S(1)} collective-permute-done((f32[2,2,128,128]{3,2,1,0:T(8,128)S(1)}, f32[2,2,128,128]{3,2,1,0:T(8,128)S(1)}, u32[]{:S(2)}, u32[]{:S(2)}) %collective-permute-start.5) | collective-permute-done | bytes 262176 | tf_op jit(solution)/shard_map/ppermute | solution.py:19
  174.4 2.0 multiply_reduce_fusion
  179.8 3.7 %fusion.83 = bf16[1024,256]{1,0:T(8,128)(2,1)S(1)} fusion(bf16[1024,2048]{1,0:T(8,128)(2,1)} %copy-done.1, bf16[2048,256]{1,0:T(8,128)(2,1)S(1)} %copy-done.30, f32[128,8,2,128]{3,2,1,0:T(2,128)S(1)} %bitcast.207, f32[128,8,2,128]{3,2,1,0:T(2,128)S(1)} %bitcast.208, f32[256]{0:T(256)S(1)} %broadcast_bitcast_fusion), kind=kOutput, calls=%fused_computation.109 | convolution fusion | flops 1076363264 | bytes 7865344 | tf_op jit(solution)/shard_map/dot_general | solution.py:133
  183.5 3.3 convolution_convert_fusion
  188.2 61.9 %reduce-scatter.2.cloned.1.call-done = bf16[64,2048]{1,0:T(8,128)(2,1)} async-done(((bf16[1024,2048]{1,0:T(8,128)(2,1)}), bf16[64,2048]{1,0:T(8,128)(2,1)}) %reduce-scatter.2.cloned.1.call-update) | async-done | bytes 262160 | tf_op jit(solution)/shard_map/reduce_scatter | solution.py:211
  253.6 36.3 %all_to_all.8 = bf16[16,1,16,2048]{3,2,1,0:T(8,128)(2,1)S(1)} all-to-all(bf16[16,1,16,2048]{3,2,1,0:T(8,128)(2,1)S(1)} %bitcast.205), channel_id=1, replica_groups=mesh['seq'=16,'exp'=16] {'exp'}, dimensions={0} | all-to-all | bytes 2097152 | tf_op jit(solution)/shard_map/all_to_all | solution.py:236
  291.4 4.0 %fusion.23 = bf16[1,16,16,2048]{3,2,0,1:T(8,128)(2,1)} fusion(bf16[1,512,2048]{2,1,0:T(8,128)(2,1)S(1)} %copy-done, bf16[1,2048,512]{2,1,0:T(8,128)(2,1)} %param.36, bf16[16,1,16,2048]{3,2,1,0:T(8,128)(2,1)S(1)} %all_to_all.8, f32[16,16,512]{2,1,0:T(8,128)} %fusion.53), kind=kOutput, calls=%fused_computation.33 | convolution fusion | flops 1075052544 | bytes 6815744 | tf_op jit(solution)/shard_map/esnf,efd->esnd/dot_general | solution.py:240
  295.4 3.7 %all-to-all-start.1 = ((bf16[1,16,16,2048]{3,2,0,1:T(8,128)(2,1)}), bf16[1,16,16,2048]{3,2,0,1:T(8,128)(2,1)S(1)}, u32[]{:S(2)}, u32[]{:S(2)}) async-start(bf16[1,16,16,2048]{3,2,0,1:T(8,128)(2,1)} %fusion.23), calls=%async_computation.2 | async-start | bytes 2097152 | tf_op jit(solution)/shard_map/all_to_all | solution.py:243
  299.3 27.1 %all-to-all-done.1 = bf16[1,16,16,2048]{3,2,0,1:T(8,128)(2,1)S(1)} async-done(((bf16[1,16,16,2048]{3,2,0,1:T(8,128)(2,1)}), bf16[1,16,16,2048]{3,2,0,1:T(8,128)(2,1)S(1)}, u32[]{:S(2)}, u32[]{:S(2)}) %all-to-all-start.1) | async-done | bytes 1048608 | tf_op jit(solution)/shard_map/all_to_all | solution.py:243
  326.8 1.7 add_convert_fusion
  (210 shorter events, 63.3 us)
Async XLA Ops:
  6.5 284.8 %copy-start = (bf16[1,512,2048]{2,1,0:T(8,128)(2,1)S(1)}, bf16[1,512,2048]{2,1,0:T(8,128)(2,1)}, u32[]{:S(2)}) copy-start(bf16[1,512,2048]{2,1,0:T(8,128)(2,1)} %param.37) | copy-start | bytes 6291460
  6.5 56.1 %all-gather.2.cloned.1.call-start = ((), (), s32[]{:S(2)}) async-start(), calls=%async_computation.3 | async-start | bytes 4456448 | tf_op jit(solution)/shard_map/all_gather | solution.py:128
  7.3 242.8 %reduce-scatter.2.cloned.1.call-start = ((), (), s32[]{:S(2)}) async-start(), calls=%async_computation.4 | async-start | bytes 4456448 | tf_op jit(solution)/shard_map/reduce_scatter | solution.py:211
  12.7 53.2 %copy-start.25 = (f32[2048]{0:T(1024)S(1)}, f32[2048]{0:T(1024)}, u32[]{:S(2)}) copy-start(f32[2048]{0:T(1024)} %param.20) | copy-start | bytes 24580
  62.6 3.4 %copy-start.4 = (bf16[1024,2048]{1,0:T(8,128)(2,1)S(1)}, bf16[1024,2048]{1,0:T(8,128)(2,1)}, u32[]{:S(2)}) copy-start(bf16[1024,2048]{1,0:T(8,128)(2,1)} %all-gather.2.cloned.1.call-done) | copy-start | bytes 12582916
  67.1 7.6 %copy-start.1 = (bf16[1024,2048]{1,0:T(8,128)(2,1)}, bf16[1024,2048]{1,0:T(8,128)(2,1)S(1)}, u32[]{:S(2)}) copy-start(bf16[1024,2048]{1,0:T(8,128)(2,1)S(1)} %fusion.2) | copy-start | bytes 12582916
  71.9 4.4 %collective-permute-start = (bf16[3,512]{1,0:T(4,128)(2,1)S(1)}, bf16[3,512]{1,0:T(4,128)(2,1)S(1)}, u32[]{:S(2)}, u32[]{:S(2)}) collective-permute-start(bf16[3,512]{1,0:T(4,128)(2,1)S(1)} %pad_maximum_fusion.4), channel_id=1, source_target_pairs={{0,16},{16,32},{32,48},{48,64},{64,80},{80,96},{96,112},{112,128},... | collective-permute-start | bytes 9224 | tf_op jit(solution)/shard_map/ppermute | solution.py:19
  83.1 2.4 copy-start.8
  104.3 2.3 copy-start.5
  106.5 18.3 %copy-start.2 = (f32[2,16,128,128]{3,2,1,0:T(8,128)}, f32[2,16,128,128]{3,2,1,0:T(8,128)S(1)}, u32[]{:S(2)}) copy-start(f32[2,16,128,128]{3,2,1,0:T(8,128)S(1)} %fusion.57) | copy-start | bytes 6291460
  111.7 13.1 %copy-start.19 = (f32[2,2,128,128]{3,2,1,0:T(8,128)}, f32[2,2,128,128]{3,2,1,0:T(8,128)S(1)}, u32[]{:S(2)}) copy-start(f32[2,2,128,128]{3,2,1,0:T(8,128)S(1)} %slice_add_fusion.6) | copy-start | bytes 786436
  112.7 39.4 %collective-permute-start.3 = (f32[2,2,128,128]{3,2,1,0:T(8,128)}, f32[2,2,128,128]{3,2,1,0:T(8,128)}, u32[]{:S(2)}, u32[]{:S(2)}) collective-permute-start(f32[2,2,128,128]{3,2,1,0:T(8,128)} %pad_maximum_fusion), channel_id=1, source_target_pairs={{0,16},{16,32},{32,48},{48,64},{64,80},{80,96},{96,112},{112,128},... | collective-permute-start | bytes 786440 | tf_op jit(solution)/shard_map/ppermute | solution.py:19
  116.5 33.3 %collective-permute-start.2 = (f32[2,2,128,128]{3,2,1,0:T(8,128)}, f32[2,2,128,128]{3,2,1,0:T(8,128)}, u32[]{:S(2)}, u32[]{:S(2)}) collective-permute-start(f32[2,2,128,128]{3,2,1,0:T(8,128)} %pad_maximum_fusion), channel_id=1, source_target_pairs={{0,32},{16,48},{32,64},{48,80},{64,96},{80,112},{96,128},{112,144}... | collective-permute-start | bytes 786440 | tf_op jit(solution)/shard_map/ppermute | solution.py:19
  120.8 27.1 %collective-permute-start.1 = (f32[2,2,128,128]{3,2,1,0:T(8,128)}, f32[2,2,128,128]{3,2,1,0:T(8,128)}, u32[]{:S(2)}, u32[]{:S(2)}) collective-permute-start(f32[2,2,128,128]{3,2,1,0:T(8,128)} %pad_maximum_fusion), channel_id=1, source_target_pairs={{0,48},{16,64},{32,80},{48,96},{64,112},{80,128},{96,144},{112,160... | collective-permute-start | bytes 786440 | tf_op jit(solution)/shard_map/ppermute | solution.py:19
  126.4 2.3 copy-start.3
  138.6 2.6 copy-start.7
  140.3 2.2 copy-start.10
  144.1 2.2 copy-start.6
  147.9 6.6 %copy-start.20 = (f32[2,2,128,128]{3,2,1,0:T(8,128)S(1)}, f32[2,2,128,128]{3,2,1,0:T(8,128)}, u32[]{:S(2)}) copy-start(f32[2,2,128,128]{3,2,1,0:T(8,128)} %copy-done.19) | copy-start | bytes 786436
  151.0 4.9 %copy-start.12 = (f32[2,15,128,128]{3,2,1,0:T(8,128)S(1)}, f32[2,15,128,128]{3,2,1,0:T(8,128)}, u32[]{:S(2)}) copy-start(f32[2,15,128,128]{3,2,1,0:T(8,128)} %slice.362) | copy-start | bytes 5898244
  151.0 4.9 %copy-start.22 = (f32[2,1,128,128]{3,2,1,0:T(8,128)S(1)}, f32[2,1,128,128]{3,2,1,0:T(8,128)}, u32[]{:S(2)}) copy-start(f32[2,1,128,128]{3,2,1,0:T(8,128)} %copy-done.21) | copy-start | bytes 393220
  154.6 10.9 %collective-permute-start.4 = (f32[2,2,128,128]{3,2,1,0:T(8,128)S(1)}, f32[2,2,128,128]{3,2,1,0:T(8,128)S(1)}, u32[]{:S(2)}, u32[]{:S(2)}) collective-permute-start(f32[2,2,128,128]{3,2,1,0:T(8,128)S(1)} %pad_maximum_fusion.1), channel_id=1, source_target_pairs={{0,208},{16,224},{32,240},{1,209},{17,225},{33,241},{2,210},{18,22... | collective-permute-start | bytes 786440 | tf_op jit(solution)/shard_map/ppermute | solution.py:19
  158.1 15.5 %collective-permute-start.7 = (f32[2,2,128,128]{3,2,1,0:T(8,128)S(1)}, f32[2,2,128,128]{3,2,1,0:T(8,128)S(1)}, u32[]{:S(2)}, u32[]{:S(2)}) collective-permute-start(f32[2,2,128,128]{3,2,1,0:T(8,128)S(1)} %pad_maximum_fusion.1), channel_id=1, source_target_pairs={{0,16},{16,32},{32,48},{48,64},{64,80},{80,96},{96,112},{112,128},... | collective-permute-start | bytes 786440 | tf_op jit(solution)/shard_map/ppermute | solution.py:19
  160.6 12.6 %collective-permute-start.6 = (f32[2,2,128,128]{3,2,1,0:T(8,128)S(1)}, f32[2,2,128,128]{3,2,1,0:T(8,128)S(1)}, u32[]{:S(2)}, u32[]{:S(2)}) collective-permute-start(f32[2,2,128,128]{3,2,1,0:T(8,128)S(1)} %pad_maximum_fusion.1), channel_id=1, source_target_pairs={{0,80},{16,96},{32,112},{48,128},{64,144},{80,160},{96,176},{112,1... | collective-permute-start | bytes 786440 | tf_op jit(solution)/shard_map/ppermute | solution.py:19
  164.2 8.8 %collective-permute-start.5 = (f32[2,2,128,128]{3,2,1,0:T(8,128)S(1)}, f32[2,2,128,128]{3,2,1,0:T(8,128)S(1)}, u32[]{:S(2)}, u32[]{:S(2)}) collective-permute-start(f32[2,2,128,128]{3,2,1,0:T(8,128)S(1)} %pad_maximum_fusion.1), channel_id=1, source_target_pairs={{0,144},{16,160},{32,176},{48,192},{64,208},{80,224},{96,240},{1,1... | collective-permute-start | bytes 786440 | tf_op jit(solution)/shard_map/ppermute | solution.py:19
  177.5 2.3 copy-start.30
  179.8 3.7 %copy-start.24 = (bf16[256,2048]{1,0:T(8,128)(2,1)S(1)}, bf16[256,2048]{1,0:T(8,128)(2,1)}, u32[]{:S(2)}) copy-start(bf16[256,2048]{1,0:T(8,128)(2,1)} %param.31) | copy-start | bytes 3145732
  186.8 64.5 %copy-start.26 = (f32[2048]{0:T(1024)S(1)}, f32[2048]{0:T(1024)}, u32[]{:S(2)}) copy-start(f32[2048]{0:T(1024)} %param.32) | copy-start | bytes 24580
  253.0 36.9 %copy-start.29 = (bf16[1,2048,512]{2,1,0:T(8,128)(2,1)S(1)}, bf16[1,2048,512]{2,1,0:T(8,128)(2,1)}, u32[]{:S(2)}) copy-start(bf16[1,2048,512]{2,1,0:T(8,128)(2,1)} %param.35) | copy-start | bytes 6291460
  295.4 31.0 %copy-start.28 = (f32[64,2]{0,1:T(2,128)S(1)}, f32[64,2]{0,1:T(2,128)}, u32[]{:S(2)}) copy-start(f32[64,2]{0,1:T(2,128)} %param.34) | copy-start | bytes 1540
  295.4 31.4 %copy-start.15 = (bf16[64,2048]{1,0:T(8,128)(2,1)S(1)}, bf16[64,2048]{1,0:T(8,128)(2,1)}, u32[]{:S(2)}) copy-start(bf16[64,2048]{1,0:T(8,128)(2,1)} %reduce-scatter.2.cloned.1.call-done) | copy-start | bytes 786436
  295.4 31.0 %all-to-all-start.1 = ((bf16[1,16,16,2048]{3,2,0,1:T(8,128)(2,1)}), bf16[1,16,16,2048]{3,2,0,1:T(8,128)(2,1)S(1)}, u32[]{:S(2)}, u32[]{:S(2)}) async-start(bf16[1,16,16,2048]{3,2,0,1:T(8,128)(2,1)} %fusion.23), calls=%async_computation.2 | async-start | bytes 2097152 | tf_op jit(solution)/shard_map/all_to_all | solution.py:243
  (12 other events, 16.9 us)
Sparse Core Ops, SparseCore 0:
  9.1 53.4 all-gather.1
  187.0 63.0 reduce-scatter.1

commit v4 on v3

--- a/solution.py
+++ b/solution.py
@@ -80,28 +80,14 @@
 
 def shard_prefix(total_map, total_add):
     place = lax.axis_index("seq")
-    count = lax.axis_size("seq")
-    eye = jnp.broadcast_to(jnp.eye(total_map.shape[-1], dtype=total_map.dtype), total_map.shape)
-
-    def fetch(maps, adds, shift):
-        got = passed_along(jnp.stack([maps, adds]), "seq", shift)
-        valid = place >= shift
-        return jnp.where(valid, got[0], eye), jnp.where(valid, got[1], 0.0)
-
-    maps, adds = total_map, total_add
-    window = 1
-    while window * RADIX < count:
-        parts = [fetch(maps, adds, window * step) for step in range(RADIX - 1, 0, -1)]
-        for prev_map, prev_add in parts[1:] + [(maps, adds)]:
-            parts[0] = compose(parts[0][0], parts[0][1], prev_map, prev_add)
-        maps, adds = parts[0]
-        window *= RADIX
-    shifts = list(range(1, count, window))[::-1]
-    parts = [fetch(maps, adds, shift) for shift in shifts]
-    run_map, run_add = parts[0]
-    for prev_map, prev_add in parts[1:]:
-        run_map, run_add = compose(run_map, run_add, prev_map, prev_add)
-    return run_add
+    gathered = lax.all_gather(jnp.stack([total_map, total_add]), "seq")
+    earlier = (jnp.arange(gathered.shape[0]) < place)[:, None, None, None]
+    eye = jnp.eye(total_map.shape[-1], dtype=total_map.dtype)
+    maps = jnp.where(earlier, gathered[:, 0], eye)
+    adds = jnp.where(earlier, gathered[:, 1], 0.0)
+    while maps.shape[0] > 1:
+        maps, adds = compose(maps[0::2], adds[0::2], maps[1::2], adds[1::2])
+    return adds[0]
 
 
 def per_device(

time: 342 us -> 341 us (level)
  starting transfers between devices: 27.2 us -> 6.78 us
  waiting for transfers between devices: 147 us -> 162 us
  local copies, waits for them, and re-layouts: 26.8 us -> 30.5 us
    all_gather x0 -> x1, waiting for transfers between devices: none -> 24.5 us  [shard_prefix(): gathered = lax.all_gather(jnp.stack([total_map, total_add]), 'seq')]
    ppermute x8 -> x1, starting transfers between devices: 23.5 us -> 2.8 us  [passed_along(): return lax.ppermute(block, axis, route)]
    ppermute x8 -> x1, waiting for transfers between devices: 7.44 us -> 0.01 us  [passed_along(): return lax.ppermute(block, axis, route)]
    unnamed x65 -> x71, local copies, waits for them, and re-layouts: 6.24 us -> 9.95 us
    dot_general x36 -> x34, matrix products: 37.4 us -> 40.4 us  [mix(): return jnp.einsum(form, left_arr, right_arr, precision=HIGH)]
  transfers between devices with their start and end apart: 11 -> 5, of which waited for: 4 -> 4; matrix products, arithmetic and copies ran while one was open for 10% -> 9% of each run, Pallas kernels for 0% -> 0%
where the time goes in v4:
time: 341 us; the launch traced here: 335 us
  waiting for transfers between devices  162 us (48%)
  matrix products  59.6 us (17%)
  blocking collectives  36.3 us (11%)
  local copies, waits for them, and re-layouts  30.5 us (9%)
  other arithmetic  25.3 us (7%)
  between operations  14.5 us (4%)
  starting transfers between devices  6.78 us (2%)
    reduce_scatter x1, waiting for transfers between devices, per_device(): lax.psum_scatter(jnp.dot(gated, w_out, preferred_element_type=jnp.float32...  58.9 us
    all_gather x1, waiting for transfers between devices, per_device(): whole = lax.all_gather(tokens, 'exp', axis=1, tiled=True)  50.6 us
    dot_general x34, matrix products, mix(): return jnp.einsum(form, left_arr, right_arr, precision=HIGH)  40.4 us
    all_to_all x1, blocking collectives, per_device(): lax.all_to_all(outgoing, 'exp', split_axis=0, concat_axis=1, tiled=True)  36.3 us
    all_to_all x1, waiting for transfers between devices, per_device(): lax.all_to_all(processed, 'exp', split_axis=1, concat_axis=0, tiled=True)  27.1 us
    all_gather x1, waiting for transfers between devices, shard_prefix(): gathered = lax.all_gather(jnp.stack([total_map, total_add]), 'seq')  24.5 us
    unnamed x71, local copies, waits for them, and re-layouts  9.95 us
    dot_general x7, matrix products, project(): jnp.dot(rows, weight, preferred_element_type=jnp.float32)  9.49 us
  transfers between devices with their start and end apart: 5, of which 4 were waited for; matrix products, arithmetic and copies ran while one was open for 9% of the time, Pallas kernels for 0%

profile of v4, /device:TPU:1, one launch (start us, length us, event | category | flops | bytes accessed | tf_op | source)
XLA Modules:
  0.0 334.8 jit_solution(9424674949487077946)
XLA Ops:
  12.0 50.6 %all-gather.4.cloned.1.call-done = bf16[1024,2048]{1,0:T(8,128)(2,1)} async-done(((bf16[1024,128]{1,0:T(8,128)(2,1)}), bf16[1024,2048]{1,0:T(8,128)(2,1)}) %all-gather.4.cloned.1.call-update) | async-done | bytes 4194320 | tf_op jit(solution)/shard_map/all_gather | solution.py:114
  62.6 3.2 fusion
  69.6 2.2 convolution_convert_fusion.4
  71.9 2.8 collective-permute-start
  76.5 1.6 maximum_convert_fusion
  78.1 2.7 divide_multiply_fusion
  93.4 1.6 fusion.267
  94.9 3.0 reshape.226
  97.9 3.3 copy.78
  101.3 1.7 bitcast_multiply_fusion.1
  104.3 2.1 fusion.63
  106.6 2.4 multiply_subtract_fusion
  115.9 2.3 fusion.9
  120.4 2.3 fusion.7
  123.3 2.2 fusion.5
  127.4 2.2 fusion.3
  129.7 1.7 slice.364
  135.3 1.7 convolution_subtract_fusion
  137.0 3.6 %fusion.44 = f32[2,16,64,128]{3,2,1,0:T(8,128)} fusion(f32[2,16,64,128]{3,2,1,0:T(8,128)S(1)} %convolution_subtract_fusion, f32[2,15,128,128]{3,2,1,0:T(8,128)S(1)} %copy-done.16, f32[2,1,128,128]{3,2,1,0:T(8,128)S(1)} %broadcast_in_dim.134), kind=kOutput, calls=%fused_computation.64 | convolution fusion | flops 201850880 | bytes 4194304 | tf_op jit(solution)/shard_map/hnik,hnlk->hnil/dot_general | solution.py:27
  140.6 1.7 fusion.115
  143.7 24.5 %all-gather.6.cloned.1.call-done = f32[32,2,128,128]{3,2,1,0:T(8,128)} async-done(((f32[2,2,128,128]{3,2,1,0:T(8,128)}), f32[32,2,128,128]{3,2,1,0:T(8,128)}) %all-gather.6.cloned.1.call-update) | async-done | bytes 4194320 | tf_op jit(solution)/shard_map/all_gather | solution.py:83
  168.2 2.7 fusion.25
  175.5 3.0 multiply_reduce_fusion
  178.7 2.1 copy.82
  182.3 3.7 %fusion.88 = bf16[1024,256]{1,0:T(8,128)(2,1)S(1)} fusion(bf16[1024,2048]{1,0:T(8,128)(2,1)} %copy-done.1, bf16[2048,256]{1,0:T(8,128)(2,1)S(1)} %copy-done.32, f32[128,8,2,128]{3,2,1,0:T(2,128)S(1)} %bitcast.160, f32[128,8,2,128]{3,2,1,0:T(2,128)S(1)} %bitcast.161, f32[256]{0:T(256)S(1)} %broadcast_bitcast_fusion), kind=kOutput, calls=%fused_computation.116 | convolution fusion | flops 1076363264 | bytes 7865344 | tf_op jit(solution)/shard_map/dot_general | solution.py:119
  186.0 3.3 convolution_convert_fusion
  190.6 58.9 %reduce-scatter.2.cloned.1.call-done = bf16[64,2048]{1,0:T(8,128)(2,1)} async-done(((bf16[1024,2048]{1,0:T(8,128)(2,1)}), bf16[64,2048]{1,0:T(8,128)(2,1)}) %reduce-scatter.2.cloned.1.call-update) | async-done | bytes 262160 | tf_op jit(solution)/shard_map/reduce_scatter | solution.py:197
  253.1 36.3 %all_to_all.8 = bf16[16,1,16,2048]{3,2,1,0:T(8,128)(2,1)S(1)} all-to-all(bf16[16,1,16,2048]{3,2,1,0:T(8,128)(2,1)S(1)} %bitcast.158), channel_id=1, replica_groups=mesh['seq'=16,'exp'=16] {'exp'}, dimensions={0} | all-to-all | bytes 2097152 | tf_op jit(solution)/shard_map/all_to_all | solution.py:222
  290.9 4.0 %fusion.23 = bf16[1,16,16,2048]{3,2,0,1:T(8,128)(2,1)} fusion(bf16[1,512,2048]{2,1,0:T(8,128)(2,1)S(1)} %copy-done, bf16[1,2048,512]{2,1,0:T(8,128)(2,1)} %param.36, bf16[16,1,16,2048]{3,2,1,0:T(8,128)(2,1)S(1)} %all_to_all.8, f32[16,16,512]{2,1,0:T(8,128)} %fusion.59), kind=kOutput, calls=%fused_computation.33 | convolution fusion | flops 1075052544 | bytes 6815744 | tf_op jit(solution)/shard_map/esnf,efd->esnd/dot_general | solution.py:226
  294.9 3.7 %all-to-all-start.1 = ((bf16[1,16,16,2048]{3,2,0,1:T(8,128)(2,1)}), bf16[1,16,16,2048]{3,2,0,1:T(8,128)(2,1)S(1)}, u32[]{:S(2)}, u32[]{:S(2)}) async-start(bf16[1,16,16,2048]{3,2,0,1:T(8,128)(2,1)} %fusion.23), calls=%async_computation.2 | async-start | bytes 2097152 | tf_op jit(solution)/shard_map/all_to_all | solution.py:229
  298.8 27.1 %all-to-all-done.1 = bf16[1,16,16,2048]{3,2,0,1:T(8,128)(2,1)S(1)} async-done(((bf16[1,16,16,2048]{3,2,0,1:T(8,128)(2,1)}), bf16[1,16,16,2048]{3,2,0,1:T(8,128)(2,1)S(1)}, u32[]{:S(2)}, u32[]{:S(2)}) %all-to-all-start.1) | async-done | bytes 1048608 | tf_op jit(solution)/shard_map/all_to_all | solution.py:229
  326.3 1.7 add_convert_fusion
  (207 shorter events, 54.3 us)
Async XLA Ops:
  6.5 284.3 %copy-start = (bf16[1,512,2048]{2,1,0:T(8,128)(2,1)S(1)}, bf16[1,512,2048]{2,1,0:T(8,128)(2,1)}, u32[]{:S(2)}) copy-start(bf16[1,512,2048]{2,1,0:T(8,128)(2,1)} %param.37) | copy-start | bytes 6291460
  6.5 56.1 %all-gather.4.cloned.1.call-start = ((), (), s32[]{:S(2)}) async-start(), calls=%async_computation.3 | async-start | bytes 4456448 | tf_op jit(solution)/shard_map/all_gather | solution.py:114
  7.3 161.0 %all-gather.6.cloned.1.call-start = ((), (), s32[]{:S(2)}) async-start(), calls=%async_computation.5 | async-start | bytes 4456448 | tf_op jit(solution)/shard_map/all_gather | solution.py:83
  12.0 53.8 %copy-start.27 = (f32[2048]{0:T(1024)S(1)}, f32[2048]{0:T(1024)}, u32[]{:S(2)}) copy-start(f32[2048]{0:T(1024)} %param.20) | copy-start | bytes 24580
  62.6 3.4 %copy-start.6 = (bf16[1024,2048]{1,0:T(8,128)(2,1)S(1)}, bf16[1024,2048]{1,0:T(8,128)(2,1)}, u32[]{:S(2)}) copy-start(bf16[1024,2048]{1,0:T(8,128)(2,1)} %all-gather.4.cloned.1.call-done) | copy-start | bytes 12582916
  67.1 7.6 %copy-start.1 = (bf16[1024,2048]{1,0:T(8,128)(2,1)}, bf16[1024,2048]{1,0:T(8,128)(2,1)S(1)}, u32[]{:S(2)}) copy-start(bf16[1024,2048]{1,0:T(8,128)(2,1)S(1)} %fusion.2) | copy-start | bytes 12582916
  67.3 2.0 copy-start.25
  69.6 2.2 copy-start.24
  71.9 4.4 %collective-permute-start = (bf16[3,512]{1,0:T(4,128)(2,1)S(1)}, bf16[3,512]{1,0:T(4,128)(2,1)S(1)}, u32[]{:S(2)}, u32[]{:S(2)}) collective-permute-start(bf16[3,512]{1,0:T(4,128)(2,1)S(1)} %pad_maximum_fusion.1), channel_id=1, source_target_pairs={{0,16},{16,32},{32,48},{48,64},{64,80},{80,96},{96,112},{112,128},... | collective-permute-start | bytes 9224 | tf_op jit(solution)/shard_map/ppermute | solution.py:19
  83.1 2.4 copy-start.10
  101.3 1.7 copy-start.19
  101.3 1.9 copy-start.21
  104.3 2.3 copy-start.7
  106.5 3.7 %copy-start.2 = (f32[2,16,128,128]{3,2,1,0:T(8,128)}, f32[2,16,128,128]{3,2,1,0:T(8,128)S(1)}, u32[]{:S(2)}) copy-start(f32[2,16,128,128]{3,2,1,0:T(8,128)S(1)} %fusion.63) | copy-start | bytes 6291460
  111.3 1.8 copy-start.33
  112.8 136.7 %reduce-scatter.2.cloned.1.call-start = ((), (), s32[]{:S(2)}) async-start(), calls=%async_computation.4 | async-start | bytes 4456448 | tf_op jit(solution)/shard_map/reduce_scatter | solution.py:197
  113.2 2.2 slice-start
  113.2 2.8 slice-start.1
  129.6 2.6 copy-start.9
  131.3 2.1 copy-start.12
  133.5 1.8 copy-start.8
  134.5 2.5 copy-start.16
  137.0 5.2 %copy-start.14 = (f32[2,16,128,128]{3,2,1,0:T(8,128)S(1)}, f32[2,16,128,128]{3,2,1,0:T(8,128)}, u32[]{:S(2)}) copy-start(f32[2,16,128,128]{3,2,1,0:T(8,128)} %copy-done.13) | copy-start | bytes 6291460
  140.6 1.7 slice-start.2
  173.6 1.9 copy-start.18
  178.7 3.6 %copy-start.32 = (bf16[2048,256]{1,0:T(8,128)(2,1)S(1)}, bf16[2048,256]{1,0:T(8,128)(2,1)}, u32[]{:S(2)}) copy-start(bf16[2048,256]{1,0:T(8,128)(2,1)} %param.24) | copy-start | bytes 3145732
  182.3 3.7 %copy-start.26 = (bf16[256,2048]{1,0:T(8,128)(2,1)S(1)}, bf16[256,2048]{1,0:T(8,128)(2,1)}, u32[]{:S(2)}) copy-start(bf16[256,2048]{1,0:T(8,128)(2,1)} %param.31) | copy-start | bytes 3145732
  189.3 61.5 %copy-start.28 = (f32[2048]{0:T(1024)S(1)}, f32[2048]{0:T(1024)}, u32[]{:S(2)}) copy-start(f32[2048]{0:T(1024)} %param.32) | copy-start | bytes 24580
  252.5 36.9 %copy-start.31 = (bf16[1,2048,512]{2,1,0:T(8,128)(2,1)S(1)}, bf16[1,2048,512]{2,1,0:T(8,128)(2,1)}, u32[]{:S(2)}) copy-start(bf16[1,2048,512]{2,1,0:T(8,128)(2,1)} %param.35) | copy-start | bytes 6291460
  294.9 31.1 %copy-start.30 = (f32[64,2]{0,1:T(2,128)S(1)}, f32[64,2]{0,1:T(2,128)}, u32[]{:S(2)}) copy-start(f32[64,2]{0,1:T(2,128)} %param.34) | copy-start | bytes 1540
  294.9 31.4 %copy-start.22 = (bf16[64,2048]{1,0:T(8,128)(2,1)S(1)}, bf16[64,2048]{1,0:T(8,128)(2,1)}, u32[]{:S(2)}) copy-start(bf16[64,2048]{1,0:T(8,128)(2,1)} %reduce-scatter.2.cloned.1.call-done) | copy-start | bytes 786436
  294.9 31.0 %all-to-all-start.1 = ((bf16[1,16,16,2048]{3,2,0,1:T(8,128)(2,1)}), bf16[1,16,16,2048]{3,2,0,1:T(8,128)(2,1)S(1)}, u32[]{:S(2)}, u32[]{:S(2)}) async-start(bf16[1,16,16,2048]{3,2,0,1:T(8,128)(2,1)} %fusion.23), calls=%async_computation.2 | async-start | bytes 2097152 | tf_op jit(solution)/shard_map/all_to_all | solution.py:229
  (10 other events, 12.6 us)
Sparse Core Ops, SparseCore 0:
  9.1 53.4 all-gather.3
  113.0 55.2 all-gather.5
  189.4 60.1 reduce-scatter.1

commit v5 on v4

--- a/solution.py
+++ b/solution.py
@@ -118,27 +118,47 @@
     def project(rows, weight):
         return jnp.dot(rows, weight, preferred_element_type=jnp.float32).astype(jnp.bfloat16)
 
-    conv_all = jnp.concatenate([conv_query, conv_key, conv_value], 1)
+    value_heads = w_value.shape[1] // DV
+
+    def project_heads(rows, weight):
+        split = weight.reshape(weight.shape[0], value_heads, -1)
+        return jnp.einsum(
+            "td,dhe->hte", rows, split, preferred_element_type=jnp.float32
+        ).astype(jnp.bfloat16)
+
+    conv_all = jnp.concatenate([conv_query, conv_key], 1)
     taps = conv_all.shape[0]
     length = normed.shape[0]
     last_rows = normed[length - (taps - 1) :]
-    tail = jnp.concatenate([project(last_rows, w) for w in (w_query, w_key, w_value)], 1)
+    tail_v = project_heads(last_rows, w_value)
+    tail = jnp.concatenate(
+        [project(last_rows, w) for w in (w_query, w_key)]
+        + [tail_v.transpose(1, 0, 2).reshape(taps - 1, -1)],
+        1,
+    )
     before = passed_along(tail, "seq", 1)
-    projected = jnp.concatenate([project(normed, w) for w in (w_query, w_key, w_value)], 1)
-    z_gate = project(normed, w_zgate)
-    extended = jnp.concatenate([before, projected], 0).astype(jnp.float32)
+    projected = jnp.concatenate([project(normed, w) for w in (w_query, w_key)], 1)
+    v_raw = project_heads(normed, w_value)
+    z_heads = project_heads(normed, w_zgate)
+    width_q = w_query.shape[1]
+    width_k = w_key.shape[1]
+    split_at = width_q + width_k
+    extended = jnp.concatenate([before[:, :split_at], projected], 0).astype(jnp.float32)
     conv_out = conv_all[0] * extended[0:length]
     for index in range(1, taps):
         conv_out = conv_out + conv_all[index] * extended[index : index + length]
     conv_out = jax.nn.silu(conv_out)
-    width_q = w_query.shape[1]
-    width_k = w_key.shape[1]
+    before_v = before[:, split_at:].reshape(taps - 1, value_heads, DV).transpose(1, 0, 2)
+    extended_v = jnp.concatenate([before_v, v_raw], 1).astype(jnp.float32)
+    taps_v = conv_value.reshape(taps, value_heads, 1, DV)
+    conv_v = taps_v[0] * extended_v[:, 0:length]
+    for index in range(1, taps):
+        conv_v = conv_v + taps_v[index] * extended_v[:, index : index + length]
+    conv_v = jax.nn.silu(conv_v)
     key_heads = width_q // DK
-    value_heads = w_value.shape[1] // DV
     group = value_heads // key_heads
     query = unit_heads(conv_out[:, :width_q], key_heads) * DK ** (-0.5)
     keyvec = unit_heads(conv_out[:, width_q : width_q + width_k], key_heads)
-    values = conv_out[:, width_q + width_k :].reshape(length, value_heads, DV)
     query = jnp.repeat(query, group, axis=1)
     keyvec = jnp.repeat(keyvec, group, axis=1)
     blocks = length // STRETCH
@@ -148,7 +168,7 @@
 
     q_blk = by_block(query)
     k_blk = by_block(keyvec)
-    v_blk = by_block(values)
+    v_blk = conv_v.reshape(value_heads, blocks, STRETCH, DV)
     g_blk = log_decay.reshape(blocks, STRETCH, value_heads).transpose(2, 0, 1)
     b_blk = write_rate.reshape(blocks, STRETCH, value_heads).transpose(2, 0, 1)
     cumul = jnp.cumsum(g_blk, -1)
@@ -184,18 +204,19 @@
     carried = mix("hnik,hnlk->hnil", reach, map_prefix)
     local = mix("hnik,hnvk->hniv", reach, add_prefix) + mix("hnij,hnjv->hniv", scores, u_mat)
     out_blk = mix("hnil,hvl->hniv", carried, incoming) + local
-    delta_out = out_blk.transpose(1, 2, 0, 3).reshape(length, value_heads, DV)
-    gate_z = z_gate.astype(jnp.float32).reshape(length, value_heads, DV)
-    gated = (
-        (rms_scale(delta_out, norm_gain) * jax.nn.silu(gate_z))
-        .astype(jnp.bfloat16)
-        .reshape(length, value_heads * DV)
-    )
+    delta_out = out_blk.reshape(value_heads, length, DV)
+    gate_z = z_heads.astype(jnp.float32)
+    gated = (rms_scale(delta_out, norm_gain) * jax.nn.silu(gate_z)).astype(jnp.bfloat16)
     n_exp = lax.axis_size("exp")
     row_share = length // n_exp
     gated = lax.optimization_barrier(gated)
     attn_rows = lax.psum_scatter(
-        jnp.dot(gated, w_out, preferred_element_type=jnp.float32).astype(jnp.bfloat16),
+        jnp.einsum(
+            "htv,hvd->td",
+            gated,
+            w_out.reshape(value_heads, DV, -1),
+            preferred_element_type=jnp.float32,
+        ).astype(jnp.bfloat16),
         "exp",
         scatter_dimension=0,
         tiled=True,

time: 341 us -> 327 us (0.959)
  local copies, waits for them, and re-layouts: 30.5 us -> 21.4 us
  waiting for transfers between devices: 162 us -> 158 us
    dot_general x1 -> x4, matrix products: 3.29 us -> 9.84 us  [the longest x3 6.56 us: project_heads(): jnp.einsum('td,dhe->hte', rows, split, preferred_element_type=jnp.float32)]
    another operation x2 -> x0, local copies, waits for them, and re-layouts: 6.36 us -> none  [by_block(): return array.reshape(blocks, STRETCH, value_heads, -1).transpose(2, 0, 1, 3)]
    dot_general x7 -> x4, matrix products: 9.49 us -> 5.58 us  [project(): jnp.dot(rows, weight, preferred_element_type=jnp.float32)]
    unnamed x71 -> x84, local copies, waits for them, and re-layouts: 9.95 us -> 9.42 us
  transfers between devices with their start and end apart: 5 -> 5, of which waited for: 4 -> 4; matrix products, arithmetic and copies ran while one was open for 9% -> 11% of each run, Pallas kernels for 0% -> 0%
where the time goes in v5:
time: 327 us; the launch traced here: 322 us
  waiting for transfers between devices  158 us (48%)
  matrix products  61.4 us (19%)
  blocking collectives  36.1 us (11%)
  other arithmetic  22.9 us (7%)
  local copies, waits for them, and re-layouts  21.4 us (7%)
  between operations  14.8 us (5%)
  starting transfers between devices  7.25 us (2%)
    reduce_scatter x1, waiting for transfers between devices, per_device(): lax.psum_scatter(jnp.einsum('htv,hvd->td', gated, w_out.reshape(value_hea...  59.1 us
    all_gather x1, waiting for transfers between devices, per_device(): whole = lax.all_gather(tokens, 'exp', axis=1, tiled=True)  47.6 us
    dot_general x34, matrix products, mix(): return jnp.einsum(form, left_arr, right_arr, precision=HIGH)  39.5 us
    all_to_all x1, blocking collectives, per_device(): lax.all_to_all(outgoing, 'exp', split_axis=0, concat_axis=1, tiled=True)  36.1 us
    all_to_all x1, waiting for transfers between devices, per_device(): lax.all_to_all(processed, 'exp', split_axis=1, concat_axis=0, tiled=True)  27.1 us
    all_gather x1, waiting for transfers between devices, shard_prefix(): gathered = lax.all_gather(jnp.stack([total_map, total_add]), 'seq')  23.7 us
    unnamed x84, local copies, waits for them, and re-layouts  9.42 us
    dot_general x3, matrix products, project_heads(): jnp.einsum('td,dhe->hte', rows, split, preferred_element_type=jnp.float32)  6.56 us
  transfers between devices with their start and end apart: 5, of which 4 were waited for; matrix products, arithmetic and copies ran while one was open for 11% of the time, Pallas kernels for 0%

profile of v5, /device:TPU:1, one launch (start us, length us, event | category | flops | bytes accessed | tf_op | source)
XLA Modules:
  0.0 322.2 jit_solution(12523206552679091834)
XLA Ops:
  12.7 1.4 fusion.292
  15.0 47.6 %all-gather.4.cloned.1.call-done = bf16[1024,2048]{1,0:T(8,128)(2,1)} async-done(((bf16[1024,128]{1,0:T(8,128)(2,1)}), bf16[1024,2048]{1,0:T(8,128)(2,1)}) %all-gather.4.cloned.1.call-update) | async-done | bytes 4194320 | tf_op jit(solution)/shard_map/all_gather | solution.py:114
  62.6 3.2 fusion
  67.3 1.5 convolution_convert_fusion.2
  69.6 2.1 fusion.91
  72.0 3.3 %collective-permute-start = (bf16[3,512]{0,1:T(8,128)(2,1)S(1)}, bf16[3,512]{0,1:T(8,128)(2,1)S(1)}, u32[]{:S(2)}, u32[]{:S(2)}) collective-permute-start(bf16[3,512]{0,1:T(8,128)(2,1)S(1)} %copy.82), channel_id=1, source_target_pairs={{0,16},{16,32},{32,48},{48,64},{64,80},{80,96},{96,112},{112,128},... | collective-permute-start | bytes 9224 | tf_op jit(solution)/shard_map/ppermute | solution.py:19
  75.3 3.7 %convolution_convert_fusion.3 = bf16[1024,128]{0,1:T(8,128)(2,1)S(1)} fusion(bf16[1024,2048]{1,0:T(8,128)(2,1)} %copy-done.1, bf16[2048,128]{1,0:T(8,128)(2,1)S(1)} %copy-done.19), kind=kOutput, calls=%fused_computation.101 | convolution fusion | flops 537001984 | bytes 4980736 | tf_op jit(solution)/shard_map/dot_general | solution.py:119
  95.5 2.2 fusion.64
  97.8 2.4 multiply_subtract_fusion
  104.4 1.5 copy-done.5
  107.1 2.3 fusion.9
  109.6 1.4 copy-done.3
  111.6 2.3 fusion.7
  114.6 2.3 fusion.5
  118.7 2.2 fusion.3
  120.9 1.7 slice.409
  126.5 1.7 convolution_subtract_fusion
  128.3 3.4 %fusion.45 = f32[2,16,64,128]{3,2,1,0:T(8,128)} fusion(f32[2,16,64,128]{3,2,1,0:T(8,128)S(1)} %convolution_subtract_fusion, f32[2,15,128,128]{3,2,1,0:T(8,128)S(1)} %copy-done.13, f32[2,1,128,128]{3,2,1,0:T(8,128)S(1)} %broadcast_in_dim.134), kind=kOutput, calls=%fused_computation.61 | convolution fusion | flops 201850880 | bytes 4194304 | tf_op jit(solution)/shard_map/hnik,hnlk->hnil/dot_general | solution.py:27
  131.7 1.7 fusion.136
  133.4 1.5 slice_add_fusion.3
  134.9 23.7 %all-gather.6.cloned.1.call-done = f32[32,2,128,128]{3,2,1,0:T(8,128)} async-done(((f32[2,2,128,128]{3,2,1,0:T(8,128)}), f32[32,2,128,128]{3,2,1,0:T(8,128)}) %all-gather.6.cloned.1.call-update) | async-done | bytes 4194320 | tf_op jit(solution)/shard_map/all_gather | solution.py:83
  158.6 2.7 fusion.29
  165.9 3.0 multiply_reduce_fusion
  168.9 4.2 %fusion.120 = bf16[2,1024,128]{2,1,0:T(8,128)(2,1)S(1)} fusion(f32[2,16,64,128]{3,2,1,0:T(8,128)} %get-tuple-element.41, bf16[1024,2048]{1,0:T(8,128)(2,1)} %copy-done.1, f32[128]{0:T(128)S(1)} %copy-done.40, f32[2,1024]{1,0:T(2,128)S(1)} %rsqrt.47, bf16[2048,256]{1,0:T(8,128)(2,1)} %param.24), kind=kOutput, calls=%fused_computation.141 | convolution fusion | flops 1076363264 | bytes 6824448 | tf_op jit(solution)/shard_map/td,dhe->hte/dot_general | solution.py:125
  173.2 3.3 %bitcast_convert_fusion = bf16[1024,2048]{1,0:T(8,128)(2,1)} fusion(bf16[2,1024,128]{2,1,0:T(8,128)(2,1)S(1)} %fusion.120, bf16[2,128,2048]{2,1,0:T(8,128)(2,1)S(1)} %bitcast.202), kind=kOutput, calls=%fused_computation.5 | convolution fusion | flops 1075838976 | bytes 5767168 | tf_op jit(solution)/shard_map/htv,hvd->td/dot_general | solution.py:214
  177.8 59.1 %reduce-scatter.2.cloned.1.call-done = bf16[64,2048]{1,0:T(8,128)(2,1)} async-done(((bf16[1024,2048]{1,0:T(8,128)(2,1)}), bf16[64,2048]{1,0:T(8,128)(2,1)}) %reduce-scatter.2.cloned.1.call-update) | async-done | bytes 262160 | tf_op jit(solution)/shard_map/reduce_scatter | solution.py:213
  240.4 36.1 %all_to_all.8 = bf16[16,1,16,2048]{3,2,1,0:T(8,128)(2,1)S(1)} all-to-all(bf16[16,1,16,2048]{3,2,1,0:T(8,128)(2,1)S(1)} %bitcast.200), channel_id=1, replica_groups=mesh['seq'=16,'exp'=16] {'exp'}, dimensions={0} | all-to-all | bytes 2097152 | tf_op jit(solution)/shard_map/all_to_all | solution.py:243
  276.6 1.5 fusion.60
  278.1 4.0 %fusion.27 = bf16[1,16,16,2048]{3,2,0,1:T(8,128)(2,1)} fusion(bf16[1,512,2048]{2,1,0:T(8,128)(2,1)S(1)} %copy-done, bf16[1,2048,512]{2,1,0:T(8,128)(2,1)} %param.36, bf16[16,1,16,2048]{3,2,1,0:T(8,128)(2,1)S(1)} %all_to_all.8, f32[16,16,512]{2,1,0:T(8,128)} %fusion.60), kind=kOutput, calls=%fused_computation.37 | convolution fusion | flops 1075052544 | bytes 6815744 | tf_op jit(solution)/shard_map/esnf,efd->esnd/dot_general | solution.py:247
  282.1 3.7 %all-to-all-start.1 = ((bf16[1,16,16,2048]{3,2,0,1:T(8,128)(2,1)}), bf16[1,16,16,2048]{3,2,0,1:T(8,128)(2,1)S(1)}, u32[]{:S(2)}, u32[]{:S(2)}) async-start(bf16[1,16,16,2048]{3,2,0,1:T(8,128)(2,1)} %fusion.27), calls=%async_computation.2 | async-start | bytes 2097152 | tf_op jit(solution)/shard_map/all_to_all | solution.py:250
  286.0 27.1 %all-to-all-done.1 = bf16[1,16,16,2048]{3,2,0,1:T(8,128)(2,1)S(1)} async-done(((bf16[1,16,16,2048]{3,2,0,1:T(8,128)(2,1)}), bf16[1,16,16,2048]{3,2,0,1:T(8,128)(2,1)S(1)}, u32[]{:S(2)}, u32[]{:S(2)}) %all-to-all-start.1) | async-done | bytes 1048608 | tf_op jit(solution)/shard_map/all_to_all | solution.py:250
  313.5 1.7 add_convert_fusion
  (219 shorter events, 47.8 us)
Async XLA Ops:
  6.5 271.6 %copy-start = (bf16[1,512,2048]{2,1,0:T(8,128)(2,1)S(1)}, bf16[1,512,2048]{2,1,0:T(8,128)(2,1)}, u32[]{:S(2)}) copy-start(bf16[1,512,2048]{2,1,0:T(8,128)(2,1)} %param.37) | copy-start | bytes 6291460
  6.5 56.1 %all-gather.4.cloned.1.call-start = ((), (), s32[]{:S(2)}) async-start(), calls=%async_computation.3 | async-start | bytes 4456448 | tf_op jit(solution)/shard_map/all_gather | solution.py:114
  7.3 151.4 %all-gather.6.cloned.1.call-start = ((), (), s32[]{:S(2)}) async-start(), calls=%async_computation.5 | async-start | bytes 4456448 | tf_op jit(solution)/shard_map/all_gather | solution.py:83
  15.0 50.8 %copy-start.24 = (f32[2048]{0:T(1024)S(1)}, f32[2048]{0:T(1024)}, u32[]{:S(2)}) copy-start(f32[2048]{0:T(1024)} %param.20) | copy-start | bytes 24580
  62.6 3.4 %copy-start.6 = (bf16[1024,2048]{1,0:T(8,128)(2,1)S(1)}, bf16[1024,2048]{1,0:T(8,128)(2,1)}, u32[]{:S(2)}) copy-start(bf16[1024,2048]{1,0:T(8,128)(2,1)} %all-gather.4.cloned.1.call-done) | copy-start | bytes 12582916
  67.1 4.6 %copy-start.1 = (bf16[1024,2048]{1,0:T(8,128)(2,1)}, bf16[1024,2048]{1,0:T(8,128)(2,1)S(1)}, u32[]{:S(2)}) copy-start(bf16[1024,2048]{1,0:T(8,128)(2,1)S(1)} %fusion.2) | copy-start | bytes 12582916
  67.3 2.0 copy-start.39
  69.6 2.1 copy-start.19
  72.0 7.0 %collective-permute-start = (bf16[3,512]{0,1:T(8,128)(2,1)S(1)}, bf16[3,512]{0,1:T(8,128)(2,1)S(1)}, u32[]{:S(2)}, u32[]{:S(2)}) collective-permute-start(bf16[3,512]{0,1:T(8,128)(2,1)S(1)} %copy.82), channel_id=1, source_target_pairs={{0,16},{16,32},{32,48},{48,64},{64,80},{80,96},{96,112},{112,128},... | collective-permute-start | bytes 9224 | tf_op jit(solution)/shard_map/ppermute | solution.py:19
  80.9 2.3 copy-start.27
  80.9 2.3 copy-start.28
  80.9 2.3 copy-start.29
  80.9 2.3 copy-start.30
  95.5 2.3 copy-start.7
  95.5 2.3 copy-start.36
  97.7 3.7 %copy-start.2 = (f32[2,16,128,128]{3,2,1,0:T(8,128)}, f32[2,16,128,128]{3,2,1,0:T(8,128)S(1)}, u32[]{:S(2)}) copy-start(f32[2,16,128,128]{3,2,1,0:T(8,128)S(1)} %fusion.64) | copy-start | bytes 6291460
  104.1 132.9 %reduce-scatter.2.cloned.1.call-start = ((), (), s32[]{:S(2)}) async-start(), calls=%async_computation.4 | async-start | bytes 4456448 | tf_op jit(solution)/shard_map/reduce_scatter | solution.py:213
  104.4 2.2 slice-start
  104.4 2.8 slice-start.1
  120.9 2.6 copy-start.9
  124.7 1.8 copy-start.8
  125.7 2.5 copy-start.13
  128.3 5.1 %copy-start.11 = (f32[2,16,128,128]{3,2,1,0:T(8,128)S(1)}, f32[2,16,128,128]{3,2,1,0:T(8,128)}, u32[]{:S(2)}) copy-start(f32[2,16,128,128]{3,2,1,0:T(8,128)} %copy-done.10) | copy-start | bytes 6291460
  131.7 1.7 slice-start.2
  164.0 1.9 copy-start.15
  165.8 3.1 copy-start.40
  168.9 4.3 %copy-start.20 = (bf16[256,2048]{1,0:T(8,128)(2,1)S(1)}, bf16[256,2048]{1,0:T(8,128)(2,1)}, u32[]{:S(2)}) copy-start(bf16[256,2048]{1,0:T(8,128)(2,1)} %param.31) | copy-start | bytes 3145732
  176.5 61.7 %copy-start.25 = (f32[2048]{0:T(1024)S(1)}, f32[2048]{0:T(1024)}, u32[]{:S(2)}) copy-start(f32[2048]{0:T(1024)} %param.32) | copy-start | bytes 24580
  239.9 36.7 %copy-start.38 = (bf16[1,2048,512]{2,1,0:T(8,128)(2,1)S(1)}, bf16[1,2048,512]{2,1,0:T(8,128)(2,1)}, u32[]{:S(2)}) copy-start(bf16[1,2048,512]{2,1,0:T(8,128)(2,1)} %param.35) | copy-start | bytes 6291460
  282.1 31.0 %copy-start.37 = (f32[64,2]{0,1:T(2,128)S(1)}, f32[64,2]{0,1:T(2,128)}, u32[]{:S(2)}) copy-start(f32[64,2]{0,1:T(2,128)} %param.34) | copy-start | bytes 1540
  282.1 31.4 %copy-start.17 = (bf16[64,2048]{1,0:T(8,128)(2,1)S(1)}, bf16[64,2048]{1,0:T(8,128)(2,1)}, u32[]{:S(2)}) copy-start(bf16[64,2048]{1,0:T(8,128)(2,1)} %reduce-scatter.2.cloned.1.call-done) | copy-start | bytes 786436
  282.1 31.0 %all-to-all-start.1 = ((bf16[1,16,16,2048]{3,2,0,1:T(8,128)(2,1)}), bf16[1,16,16,2048]{3,2,0,1:T(8,128)(2,1)S(1)}, u32[]{:S(2)}, u32[]{:S(2)}) async-start(bf16[1,16,16,2048]{3,2,0,1:T(8,128)(2,1)} %fusion.27), calls=%async_computation.2 | async-start | bytes 2097152 | tf_op jit(solution)/shard_map/all_to_all | solution.py:250
  (17 other events, 18.0 us)
Sparse Core Ops, SparseCore 0:
  9.1 53.4 all-gather.3
  104.2 54.4 all-gather.5
  176.6 60.2 reduce-scatter.1

commit v6 on v5

--- a/solution.py
+++ b/solution.py
@@ -80,7 +80,8 @@
 
 def shard_prefix(total_map, total_add):
     place = lax.axis_index("seq")
-    gathered = lax.all_gather(jnp.stack([total_map, total_add]), "seq")
+    packed = jnp.stack([total_map, total_add]).astype(jnp.bfloat16)
+    gathered = lax.all_gather(packed, "seq").astype(total_map.dtype)
     earlier = (jnp.arange(gathered.shape[0]) < place)[:, None, None, None]
     eye = jnp.eye(total_map.shape[-1], dtype=total_map.dtype)
     maps = jnp.where(earlier, gathered[:, 0], eye)

time: 327 us -> 323 us (0.988)
  waiting for transfers between devices: 158 us -> 151 us
    all_gather x1, waiting for transfers between devices: 23.7 us -> 15.9 us  [shard_prefix(): gathered = lax.all_gather(packed, 'seq').astype(total_map.dtype)]
  transfers between devices with their start and end apart: 5 -> 5, of which waited for: 4 -> 4; matrix products, arithmetic and copies ran while one was open for 11% -> 12% of each run, Pallas kernels for 0% -> 0%
where the time goes in v6:
time: 323 us; the launch traced here: 318 us
  waiting for transfers between devices  151 us (47%)
  matrix products  64 us (20%)
  blocking collectives  36.1 us (11%)
  other arithmetic  23.5 us (7%)
  local copies, waits for them, and re-layouts  21.5 us (7%)
  between operations  14.8 us (5%)
  starting transfers between devices  7.25 us (2%)
    reduce_scatter x1, waiting for transfers between devices, per_device(): lax.psum_scatter(jnp.einsum('htv,hvd->td', gated, w_out.reshape(value_hea...  60.2 us
    all_gather x1, waiting for transfers between devices, per_device(): whole = lax.all_gather(tokens, 'exp', axis=1, tiled=True)  47 us
    dot_general x34, matrix products, mix(): return jnp.einsum(form, left_arr, right_arr, precision=HIGH)  42.1 us
    all_to_all x1, blocking collectives, per_device(): lax.all_to_all(outgoing, 'exp', split_axis=0, concat_axis=1, tiled=True)  36.1 us
    all_to_all x1, waiting for transfers between devices, per_device(): lax.all_to_all(processed, 'exp', split_axis=1, concat_axis=0, tiled=True)  27.1 us
    all_gather x1, waiting for transfers between devices, shard_prefix(): gathered = lax.all_gather(packed, 'seq').astype(total_map.dtype)  15.9 us
    unnamed x84, local copies, waits for them, and re-layouts  7.96 us
    dot_general x3, matrix products, project_heads(): jnp.einsum('td,dhe->hte', rows, split, preferred_element_type=jnp.float32)  6.57 us
  transfers between devices with their start and end apart: 5, of which 4 were waited for; matrix products, arithmetic and copies ran while one was open for 12% of the time, Pallas kernels for 0%

profile of v6, /device:TPU:1, one launch (start us, length us, event | category | flops | bytes accessed | tf_op | source)
XLA Modules:
  0.0 318.2 jit_solution(10506421174381902094)
XLA Ops:
  13.3 1.4 fusion.294
  15.6 47.0 %all-gather.3.cloned.1.call-done = bf16[1024,2048]{1,0:T(8,128)(2,1)} async-done(((bf16[1024,128]{1,0:T(8,128)(2,1)}), bf16[1024,2048]{1,0:T(8,128)(2,1)}) %all-gather.3.cloned.1.call-update) | async-done | bytes 4194320 | tf_op jit(solution)/shard_map/all_gather | solution.py:115
  62.6 3.2 %fusion = f32[1024]{0:T(1024)S(1)} fusion(bf16[1024,2048]{1,0:T(8,128)(2,1)} %all-gather.3.cloned.1.call-done), kind=kLoop, calls=%fused_computation.2 | loop fusion | flops 6290432 | bytes 4198400 | tf_op jit(solution)/shard_map/reduce_sum | solution.py:23
  67.3 1.5 convolution_convert_fusion.2
  69.6 2.1 fusion.91
  72.1 3.3 %collective-permute-start = (bf16[3,512]{0,1:T(8,128)(2,1)S(1)}, bf16[3,512]{0,1:T(8,128)(2,1)S(1)}, u32[]{:S(2)}, u32[]{:S(2)}) collective-permute-start(bf16[3,512]{0,1:T(8,128)(2,1)S(1)} %copy.65), channel_id=1, source_target_pairs={{0,16},{16,32},{32,48},{48,64},{64,80},{80,96},{96,112},{112,128},... | collective-permute-start | bytes 9224 | tf_op jit(solution)/shard_map/ppermute | solution.py:19
  75.3 3.7 %convolution_convert_fusion.3 = bf16[1024,128]{0,1:T(8,128)(2,1)S(1)} fusion(bf16[1024,2048]{1,0:T(8,128)(2,1)} %copy-done.1, bf16[2048,128]{1,0:T(8,128)(2,1)S(1)} %copy-done.18), kind=kOutput, calls=%fused_computation.102 | convolution fusion | flops 537001984 | bytes 4980736 | tf_op jit(solution)/shard_map/dot_general | solution.py:120
  95.5 2.2 fusion.64
  97.8 2.4 multiply_subtract_fusion
  103.2 1.4 slice.397
  104.7 1.4 slice.395
  107.0 4.9 %fusion.9 = f32[2,16,256,128]{3,2,1,0:T(8,128)S(1)} fusion(f32[2,16,128,128]{3,2,1,0:T(8,128)} %copy-done.4, f32[2,15,128,128]{3,2,1,0:T(8,128)} %slice.397, f32[2,15,128,128]{3,2,1,0:T(8,128)} %slice.395, f32[2,1,128,128]{3,2,1,0:T(8,128)S(1)} %broadcast_in_dim.134), kind=kOutput, calls=%fused_computation.16 | convolution fusion | flops 809500672 | bytes 10354688 | tf_op jit(solution)/shard_map/...kl,...lm->...km/dot_general | solution.py:27
  114.1 2.3 fusion.7
  117.1 2.2 fusion.5
  121.2 2.2 fusion.3
  123.4 1.6 slice.410
  129.1 1.7 convolution_subtract_fusion
  130.8 3.4 %fusion.45 = f32[2,16,64,128]{3,2,1,0:T(8,128)} fusion(f32[2,16,64,128]{3,2,1,0:T(8,128)S(1)} %convolution_subtract_fusion, f32[2,15,128,128]{3,2,1,0:T(8,128)S(1)} %copy-done.12, f32[2,1,128,128]{3,2,1,0:T(8,128)S(1)} %broadcast_in_dim.134), kind=kOutput, calls=%fused_computation.61 | convolution fusion | flops 201850880 | bytes 4194304 | tf_op jit(solution)/shard_map/hnik,hnlk->hnil/dot_general | solution.py:27
  134.2 1.7 fusion.136
  136.0 1.5 slice_add_fusion.3
  137.5 15.9 %all-gather.5.cloned.1.call-done = bf16[16,2,2,128,128]{4,3,2,1,0:T(8,128)(2,1)} async-done(((bf16[1,2,2,128,128]{4,3,2,1,0:T(8,128)(2,1)}), bf16[16,2,2,128,128]{4,3,2,1,0:T(8,128)(2,1)}) %all-gather.5.cloned.1.call-update) | async-done | bytes 2097168 | tf_op jit(solution)/shard_map/all_gather | solution.py:84
  153.4 2.1 copy_convert_fusion
  160.7 3.0 multiply_reduce_fusion
  163.8 4.2 %fusion.120 = bf16[2,1024,128]{2,1,0:T(8,128)(2,1)S(1)} fusion(f32[2,16,64,128]{3,2,1,0:T(8,128)} %get-tuple-element.41, bf16[1024,2048]{1,0:T(8,128)(2,1)} %copy-done.1, f32[128]{0:T(128)S(1)} %copy-done.40, f32[2,1024]{1,0:T(2,128)S(1)} %rsqrt.47, bf16[2048,256]{1,0:T(8,128)(2,1)} %param.24), kind=kOutput, calls=%fused_computation.142 | convolution fusion | flops 1076363264 | bytes 6824448 | tf_op jit(solution)/shard_map/td,dhe->hte/dot_general | solution.py:126
  168.1 3.3 %bitcast_convert_fusion = bf16[1024,2048]{1,0:T(8,128)(2,1)} fusion(bf16[2,1024,128]{2,1,0:T(8,128)(2,1)S(1)} %fusion.120, bf16[2,128,2048]{2,1,0:T(8,128)(2,1)S(1)} %bitcast.198), kind=kOutput, calls=%fused_computation.5 | convolution fusion | flops 1075838976 | bytes 5767168 | tf_op jit(solution)/shard_map/htv,hvd->td/dot_general | solution.py:215
  172.7 60.2 %reduce-scatter.2.cloned.1.call-done = bf16[64,2048]{1,0:T(8,128)(2,1)} async-done(((bf16[1024,2048]{1,0:T(8,128)(2,1)}), bf16[64,2048]{1,0:T(8,128)(2,1)}) %reduce-scatter.2.cloned.1.call-update) | async-done | bytes 262160 | tf_op jit(solution)/shard_map/reduce_scatter | solution.py:214
  236.4 36.1 %all_to_all.8 = bf16[16,1,16,2048]{3,2,1,0:T(8,128)(2,1)S(1)} all-to-all(bf16[16,1,16,2048]{3,2,1,0:T(8,128)(2,1)S(1)} %bitcast.196), channel_id=1, replica_groups=mesh['seq'=16,'exp'=16] {'exp'}, dimensions={0} | all-to-all | bytes 2097152 | tf_op jit(solution)/shard_map/all_to_all | solution.py:244
  272.5 1.5 fusion.60
  274.0 4.0 %fusion.27 = bf16[1,16,16,2048]{3,2,0,1:T(8,128)(2,1)} fusion(bf16[1,512,2048]{2,1,0:T(8,128)(2,1)S(1)} %copy-done, bf16[1,2048,512]{2,1,0:T(8,128)(2,1)} %param.36, bf16[16,1,16,2048]{3,2,1,0:T(8,128)(2,1)S(1)} %all_to_all.8, f32[16,16,512]{2,1,0:T(8,128)} %fusion.60), kind=kOutput, calls=%fused_computation.37 | convolution fusion | flops 1075052544 | bytes 6815744 | tf_op jit(solution)/shard_map/esnf,efd->esnd/dot_general | solution.py:248
  278.0 3.7 %all-to-all-start.1 = ((bf16[1,16,16,2048]{3,2,0,1:T(8,128)(2,1)}), bf16[1,16,16,2048]{3,2,0,1:T(8,128)(2,1)S(1)}, u32[]{:S(2)}, u32[]{:S(2)}) async-start(bf16[1,16,16,2048]{3,2,0,1:T(8,128)(2,1)} %fusion.27), calls=%async_computation.2 | async-start | bytes 2097152 | tf_op jit(solution)/shard_map/all_to_all | solution.py:251
  282.0 27.1 %all-to-all-done.1 = bf16[1,16,16,2048]{3,2,0,1:T(8,128)(2,1)S(1)} async-done(((bf16[1,16,16,2048]{3,2,0,1:T(8,128)(2,1)}), bf16[1,16,16,2048]{3,2,0,1:T(8,128)(2,1)S(1)}, u32[]{:S(2)}, u32[]{:S(2)}) %all-to-all-start.1) | async-done | bytes 1048608 | tf_op jit(solution)/shard_map/all_to_all | solution.py:251
  309.5 1.7 add_convert_fusion
  (218 shorter events, 49.3 us)
Async XLA Ops:
  6.5 267.5 %copy-start = (bf16[1,512,2048]{2,1,0:T(8,128)(2,1)S(1)}, bf16[1,512,2048]{2,1,0:T(8,128)(2,1)}, u32[]{:S(2)}) copy-start(bf16[1,512,2048]{2,1,0:T(8,128)(2,1)} %param.37) | copy-start | bytes 6291460
  6.5 56.1 %all-gather.3.cloned.1.call-start = ((), (), s32[]{:S(2)}) async-start(), calls=%async_computation.3 | async-start | bytes 4456448 | tf_op jit(solution)/shard_map/all_gather | solution.py:115
  7.3 146.2 %all-gather.5.cloned.1.call-start = ((), (), s32[]{:S(2)}) async-start(), calls=%async_computation.4 | async-start | bytes 2228224 | tf_op jit(solution)/shard_map/all_gather | solution.py:84
  15.6 50.3 %copy-start.23 = (f32[2048]{0:T(1024)S(1)}, f32[2048]{0:T(1024)}, u32[]{:S(2)}) copy-start(f32[2048]{0:T(1024)} %param.20) | copy-start | bytes 24580
  62.6 3.4 %copy-start.5 = (bf16[1024,2048]{1,0:T(8,128)(2,1)S(1)}, bf16[1024,2048]{1,0:T(8,128)(2,1)}, u32[]{:S(2)}) copy-start(bf16[1024,2048]{1,0:T(8,128)(2,1)} %all-gather.3.cloned.1.call-done) | copy-start | bytes 12582916
  67.1 4.6 %copy-start.1 = (bf16[1024,2048]{1,0:T(8,128)(2,1)}, bf16[1024,2048]{1,0:T(8,128)(2,1)S(1)}, u32[]{:S(2)}) copy-start(bf16[1024,2048]{1,0:T(8,128)(2,1)S(1)} %fusion.2) | copy-start | bytes 12582916
  67.3 2.0 copy-start.39
  69.6 2.1 copy-start.18
  72.1 7.0 %collective-permute-start = (bf16[3,512]{0,1:T(8,128)(2,1)S(1)}, bf16[3,512]{0,1:T(8,128)(2,1)S(1)}, u32[]{:S(2)}, u32[]{:S(2)}) collective-permute-start(bf16[3,512]{0,1:T(8,128)(2,1)S(1)} %copy.65), channel_id=1, source_target_pairs={{0,16},{16,32},{32,48},{48,64},{64,80},{80,96},{96,112},{112,128},... | collective-permute-start | bytes 9224 | tf_op jit(solution)/shard_map/ppermute | solution.py:19
  80.9 2.3 copy-start.26
  80.9 2.3 copy-start.27
  80.9 2.3 copy-start.28
  80.9 2.3 copy-start.29
  95.5 2.3 copy-start.6
  95.5 2.3 copy-start.35
  97.7 5.5 %copy-start.2 = (f32[2,16,128,128]{3,2,1,0:T(8,128)}, f32[2,16,128,128]{3,2,1,0:T(8,128)S(1)}, u32[]{:S(2)}) copy-start(f32[2,16,128,128]{3,2,1,0:T(8,128)S(1)} %fusion.64) | copy-start | bytes 6291460
  100.2 4.5 %copy-start.4 = (f32[2,16,128,128]{3,2,1,0:T(8,128)}, f32[2,16,128,128]{3,2,1,0:T(8,128)S(1)}, u32[]{:S(2)}) copy-start(f32[2,16,128,128]{3,2,1,0:T(8,128)S(1)} %multiply_subtract_fusion) | copy-start | bytes 6291460
  106.7 126.1 %reduce-scatter.2.cloned.1.call-start = ((), (), s32[]{:S(2)}) async-start(), calls=%async_computation.5 | async-start | bytes 4456448 | tf_op jit(solution)/shard_map/reduce_scatter | solution.py:214
  123.4 2.6 copy-start.8
  127.3 1.8 copy-start.7
  128.3 2.5 copy-start.12
  130.8 5.1 %copy-start.10 = (f32[2,16,128,128]{3,2,1,0:T(8,128)S(1)}, f32[2,16,128,128]{3,2,1,0:T(8,128)}, u32[]{:S(2)}) copy-start(f32[2,16,128,128]{3,2,1,0:T(8,128)} %copy-done.9) | copy-start | bytes 6291460
  134.2 1.7 slice-start
  137.5 18.0 %copy-start.37 = (pred[16]{0:T(512)(128)(4,1)S(1)}, pred[16]{0:T(512)(128)(4,1)}, u32[]{:S(2)}) copy-start(pred[16]{0:T(512)(128)(4,1)} %iota_compare_fusion.13) | copy-start | bytes 52
  158.8 1.9 copy-start.14
  160.7 3.1 copy-start.40
  163.8 4.3 %copy-start.19 = (bf16[256,2048]{1,0:T(8,128)(2,1)S(1)}, bf16[256,2048]{1,0:T(8,128)(2,1)}, u32[]{:S(2)}) copy-start(bf16[256,2048]{1,0:T(8,128)(2,1)} %param.31) | copy-start | bytes 3145732
  171.4 62.8 %copy-start.24 = (f32[2048]{0:T(1024)S(1)}, f32[2048]{0:T(1024)}, u32[]{:S(2)}) copy-start(f32[2048]{0:T(1024)} %param.32) | copy-start | bytes 24580
  235.8 36.7 %copy-start.38 = (bf16[1,2048,512]{2,1,0:T(8,128)(2,1)S(1)}, bf16[1,2048,512]{2,1,0:T(8,128)(2,1)}, u32[]{:S(2)}) copy-start(bf16[1,2048,512]{2,1,0:T(8,128)(2,1)} %param.35) | copy-start | bytes 6291460
  278.0 31.0 %copy-start.36 = (f32[64,2]{0,1:T(2,128)S(1)}, f32[64,2]{0,1:T(2,128)}, u32[]{:S(2)}) copy-start(f32[64,2]{0,1:T(2,128)} %param.34) | copy-start | bytes 1540
  278.0 31.4 %copy-start.16 = (bf16[64,2048]{1,0:T(8,128)(2,1)S(1)}, bf16[64,2048]{1,0:T(8,128)(2,1)}, u32[]{:S(2)}) copy-start(bf16[64,2048]{1,0:T(8,128)(2,1)} %reduce-scatter.2.cloned.1.call-done) | copy-start | bytes 786436
  278.0 31.0 %all-to-all-start.1 = ((bf16[1,16,16,2048]{3,2,0,1:T(8,128)(2,1)}), bf16[1,16,16,2048]{3,2,0,1:T(8,128)(2,1)S(1)}, u32[]{:S(2)}, u32[]{:S(2)}) async-start(bf16[1,16,16,2048]{3,2,0,1:T(8,128)(2,1)} %fusion.27), calls=%async_computation.2 | async-start | bytes 2097152 | tf_op jit(solution)/shard_map/all_to_all | solution.py:251
  (15 other events, 15.2 us)
Sparse Core Ops, SparseCore 0:
  9.1 53.4 all-gather.2
  106.9 46.4 all-gather.4
  171.5 61.3 reduce-scatter.1

commit v7 on v6

--- a/solution.py
+++ b/solution.py
@@ -74,7 +74,11 @@
 
 def block_total(maps, adds):
     while maps.shape[1] > 1:
-        maps, adds = compose(maps[:, 0::2], adds[:, 0::2], maps[:, 1::2], adds[:, 1::2])
+        paired_maps = maps.reshape(maps.shape[0], -1, 2, *maps.shape[2:])
+        paired_adds = adds.reshape(adds.shape[0], -1, 2, *adds.shape[2:])
+        maps, adds = compose(
+            paired_maps[:, :, 0], paired_adds[:, :, 0], paired_maps[:, :, 1], paired_adds[:, :, 1]
+        )
     return maps[:, 0], adds[:, 0]
 
 
@@ -87,7 +91,11 @@
     maps = jnp.where(earlier, gathered[:, 0], eye)
     adds = jnp.where(earlier, gathered[:, 1], 0.0)
     while maps.shape[0] > 1:
-        maps, adds = compose(maps[0::2], adds[0::2], maps[1::2], adds[1::2])
+        paired_maps = maps.reshape(-1, 2, *maps.shape[1:])
+        paired_adds = adds.reshape(-1, 2, *adds.shape[1:])
+        maps, adds = compose(
+            paired_maps[:, 0], paired_adds[:, 0], paired_maps[:, 1], paired_adds[:, 1]
+        )
     return adds[0]
 
 

time: 323 us -> 324 us (level)
    unnamed x84 -> x85, local copies, waits for them, and re-layouts: 7.96 us -> 8.23 us
where the time goes in v7:
time: 324 us; the launch traced here: 319 us
  waiting for transfers between devices  151 us (47%)
  matrix products  63.9 us (20%)
  blocking collectives  36.1 us (11%)
  other arithmetic  23.6 us (7%)
  local copies, waits for them, and re-layouts  22.3 us (7%)
  between operations  14.8 us (5%)
  starting transfers between devices  7.25 us (2%)
    reduce_scatter x1, waiting for transfers between devices, per_device(): lax.psum_scatter(jnp.einsum('htv,hvd->td', gated, w_out.reshape(value_hea...  60.2 us
    all_gather x1, waiting for transfers between devices, per_device(): whole = lax.all_gather(tokens, 'exp', axis=1, tiled=True)  47 us
    dot_general x34, matrix products, mix(): return jnp.einsum(form, left_arr, right_arr, precision=HIGH)  42.1 us
    all_to_all x1, blocking collectives, per_device(): lax.all_to_all(outgoing, 'exp', split_axis=0, concat_axis=1, tiled=True)  36.1 us
    all_to_all x1, waiting for transfers between devices, per_device(): lax.all_to_all(processed, 'exp', split_axis=1, concat_axis=0, tiled=True)  27.1 us
    all_gather x1, waiting for transfers between devices, shard_prefix(): gathered = lax.all_gather(packed, 'seq').astype(total_map.dtype)  15.9 us
    unnamed x85, local copies, waits for them, and re-layouts  8.23 us
    dot_general x3, matrix products, project_heads(): jnp.einsum('td,dhe->hte', rows, split, preferred_element_type=jnp.float32)  6.55 us
  transfers between devices with their start and end apart: 5, of which 4 were waited for; matrix products, arithmetic and copies ran while one was open for 12% of the time, Pallas kernels for 0%

profile of v7, /device:TPU:1, one launch (start us, length us, event | category | flops | bytes accessed | tf_op | source)
XLA Modules:
  0.0 319.0 jit_solution(14799399594952528686)
XLA Ops:
  13.3 1.4 fusion.298
  15.7 47.0 %all-gather.3.cloned.1.call-done = bf16[1024,2048]{1,0:T(8,128)(2,1)} async-done(((bf16[1024,128]{1,0:T(8,128)(2,1)}), bf16[1024,2048]{1,0:T(8,128)(2,1)}) %all-gather.3.cloned.1.call-update) | async-done | bytes 4194320 | tf_op jit(solution)/shard_map/all_gather | solution.py:123
  62.6 3.2 %fusion = f32[1024]{0:T(1024)S(1)} fusion(bf16[1024,2048]{1,0:T(8,128)(2,1)} %all-gather.3.cloned.1.call-done), kind=kLoop, calls=%fused_computation.2 | loop fusion | flops 6290432 | bytes 4198400 | tf_op jit(solution)/shard_map/reduce_sum | solution.py:23
  67.3 1.5 convolution_convert_fusion.2
  69.6 2.1 fusion.89
  72.0 3.3 %collective-permute-start = (bf16[3,512]{0,1:T(8,128)(2,1)S(1)}, bf16[3,512]{0,1:T(8,128)(2,1)S(1)}, u32[]{:S(2)}, u32[]{:S(2)}) collective-permute-start(bf16[3,512]{0,1:T(8,128)(2,1)S(1)} %copy.163), channel_id=1, source_target_pairs={{0,16},{16,32},{32,48},{48,64},{64,80},{80,96},{96,112},{112,128},... | collective-permute-start | bytes 9224 | tf_op jit(solution)/shard_map/ppermute | solution.py:19
  75.3 3.7 %convolution_convert_fusion.3 = bf16[1024,128]{0,1:T(8,128)(2,1)S(1)} fusion(bf16[1024,2048]{1,0:T(8,128)(2,1)} %copy-done.1, bf16[2048,128]{1,0:T(8,128)(2,1)S(1)} %copy-done.18), kind=kOutput, calls=%fused_computation.100 | convolution fusion | flops 537001984 | bytes 4980736 | tf_op jit(solution)/shard_map/dot_general | solution.py:128
  95.5 2.2 fusion.62
  97.7 2.4 multiply_subtract_fusion
  103.3 1.5 slice.391
  104.7 1.4 slice.389
  107.1 4.9 %fusion.9 = f32[2,16,256,128]{3,2,1,0:T(8,128)S(1)} fusion(f32[2,16,128,128]{3,2,1,0:T(8,128)} %copy-done.4, f32[2,15,128,128]{3,2,1,0:T(8,128)} %slice.391, f32[2,15,128,128]{3,2,1,0:T(8,128)} %slice.389, f32[2,1,128,128]{3,2,1,0:T(8,128)S(1)} %broadcast_in_dim.134), kind=kOutput, calls=%fused_computation.16 | convolution fusion | flops 809500672 | bytes 10354688 | tf_op jit(solution)/shard_map/...kl,...lm->...km/dot_general | solution.py:27
  114.2 2.3 fusion.7
  117.1 2.2 fusion.5
  121.3 2.2 fusion.3
  123.5 1.6 slice.404
  129.1 1.7 convolution_subtract_fusion
  130.9 3.4 %fusion.43 = f32[2,16,64,128]{3,2,1,0:T(8,128)} fusion(f32[2,16,64,128]{3,2,1,0:T(8,128)S(1)} %convolution_subtract_fusion, f32[2,15,128,128]{3,2,1,0:T(8,128)S(1)} %copy-done.12, f32[2,1,128,128]{3,2,1,0:T(8,128)S(1)} %broadcast_in_dim.134), kind=kOutput, calls=%fused_computation.57 | convolution fusion | flops 201850880 | bytes 4194304 | tf_op jit(solution)/shard_map/hnik,hnlk->hnil/dot_general | solution.py:27
  134.3 1.7 fusion.134
  136.0 1.5 slice_add_fusion.3
  137.5 15.9 %all-gather.5.cloned.1.call-done = bf16[16,2,2,128,128]{4,3,2,1,0:T(8,128)(2,1)} async-done(((bf16[1,2,2,128,128]{4,3,2,1,0:T(8,128)(2,1)}), bf16[16,2,2,128,128]{4,3,2,1,0:T(8,128)(2,1)}) %all-gather.5.cloned.1.call-update) | async-done | bytes 2097168 | tf_op jit(solution)/shard_map/all_gather | solution.py:88
  153.5 2.1 copy_convert_fusion
  161.5 2.9 multiply_reduce_fusion
  164.6 4.2 %fusion.120 = bf16[2,1024,128]{2,1,0:T(8,128)(2,1)S(1)} fusion(f32[2,16,64,128]{3,2,1,0:T(8,128)} %get-tuple-element.47, bf16[1024,2048]{1,0:T(8,128)(2,1)} %copy-done.1, f32[128]{0:T(128)S(1)} %copy-done.40, f32[2,1024]{1,0:T(2,128)S(1)} %rsqrt.47, bf16[2048,256]{1,0:T(8,128)(2,1)} %param.24), kind=kOutput, calls=%fused_computation.148 | convolution fusion | flops 1076363264 | bytes 6824448 | tf_op jit(solution)/shard_map/td,dhe->hte/dot_general | solution.py:134
  168.8 3.3 %bitcast_convert_fusion = bf16[1024,2048]{1,0:T(8,128)(2,1)} fusion(bf16[2,1024,128]{2,1,0:T(8,128)(2,1)S(1)} %fusion.120, bf16[2,128,2048]{2,1,0:T(8,128)(2,1)S(1)} %bitcast.362), kind=kOutput, calls=%fused_computation.5 | convolution fusion | flops 1075838976 | bytes 5767168 | tf_op jit(solution)/shard_map/htv,hvd->td/dot_general | solution.py:223
  173.5 60.2 %reduce-scatter.2.cloned.1.call-done = bf16[64,2048]{1,0:T(8,128)(2,1)} async-done(((bf16[1024,2048]{1,0:T(8,128)(2,1)}), bf16[64,2048]{1,0:T(8,128)(2,1)}) %reduce-scatter.2.cloned.1.call-update) | async-done | bytes 262160 | tf_op jit(solution)/shard_map/reduce_scatter | solution.py:222
  237.1 36.1 %all_to_all.8 = bf16[16,1,16,2048]{3,2,1,0:T(8,128)(2,1)S(1)} all-to-all(bf16[16,1,16,2048]{3,2,1,0:T(8,128)(2,1)S(1)} %bitcast.350), channel_id=1, replica_groups=mesh['seq'=16,'exp'=16] {'exp'}, dimensions={0} | all-to-all | bytes 2097152 | tf_op jit(solution)/shard_map/all_to_all | solution.py:252
  273.3 1.5 fusion.58
  274.8 4.0 %fusion.27 = bf16[1,16,16,2048]{3,2,0,1:T(8,128)(2,1)} fusion(bf16[1,512,2048]{2,1,0:T(8,128)(2,1)S(1)} %copy-done, bf16[1,2048,512]{2,1,0:T(8,128)(2,1)} %param.36, bf16[16,1,16,2048]{3,2,1,0:T(8,128)(2,1)S(1)} %all_to_all.8, f32[16,16,512]{2,1,0:T(8,128)} %fusion.58), kind=kOutput, calls=%fused_computation.37 | convolution fusion | flops 1075052544 | bytes 6815744 | tf_op jit(solution)/shard_map/esnf,efd->esnd/dot_general | solution.py:256
  278.8 3.7 %all-to-all-start.1 = ((bf16[1,16,16,2048]{3,2,0,1:T(8,128)(2,1)}), bf16[1,16,16,2048]{3,2,0,1:T(8,128)(2,1)S(1)}, u32[]{:S(2)}, u32[]{:S(2)}) async-start(bf16[1,16,16,2048]{3,2,0,1:T(8,128)(2,1)} %fusion.27), calls=%async_computation.2 | async-start | bytes 2097152 | tf_op jit(solution)/shard_map/all_to_all | solution.py:259
  282.7 27.1 %all-to-all-done.1 = bf16[1,16,16,2048]{3,2,0,1:T(8,128)(2,1)S(1)} async-done(((bf16[1,16,16,2048]{3,2,0,1:T(8,128)(2,1)}), bf16[1,16,16,2048]{3,2,0,1:T(8,128)(2,1)S(1)}, u32[]{:S(2)}, u32[]{:S(2)}) %all-to-all-start.1) | async-done | bytes 1048608 | tf_op jit(solution)/shard_map/all_to_all | solution.py:259
  310.2 1.7 add_convert_fusion
  (220 shorter events, 50.2 us)
Async XLA Ops:
  6.5 268.3 %copy-start = (bf16[1,512,2048]{2,1,0:T(8,128)(2,1)S(1)}, bf16[1,512,2048]{2,1,0:T(8,128)(2,1)}, u32[]{:S(2)}) copy-start(bf16[1,512,2048]{2,1,0:T(8,128)(2,1)} %param.37) | copy-start | bytes 6291460
  6.5 56.1 %all-gather.3.cloned.1.call-start = ((), (), s32[]{:S(2)}) async-start(), calls=%async_computation.3 | async-start | bytes 4456448 | tf_op jit(solution)/shard_map/all_gather | solution.py:123
  7.3 146.2 %all-gather.5.cloned.1.call-start = ((), (), s32[]{:S(2)}) async-start(), calls=%async_computation.4 | async-start | bytes 2228224 | tf_op jit(solution)/shard_map/all_gather | solution.py:88
  15.7 50.2 %copy-start.23 = (f32[2048]{0:T(1024)S(1)}, f32[2048]{0:T(1024)}, u32[]{:S(2)}) copy-start(f32[2048]{0:T(1024)} %param.20) | copy-start | bytes 24580
  62.6 3.4 %copy-start.5 = (bf16[1024,2048]{1,0:T(8,128)(2,1)S(1)}, bf16[1024,2048]{1,0:T(8,128)(2,1)}, u32[]{:S(2)}) copy-start(bf16[1024,2048]{1,0:T(8,128)(2,1)} %all-gather.3.cloned.1.call-done) | copy-start | bytes 12582916
  67.1 4.5 %copy-start.1 = (bf16[1024,2048]{1,0:T(8,128)(2,1)}, bf16[1024,2048]{1,0:T(8,128)(2,1)S(1)}, u32[]{:S(2)}) copy-start(bf16[1024,2048]{1,0:T(8,128)(2,1)S(1)} %fusion.2) | copy-start | bytes 12582916
  67.3 2.0 copy-start.39
  69.6 2.1 copy-start.18
  72.0 7.0 %collective-permute-start = (bf16[3,512]{0,1:T(8,128)(2,1)S(1)}, bf16[3,512]{0,1:T(8,128)(2,1)S(1)}, u32[]{:S(2)}, u32[]{:S(2)}) collective-permute-start(bf16[3,512]{0,1:T(8,128)(2,1)S(1)} %copy.163), channel_id=1, source_target_pairs={{0,16},{16,32},{32,48},{48,64},{64,80},{80,96},{96,112},{112,128},... | collective-permute-start | bytes 9224 | tf_op jit(solution)/shard_map/ppermute | solution.py:19
  80.9 2.3 copy-start.26
  80.9 2.3 copy-start.27
  80.9 2.3 copy-start.28
  80.9 2.3 copy-start.29
  95.5 4.6 %copy-start.6 = (f32[2,16,64,256]{3,2,1,0:T(8,128)}, f32[2,16,64,256]{3,2,1,0:T(8,128)S(1)}, u32[]{:S(2)}) copy-start(f32[2,16,64,256]{3,2,1,0:T(8,128)S(1)} %fusion.39) | copy-start | bytes 6291460
  95.5 2.2 copy-start.35
  97.7 5.6 %copy-start.2 = (f32[2,16,128,128]{3,2,1,0:T(8,128)}, f32[2,16,128,128]{3,2,1,0:T(8,128)S(1)}, u32[]{:S(2)}) copy-start(f32[2,16,128,128]{3,2,1,0:T(8,128)S(1)} %fusion.62) | copy-start | bytes 6291460
  100.1 4.6 %copy-start.4 = (f32[2,16,128,128]{3,2,1,0:T(8,128)}, f32[2,16,128,128]{3,2,1,0:T(8,128)S(1)}, u32[]{:S(2)}) copy-start(f32[2,16,128,128]{3,2,1,0:T(8,128)S(1)} %multiply_subtract_fusion) | copy-start | bytes 6291460
  106.8 126.9 %reduce-scatter.2.cloned.1.call-start = ((), (), s32[]{:S(2)}) async-start(), calls=%async_computation.5 | async-start | bytes 4456448 | tf_op jit(solution)/shard_map/reduce_scatter | solution.py:222
  123.5 2.6 copy-start.8
  127.3 1.8 copy-start.7
  128.3 2.5 copy-start.12
  130.9 5.1 %copy-start.10 = (f32[2,16,128,128]{3,2,1,0:T(8,128)S(1)}, f32[2,16,128,128]{3,2,1,0:T(8,128)}, u32[]{:S(2)}) copy-start(f32[2,16,128,128]{3,2,1,0:T(8,128)} %copy-done.9) | copy-start | bytes 6291460
  134.3 1.7 slice-start
  159.6 1.6 copy-start.11
  159.6 1.9 copy-start.14
  161.5 3.0 copy-start.40
  164.6 4.3 %copy-start.19 = (bf16[256,2048]{1,0:T(8,128)(2,1)S(1)}, bf16[256,2048]{1,0:T(8,128)(2,1)}, u32[]{:S(2)}) copy-start(bf16[256,2048]{1,0:T(8,128)(2,1)} %param.31) | copy-start | bytes 3145732
  172.1 62.8 %copy-start.24 = (f32[2048]{0:T(1024)S(1)}, f32[2048]{0:T(1024)}, u32[]{:S(2)}) copy-start(f32[2048]{0:T(1024)} %param.32) | copy-start | bytes 24580
  236.6 36.7 %copy-start.38 = (bf16[1,2048,512]{2,1,0:T(8,128)(2,1)S(1)}, bf16[1,2048,512]{2,1,0:T(8,128)(2,1)}, u32[]{:S(2)}) copy-start(bf16[1,2048,512]{2,1,0:T(8,128)(2,1)} %param.35) | copy-start | bytes 6291460
  278.8 31.1 %copy-start.36 = (f32[64,2]{0,1:T(2,128)S(1)}, f32[64,2]{0,1:T(2,128)}, u32[]{:S(2)}) copy-start(f32[64,2]{0,1:T(2,128)} %param.34) | copy-start | bytes 1540
  278.8 31.4 %copy-start.16 = (bf16[64,2048]{1,0:T(8,128)(2,1)S(1)}, bf16[64,2048]{1,0:T(8,128)(2,1)}, u32[]{:S(2)}) copy-start(bf16[64,2048]{1,0:T(8,128)(2,1)} %reduce-scatter.2.cloned.1.call-done) | copy-start | bytes 786436
  278.8 31.0 %all-to-all-start.1 = ((bf16[1,16,16,2048]{3,2,0,1:T(8,128)(2,1)}), bf16[1,16,16,2048]{3,2,0,1:T(8,128)(2,1)S(1)}, u32[]{:S(2)}, u32[]{:S(2)}) async-start(bf16[1,16,16,2048]{3,2,0,1:T(8,128)(2,1)} %fusion.27), calls=%async_computation.2 | async-start | bytes 2097152 | tf_op jit(solution)/shard_map/all_to_all | solution.py:259
  (15 other events, 14.2 us)
Sparse Core Ops, SparseCore 0:
  9.1 53.4 all-gather.2
  106.9 46.5 all-gather.4
  172.3 61.3 reduce-scatter.1

commit v8 on v6

--- a/solution.py
+++ b/solution.py
@@ -80,15 +80,19 @@
 
 def shard_prefix(total_map, total_add):
     place = lax.axis_index("seq")
-    packed = jnp.stack([total_map, total_add]).astype(jnp.bfloat16)
+    rows = total_map.shape[-2]
+    packed = jnp.concatenate([total_map, total_add], -2).astype(jnp.bfloat16)
     gathered = lax.all_gather(packed, "seq").astype(total_map.dtype)
     earlier = (jnp.arange(gathered.shape[0]) < place)[:, None, None, None]
     eye = jnp.eye(total_map.shape[-1], dtype=total_map.dtype)
-    maps = jnp.where(earlier, gathered[:, 0], eye)
-    adds = jnp.where(earlier, gathered[:, 1], 0.0)
-    while maps.shape[0] > 1:
-        maps, adds = compose(maps[0::2], adds[0::2], maps[1::2], adds[1::2])
-    return adds[0]
+    ident = jnp.concatenate([eye, jnp.zeros_like(eye)], 0)
+    pairs = jnp.where(earlier, gathered, ident)
+    while pairs.shape[0] > 1:
+        split = pairs.reshape(-1, 2, *pairs.shape[1:])
+        first, then = split[:, 0], split[:, 1]
+        moved = mix("...kl,...lm->...km", first, then[..., :rows, :])
+        pairs = jnp.concatenate([moved[..., :rows, :], moved[..., rows:, :] + then[..., rows:, :]], -2)
+    return pairs[0][..., rows:, :]
 
 
 def per_device(

time: 323 us -> 329 us (1.019)
  local copies, waits for them, and re-layouts: 21.5 us -> 26.3 us
    unnamed x84 -> x110, local copies, waits for them, and re-layouts: 7.96 us -> 12.1 us
where the time goes in v8:
time: 329 us; the launch traced here: 324 us
  waiting for transfers between devices  150 us (46%)
  matrix products  64.7 us (20%)
  blocking collectives  36.2 us (11%)
  local copies, waits for them, and re-layouts  26.3 us (8%)
  other arithmetic  25 us (8%)
  between operations  14.9 us (5%)
  starting transfers between devices  7.25 us (2%)
    reduce_scatter x1, waiting for transfers between devices, per_device(): lax.psum_scatter(jnp.einsum('htv,hvd->td', gated, w_out.reshape(value_hea...  60.2 us
    all_gather x1, waiting for transfers between devices, per_device(): whole = lax.all_gather(tokens, 'exp', axis=1, tiled=True)  46.4 us
    dot_general x34, matrix products, mix(): return jnp.einsum(form, left_arr, right_arr, precision=HIGH)  42.9 us
    all_to_all x1, blocking collectives, per_device(): lax.all_to_all(outgoing, 'exp', split_axis=0, concat_axis=1, tiled=True)  36.2 us
    all_to_all x1, waiting for transfers between devices, per_device(): lax.all_to_all(processed, 'exp', split_axis=1, concat_axis=0, tiled=True)  27.1 us
    all_gather x1, waiting for transfers between devices, shard_prefix(): gathered = lax.all_gather(packed, 'seq').astype(total_map.dtype)  15.6 us
    unnamed x110, local copies, waits for them, and re-layouts  12.1 us
  transfers between devices with their start and end apart: 5, of which 4 were waited for; matrix products, arithmetic and copies ran while one was open for 12% of the time, Pallas kernels for 0%

profile of v8, /device:TPU:1, one launch (start us, length us, event | category | flops | bytes accessed | tf_op | source)
XLA Modules:
  0.0 324.3 jit_solution(6061677567038901705)
XLA Ops:
  16.2 46.4 %all-gather.3.cloned.1.call-done = bf16[1024,2048]{1,0:T(8,128)(2,1)} async-done(((bf16[1024,128]{1,0:T(8,128)(2,1)}), bf16[1024,2048]{1,0:T(8,128)(2,1)}) %all-gather.3.cloned.1.call-update) | async-done | bytes 4194320 | tf_op jit(solution)/shard_map/all_gather | solution.py:119
  62.6 3.2 fusion
  67.3 1.5 convolution_convert_fusion.2
  69.6 2.1 fusion.86
  72.7 3.3 %collective-permute-start = (bf16[3,512]{0,1:T(8,128)(2,1)}, bf16[3,512]{0,1:T(8,128)(2,1)S(1)}, u32[]{:S(2)}, u32[]{:S(2)}) collective-permute-start(bf16[3,512]{0,1:T(8,128)(2,1)} %copy.98), channel_id=1, source_target_pairs={{0,16},{16,32},{32,48},{48,64},{64,80},{80,96},{96,112},{112,128},... | collective-permute-start | bytes 9224 | tf_op jit(solution)/shard_map/ppermute | solution.py:19
  75.9 3.7 %convolution_convert_fusion.3 = bf16[1024,128]{0,1:T(8,128)(2,1)S(1)} fusion(bf16[1024,2048]{1,0:T(8,128)(2,1)} %copy-done.1, bf16[2048,128]{1,0:T(8,128)(2,1)S(1)} %copy-done.24), kind=kOutput, calls=%fused_computation.98 | convolution fusion | flops 537001984 | bytes 4980736 | tf_op jit(solution)/shard_map/dot_general | solution.py:124
  93.4 1.6 fusion.281
  95.0 1.5 broadcast_multiply_fusion.1
  101.1 2.1 fusion.59
  103.3 2.4 multiply_subtract_fusion
  105.7 1.5 slice.392
  112.7 4.9 %fusion.9 = f32[2,16,256,128]{3,2,1,0:T(8,128)S(1)} fusion(f32[2,16,128,128]{3,2,1,0:T(8,128)} %copy-done.4, f32[2,15,128,128]{3,2,1,0:T(8,128)} %slice.394, f32[2,15,128,128]{3,2,1,0:T(8,128)} %slice.392, f32[2,1,128,128]{3,2,1,0:T(8,128)S(1)} %broadcast_in_dim.125), kind=kOutput, calls=%fused_computation.16 | convolution fusion | flops 809500672 | bytes 10354688 | tf_op jit(solution)/shard_map/...kl,...lm->...km/dot_general | solution.py:27
  119.8 2.3 fusion.7
  122.8 2.2 fusion.5
  126.9 2.2 fusion.3
  129.1 2.1 copy-done.8
  135.6 1.7 convolution_subtract_fusion
  137.4 3.4 %fusion.44 = f32[2,16,64,128]{3,2,1,0:T(8,128)} fusion(f32[2,16,64,128]{3,2,1,0:T(8,128)S(1)} %convolution_subtract_fusion, f32[2,15,128,128]{3,2,1,0:T(8,128)S(1)} %copy-done.16, f32[2,1,128,128]{3,2,1,0:T(8,128)S(1)} %broadcast_in_dim.125), kind=kOutput, calls=%fused_computation.61 | convolution fusion | flops 201850880 | bytes 4194304 | tf_op jit(solution)/shard_map/hnik,hnlk->hnil/dot_general | solution.py:27
  140.8 1.7 fusion.128
  142.5 1.5 slice_add_fusion.3
  144.0 15.6 %all-gather.5.cloned.1.call-done = bf16[16,2,256,128]{3,2,1,0:T(8,128)(2,1)} async-done(((bf16[1,2,256,128]{3,2,1,0:T(8,128)(2,1)}), bf16[16,2,256,128]{3,2,1,0:T(8,128)(2,1)}) %all-gather.5.cloned.1.call-update) | async-done | bytes 2097168 | tf_op jit(solution)/shard_map/all_gather | solution.py:85
  159.6 2.1 convert_select_fusion
  166.9 3.0 multiply_reduce_fusion
  169.9 4.2 %fusion.113 = bf16[2,1024,128]{2,1,0:T(8,128)(2,1)S(1)} fusion(f32[2,16,64,128]{3,2,1,0:T(8,128)} %get-tuple-element.43, bf16[1024,2048]{1,0:T(8,128)(2,1)} %copy-done.1, f32[128]{0:T(128)S(1)} %copy-done.53, f32[2,1024]{1,0:T(2,128)S(1)} %rsqrt.47, bf16[2048,256]{1,0:T(8,128)(2,1)} %param.24), kind=kOutput, calls=%fused_computation.139 | convolution fusion | flops 1076363264 | bytes 6824448 | tf_op jit(solution)/shard_map/td,dhe->hte/dot_general | solution.py:130
  174.2 3.3 %bitcast_convert_fusion = bf16[1024,2048]{1,0:T(8,128)(2,1)} fusion(bf16[2,1024,128]{2,1,0:T(8,128)(2,1)S(1)} %fusion.113, bf16[2,128,2048]{2,1,0:T(8,128)(2,1)S(1)} %bitcast.231), kind=kOutput, calls=%fused_computation.5 | convolution fusion | flops 1075838976 | bytes 5767168 | tf_op jit(solution)/shard_map/htv,hvd->td/dot_general | solution.py:219
  178.8 60.2 %reduce-scatter.2.cloned.1.call-done = bf16[64,2048]{1,0:T(8,128)(2,1)} async-done(((bf16[1024,2048]{1,0:T(8,128)(2,1)}), bf16[64,2048]{1,0:T(8,128)(2,1)}) %reduce-scatter.2.cloned.1.call-update) | async-done | bytes 262160 | tf_op jit(solution)/shard_map/reduce_scatter | solution.py:218
  242.5 36.2 %all_to_all.8 = bf16[16,1,16,2048]{3,2,1,0:T(8,128)(2,1)S(1)} all-to-all(bf16[16,1,16,2048]{3,2,1,0:T(8,128)(2,1)S(1)} %bitcast.229), channel_id=1, replica_groups=mesh['seq'=16,'exp'=16] {'exp'}, dimensions={0} | all-to-all | bytes 2097152 | tf_op jit(solution)/shard_map/all_to_all | solution.py:248
  278.6 1.5 fusion.55
  280.1 4.0 %fusion.27 = bf16[1,16,16,2048]{3,2,0,1:T(8,128)(2,1)} fusion(bf16[1,512,2048]{2,1,0:T(8,128)(2,1)S(1)} %copy-done, bf16[1,2048,512]{2,1,0:T(8,128)(2,1)} %param.36, bf16[16,1,16,2048]{3,2,1,0:T(8,128)(2,1)S(1)} %all_to_all.8, f32[16,16,512]{2,1,0:T(8,128)} %fusion.55), kind=kOutput, calls=%fused_computation.38 | convolution fusion | flops 1075052544 | bytes 6815744 | tf_op jit(solution)/shard_map/esnf,efd->esnd/dot_general | solution.py:252
  284.2 3.7 %all-to-all-start.1 = ((bf16[1,16,16,2048]{3,2,0,1:T(8,128)(2,1)}), bf16[1,16,16,2048]{3,2,0,1:T(8,128)(2,1)S(1)}, u32[]{:S(2)}, u32[]{:S(2)}) async-start(bf16[1,16,16,2048]{3,2,0,1:T(8,128)(2,1)} %fusion.27), calls=%async_computation.2 | async-start | bytes 2097152 | tf_op jit(solution)/shard_map/all_to_all | solution.py:255
  288.1 27.1 %all-to-all-done.1 = bf16[1,16,16,2048]{3,2,0,1:T(8,128)(2,1)S(1)} async-done(((bf16[1,16,16,2048]{3,2,0,1:T(8,128)(2,1)}), bf16[1,16,16,2048]{3,2,0,1:T(8,128)(2,1)S(1)}, u32[]{:S(2)}, u32[]{:S(2)}) %all-to-all-start.1) | async-done | bytes 1048608 | tf_op jit(solution)/shard_map/all_to_all | solution.py:255
  315.6 1.7 add_convert_fusion
  (245 shorter events, 55.6 us)
Async XLA Ops:
  6.5 273.6 %copy-start = (bf16[1,512,2048]{2,1,0:T(8,128)(2,1)S(1)}, bf16[1,512,2048]{2,1,0:T(8,128)(2,1)}, u32[]{:S(2)}) copy-start(bf16[1,512,2048]{2,1,0:T(8,128)(2,1)} %param.37) | copy-start | bytes 6291460
  6.5 56.1 %all-gather.3.cloned.1.call-start = ((), (), s32[]{:S(2)}) async-start(), calls=%async_computation.3 | async-start | bytes 4456448 | tf_op jit(solution)/shard_map/all_gather | solution.py:119
  7.3 152.3 %all-gather.5.cloned.1.call-start = ((), (), s32[]{:S(2)}) async-start(), calls=%async_computation.4 | async-start | bytes 2228224 | tf_op jit(solution)/shard_map/all_gather | solution.py:85
  16.2 49.6 %copy-start.36 = (f32[2048]{0:T(1024)S(1)}, f32[2048]{0:T(1024)}, u32[]{:S(2)}) copy-start(f32[2048]{0:T(1024)} %param.20) | copy-start | bytes 24580
  62.6 3.4 %copy-start.5 = (bf16[1024,2048]{1,0:T(8,128)(2,1)S(1)}, bf16[1024,2048]{1,0:T(8,128)(2,1)}, u32[]{:S(2)}) copy-start(bf16[1024,2048]{1,0:T(8,128)(2,1)} %all-gather.3.cloned.1.call-done) | copy-start | bytes 12582916
  67.1 4.5 %copy-start.1 = (bf16[1024,2048]{1,0:T(8,128)(2,1)}, bf16[1024,2048]{1,0:T(8,128)(2,1)S(1)}, u32[]{:S(2)}) copy-start(bf16[1024,2048]{1,0:T(8,128)(2,1)S(1)} %fusion.2) | copy-start | bytes 12582916
  72.7 7.3 %copy-start.43 = (f32[1,256]{1,0:T(1,128)S(1)}, f32[1,256]{1,0:T(1,128)}, u32[]{:S(2)}) copy-start(f32[1,256]{1,0:T(1,128)} %get-tuple-element.32) | copy-start | bytes 3076
  72.7 7.3 %copy-start.44 = (f32[1,256]{1,0:T(1,128)S(1)}, f32[1,256]{1,0:T(1,128)}, u32[]{:S(2)}) copy-start(f32[1,256]{1,0:T(1,128)} %get-tuple-element.33) | copy-start | bytes 3076
  72.7 7.3 %copy-start.45 = (f32[1,256]{1,0:T(1,128)S(1)}, f32[1,256]{1,0:T(1,128)}, u32[]{:S(2)}) copy-start(f32[1,256]{1,0:T(1,128)} %get-tuple-element.34) | copy-start | bytes 3076
  72.7 7.3 %copy-start.46 = (f32[1,256]{1,0:T(1,128)S(1)}, f32[1,256]{1,0:T(1,128)}, u32[]{:S(2)}) copy-start(f32[1,256]{1,0:T(1,128)} %get-tuple-element.35) | copy-start | bytes 3076
  72.7 7.0 %collective-permute-start = (bf16[3,512]{0,1:T(8,128)(2,1)}, bf16[3,512]{0,1:T(8,128)(2,1)S(1)}, u32[]{:S(2)}, u32[]{:S(2)}) collective-permute-start(bf16[3,512]{0,1:T(8,128)(2,1)} %copy.98), channel_id=1, source_target_pairs={{0,16},{16,32},{32,48},{48,64},{64,80},{80,96},{96,112},{112,128},... | collective-permute-start | bytes 9224 | tf_op jit(solution)/shard_map/ppermute | solution.py:19
  95.0 2.8 copy-start.39
  95.0 2.8 copy-start.40
  95.0 2.8 copy-start.41
  95.0 2.8 copy-start.42
  101.1 4.6 %copy-start.6 = (f32[2,16,64,256]{3,2,1,0:T(8,128)}, f32[2,16,64,256]{3,2,1,0:T(8,128)S(1)}, u32[]{:S(2)}) copy-start(f32[2,16,64,256]{3,2,1,0:T(8,128)S(1)} %fusion.40) | copy-start | bytes 6291460
  103.3 6.7 %copy-start.2 = (f32[2,16,128,128]{3,2,1,0:T(8,128)}, f32[2,16,128,128]{3,2,1,0:T(8,128)S(1)}, u32[]{:S(2)}) copy-start(f32[2,16,128,128]{3,2,1,0:T(8,128)S(1)} %fusion.59) | copy-start | bytes 6291460
  105.7 3.2 copy-start.4
  112.4 126.5 %reduce-scatter.2.cloned.1.call-start = ((), (), s32[]{:S(2)}) async-start(), calls=%async_computation.5 | async-start | bytes 4456448 | tf_op jit(solution)/shard_map/reduce_scatter | solution.py:218
  131.2 2.7 copy-start.12
  131.2 2.7 copy-start.35
  132.6 2.3 copy-start.26
  134.9 2.5 copy-start.16
  137.4 5.1 %copy-start.14 = (f32[2,16,128,128]{3,2,1,0:T(8,128)S(1)}, f32[2,16,128,128]{3,2,1,0:T(8,128)}, u32[]{:S(2)}) copy-start(f32[2,16,128,128]{3,2,1,0:T(8,128)} %copy-done.13) | copy-start | bytes 6291460
  142.5 17.1 %copy-start.50 = (pred[16]{0:T(512)(128)(4,1)S(1)}, pred[16]{0:T(512)(128)(4,1)}, u32[]{:S(2)}) copy-start(pred[16]{0:T(512)(128)(4,1)} %iota_compare_fusion.13) | copy-start | bytes 52
  166.9 3.0 copy-start.53
  169.9 4.3 %copy-start.25 = (bf16[256,2048]{1,0:T(8,128)(2,1)S(1)}, bf16[256,2048]{1,0:T(8,128)(2,1)}, u32[]{:S(2)}) copy-start(bf16[256,2048]{1,0:T(8,128)(2,1)} %param.31) | copy-start | bytes 3145732
  177.5 62.8 %copy-start.37 = (f32[2048]{0:T(1024)S(1)}, f32[2048]{0:T(1024)}, u32[]{:S(2)}) copy-start(f32[2048]{0:T(1024)} %param.32) | copy-start | bytes 24580
  241.9 36.7 %copy-start.51 = (bf16[1,2048,512]{2,1,0:T(8,128)(2,1)S(1)}, bf16[1,2048,512]{2,1,0:T(8,128)(2,1)}, u32[]{:S(2)}) copy-start(bf16[1,2048,512]{2,1,0:T(8,128)(2,1)} %param.35) | copy-start | bytes 6291460
  284.1 31.0 %copy-start.49 = (f32[64,2]{0,1:T(2,128)S(1)}, f32[64,2]{0,1:T(2,128)}, u32[]{:S(2)}) copy-start(f32[64,2]{0,1:T(2,128)} %param.34) | copy-start | bytes 1540
  284.2 31.4 %copy-start.22 = (bf16[64,2048]{1,0:T(8,128)(2,1)S(1)}, bf16[64,2048]{1,0:T(8,128)(2,1)}, u32[]{:S(2)}) copy-start(bf16[64,2048]{1,0:T(8,128)(2,1)} %reduce-scatter.2.cloned.1.call-done) | copy-start | bytes 786436
  284.2 31.0 %all-to-all-start.1 = ((bf16[1,16,16,2048]{3,2,0,1:T(8,128)(2,1)}), bf16[1,16,16,2048]{3,2,0,1:T(8,128)(2,1)S(1)}, u32[]{:S(2)}, u32[]{:S(2)}) async-start(bf16[1,16,16,2048]{3,2,0,1:T(8,128)(2,1)} %fusion.27), calls=%async_computation.2 | async-start | bytes 2097152 | tf_op jit(solution)/shard_map/all_to_all | solution.py:255
  (28 other events, 39.2 us)
Sparse Core Ops, SparseCore 0:
  9.1 53.4 all-gather.2
  112.6 46.9 all-gather.4
  177.6 61.3 reduce-scatter.1
